TPU v7x, 512 devices: a whole 4x4x16 slice. The times are simulated.
512 devices in a mesh: panel: 2 (over x_lo), lat: 8 (over y, core), lon: 32 (over z, x_hi).
Axes of the slice: x: 4 (x_hi: 2, x_lo: 2; x = x_hi * 2 + x_lo), y: 4, z: 16, core: 2. Of those that a mesh axis runs over, the one named last changes fastest.
Arguments:
- fields: float32 [2, 6, 4, 1024, 4096], P('panel', None, None, 'lat', 'lon'), may hold values from -6 to 6
- viscosity: float32 [2, 4, 1024, 4096], P('panel', None, 'lat', 'lon'), may hold values from 0.01 to 0.1
- partner: int32 [2, 8, 1024, 1], P('panel', 'lat', 'lon'), may hold values from 0 to 31; in each aligned block of 32 rows (0 to 31, 32 to 63, ..., all dimensions but the last counted through in order) at most 2 rows name the same one
- src_row: int32 [2, 8, 65536], P('panel', 'lat', 'lon'), may hold values from 0 to 126
- src_col: int32 [2, 8, 65536], P('panel', 'lat', 'lon'), may hold values from 0 to 126
- weight_id: int32 [2, 8, 65536], P('panel', 'lat', 'lon'), may hold values from 0 to 63
- border_angle: float32 [2, 8, 65536], P('panel', 'lat', 'lon'), may hold values from -3.140625 to 3.140625
- dest_cell: int32 [2, 8, 65536], P('panel', 'lat', 'lon'), may hold values from 0 to 16383, as said below
Outputs:
- new_fields: float32 [2, 6, 4, 1024, 4096], P('panel', None, None, 'lat', 'lon')
- pressure: float32 [2, 4, 1024, 4096], P('panel', None, 'lat', 'lon')
Inputs may be any that keep to these rules, and one draw needn't show every extreme that they name: `partner`: A border block's sources lie on the device of the other panel with the same lat index and this lon index; among the 32 blocks of one device no lon index is named by more than 2 blocks. `dest_cell`: the 2048 border cells of one device are distinct cells of its block.
All inputs are finite; a program needn't handle non-finite values.
Results may differ from a plain program's by a relative error of at most 0.0002.
Values sent between devices are 32-bit elements; how exact they have to be, the bound alone decides.
No kernel may reach another device: no remote copies, remote signals or barrier semaphores. Data moves between devices by JAX's collectives and lax.ppermute only.
A program may use at most 128 MiB of HBM per device.

v0:
```python
import math

import jax
import jax.numpy as jnp
from jax import lax
from jax.sharding import PartitionSpec as P

CAP = 2
WQ = 8


BUOYANCY = 0.5


def partner_2(block, axis, apart):
    count = lax.axis_size(axis)
    route = []
    for low in range(count):
        high = low | 1 << apart
        if high != low and high < count:
            route += [(low, high), (high, low)]
    return lax.ppermute(block, axis, route)


def padded_2(shard, sides, width):
    for axis, dim in sides:
        size, length = (lax.axis_size(axis), shard.shape[dim])
        up = [(i, (i + 1) % size) for i in range(size - 1)]
        down = [(j, i) for i, j in up]
        last = lax.slice_in_dim(shard, length - width, length, axis=dim)
        leading = lax.slice_in_dim(shard, 0, width, axis=dim)
        before = lax.ppermute(last, axis, up)
        after = lax.ppermute(leading, axis, down)
        shard = jnp.concatenate([before, shard, after], axis=dim)
    return shard


def metric(row_index, total_rows):
    colatitude = (
        math.pi / 4.0 + (row_index.astype(jnp.float32) + 0.5) * (math.pi / 2.0) / total_rows
    )
    inv_sine = 1.0 / jnp.sin(colatitude)
    return (inv_sine, inv_sine * inv_sine)


def lap_shrink(field, row_gain):
    centre = field[..., 1:-1, 1:-1]
    padded = jnp.pad(centre, [(0, 0)] * (centre.ndim - 3) + [(1, 1), (0, 0), (0, 0)])
    lat_term = field[..., 2:, 1:-1] + field[..., :-2, 1:-1] - 2.0 * centre
    lon_term = field[..., 1:-1, 2:] + field[..., 1:-1, :-2] - 2.0 * centre
    radial = padded[..., 2:, :, :] + padded[..., :-2, :, :] - 2.0 * centre
    return lat_term + row_gain[:, None] * lon_term + radial


def diverge(velocity, inv_sine):
    radial_pad = jnp.pad(velocity[0, :, 1:-1, 1:-1], ((1, 1), (0, 0), (0, 0)))
    lat_part = velocity[1, :, 2:, 1:-1] - velocity[1, :, :-2, 1:-1]
    lon_part = velocity[2, :, 1:-1, 2:] - velocity[2, :, 1:-1, :-2]
    rad_part = radial_pad[2:] - radial_pad[:-2]
    return 0.5 * (lat_part + inv_sine[:, None] * lon_part + rad_part)


def gradient(pressure, inv_sine):
    radial_pad = jnp.pad(pressure[:, 1:-1, 1:-1], ((1, 1), (0, 0), (0, 0)))
    grad_rad = 0.5 * (radial_pad[2:] - radial_pad[:-2])
    grad_lat = 0.5 * (pressure[:, 2:, 1:-1] - pressure[:, :-2, 1:-1])
    grad_lon = 0.5 * inv_sine[:, None] * (pressure[:, 1:-1, 2:] - pressure[:, 1:-1, :-2])
    return (grad_rad, grad_lat, grad_lon)


def cosine_table(length):
    mode_ids = jnp.arange(length, dtype=jnp.float32)
    cell_mid = jnp.arange(length, dtype=jnp.float32) + 0.5
    row_norm = jnp.sqrt(jnp.where(mode_ids > 0, 2.0, 1.0) / length)
    cos_table = row_norm[:, None] * jnp.cos(
        math.pi * mode_ids[:, None] * cell_mid[None, :] / length
    )
    eigenvalue = 4.0 * jnp.sin(math.pi * mode_ids / (2.0 * length)) ** 2
    return (cos_table, eigenvalue)


def coarse_divisor(levels, n_lat, n_lon):
    eig_rad = cosine_table(levels)[1]
    eig_lat = cosine_table(n_lat)[1]
    eig_lon = cosine_table(n_lon)[1]
    return (
        eig_rad[:, None, None]
        + eig_lat[None, :, None]
        + eig_lon[None, None, :]
        + 1.0 / (n_lat * n_lon)
    )


def coarse_solve(block_sum, n_lat, n_lon):
    highest = lax.Precision.HIGHEST
    tab_rad = cosine_table(block_sum.shape[0])[0]
    tab_lat = cosine_table(n_lat)[0]
    tab_lon = cosine_table(n_lon)[0]
    spectrum = jnp.einsum("kr,rlo->klo", tab_rad, block_sum, precision=highest)
    spectrum = jnp.einsum("kl,rlo->rko", tab_lat, spectrum, precision=highest)
    spectrum = jnp.einsum("ko,rlo->rlk", tab_lon, spectrum, precision=highest)
    spectrum = spectrum / coarse_divisor(block_sum.shape[0], n_lat, n_lon)
    restored = jnp.einsum("kr,klo->rlo", tab_rad, spectrum, precision=highest)
    restored = jnp.einsum("kl,rko->rlo", tab_lat, restored, precision=highest)
    restored = jnp.einsum("ko,rlk->rlo", tab_lon, restored, precision=highest)
    return restored / math.sqrt(n_lat * n_lon)


def fractions(weight_ids):
    frac_lat = ((weight_ids // WQ).astype(jnp.float32) + 0.5) / WQ
    frac_lon = ((weight_ids % WQ).astype(jnp.float32) + 0.5) / WQ
    return (frac_lat, frac_lon)


def bilinear(lower_left, lower_right, upper_left, upper_right, frac_lat, frac_lon):
    return (
        (1.0 - frac_lat) * (1.0 - frac_lon) * lower_left
        + (1.0 - frac_lat) * frac_lon * lower_right
        + frac_lat * (1.0 - frac_lon) * upper_left
        + frac_lat * frac_lon * upper_right
    )


def shards(fields, viscosity, partner, src_row, src_col, weight_id, border_angle, dest_cell):
    n_lat = lax.axis_size("lat")
    n_lon = lax.axis_size("lon")
    lat_pos = lax.axis_index("lat")
    lon_pos = lax.axis_index("lon")
    own_fields = fields[0]
    levels, rows_dev, cols_dev = (own_fields.shape[1], own_fields.shape[2], own_fields.shape[3])
    channels = 6 * levels
    blocks = partner.shape[2]
    block_cells = src_row.shape[2] // blocks
    capacity = CAP
    slot_count = n_lon * capacity
    total_rows = rows_dev * n_lat
    flat_cells = own_fields.reshape(channels, rows_dev * cols_dev)
    target = partner[0, 0, :, 0]
    onehot = (target[:, None] == jnp.arange(n_lon, dtype=jnp.int32)[None, :]).astype(jnp.int32)
    before = jnp.sum(
        (jnp.cumsum(onehot, axis=0, dtype=jnp.int32) - onehot) * onehot, axis=1, dtype=jnp.int32
    )
    slot_of = target * capacity + before
    base_cell = (src_row[0, 0] * cols_dev + src_col[0, 0]).reshape(blocks, block_cells)
    weight_ids = weight_id[0, 0].reshape(blocks, block_cells)
    empty = jnp.zeros((slot_count, block_cells), jnp.int32)
    requests = partner_2(
        empty.at[slot_of].set(base_cell).reshape(n_lon, capacity * block_cells), "panel", 0
    )
    requests = lax.all_to_all(requests, "lon", split_axis=0, concat_axis=0, tiled=True)
    served = jnp.stack(
        tuple(
            (
                jnp.take(flat_cells, requests + offset, axis=1)
                for offset in (0, 1, cols_dev, cols_dev + 1)
            )
        ),
        axis=0,
    )
    served = lax.all_to_all(served, "lon", split_axis=2, concat_axis=2, tiled=True)
    served = partner_2(served, "panel", 0)
    picked = served.reshape(4, channels, slot_count, block_cells)[:, :, slot_of, :]
    frac_lat, frac_lon = fractions(weight_ids)
    values = bilinear(picked[0], picked[1], picked[2], picked[3], frac_lat, frac_lon)
    values = values.reshape(6, levels, blocks * block_cells)
    turn = border_angle[0, 0]
    cos_angle = jnp.cos(turn)
    sin_angle = jnp.sin(turn)
    rotated = jnp.stack(
        [
            values[0],
            cos_angle * values[1] + sin_angle * values[2],
            cos_angle * values[2] - sin_angle * values[1],
            values[3],
            cos_angle * values[4] + sin_angle * values[5],
            cos_angle * values[5] - sin_angle * values[4],
        ],
        axis=0,
    ).reshape(channels, blocks * block_cells)
    filled = flat_cells.at[:, dest_cell[0, 0]].set(rotated).reshape(6, levels, rows_dev, cols_dev)
    diffusivity = viscosity[0]
    inv_own, gain_own = metric(
        lat_pos * rows_dev + jnp.arange(-0, rows_dev + 0, dtype=jnp.int32), total_rows
    )
    widened = padded_2(filled, (("lat", 2), ("lon", 3)), 1)
    stepped = filled + diffusivity[None] * lap_shrink(widened, gain_own)
    stepped = jnp.concatenate([stepped[0:1] + BUOYANCY * filled[3:4], stepped[1:]], axis=0)
    velocity = padded_2(stepped[0:3], (("lat", 2), ("lon", 3)), 1)
    divergence = diverge(velocity, inv_own)
    press_one = -divergence / (4.0 + 2.0 * gain_own)[:, None]
    press_wide = padded_2(press_one, (("lat", 1), ("lon", 2)), 1)
    resid_one = -divergence + lap_shrink(press_wide, gain_own)
    block_sum = jnp.sum(resid_one, axis=(1, 2)) * (1.0 / math.sqrt(rows_dev * cols_dev))
    gathered = lax.all_gather(block_sum[:, None], ("lat", "lon"), axis=1, tiled=True)
    coarse = coarse_solve(gathered.reshape(levels, n_lat, n_lon), n_lat, n_lon)
    start = jnp.zeros((), jnp.int32)
    own_coarse = lax.dynamic_slice(coarse, (start, lat_pos, lon_pos), (levels, 1, 1)).reshape(
        levels
    )
    pressure = press_one + own_coarse[:, None, None]
    press_rim = padded_2(pressure, (("lat", 1), ("lon", 2)), 1)
    grad_rad, grad_lat, grad_lon = gradient(press_rim, inv_own)
    result = jnp.stack(
        [
            stepped[0] - grad_rad,
            stepped[1] - grad_lat,
            stepped[2] - grad_lon,
            stepped[3],
            stepped[4],
            stepped[5],
        ],
        axis=0,
    )
    return (result[None], pressure[None])


def solution(mesh):
    return jax.shard_map(
        shards,
        mesh=mesh,
        in_specs=(
            P("panel", None, None, "lat", "lon"),
            P("panel", None, "lat", "lon"),
            P("panel", "lat", "lon", None),
            P("panel", "lat", "lon"),
            P("panel", "lat", "lon"),
            P("panel", "lat", "lon"),
            P("panel", "lat", "lon"),
            P("panel", "lat", "lon"),
        ),
        out_specs=(P("panel", None, None, "lat", "lon"), P("panel", None, "lat", "lon")),
        check_vma=False,
    )
```

profile of v0, /device:TPU:1, one launch (start us, length us, event | category | flops | bytes accessed | tf_op | source)
XLA Modules:
  0.0 1005.3 jit_solution(13711686433813685990)
XLA Ops:
  4.5 3.9 collective-permute-start
  9.7 17.9 %all-to-all-start = ((s32[32,1,128]{2,1,0:T(1,128)}), s32[32,1,128]{2,1,0:T(1,128)S(1)}, u32[]{:S(2)}, u32[]{:S(2)}) async-start(s32[32,1,128]{2,1,0:T(1,128)} %bitcast.6), calls=%async_computation | async-start | bytes 32768 | tf_op jit(solution)/shard_map/all_to_all | solution.py:150
  27.6 2.3 copy.132
  29.9 4.7 copy.95
  34.6 6.6 all-to-all-done
  41.2 14.2 %gather_fusion.1 = f32[4096,24]{1,0:T(8,128)S(1)} fusion(f32[24,16384]{0,1:T(8,128)} %copy.95, s32[4096]{0:T(1024)S(1)} %get-tuple-element.38), kind=kCustom, calls=%fused_computation.clone | custom fusion | bytes 802816 | tf_op jit(solution)/shard_map/jit(_take)/gather | solution.py:154
  55.9 14.2 %gather_fusion.2 = f32[4096,24]{1,0:T(8,128)S(1)} fusion(f32[24,16384]{0,1:T(8,128)} %copy.95, s32[4096]{0:T(1024)S(1)} %get-tuple-element.39), kind=kCustom, calls=%fused_computation.1.clone | custom fusion | bytes 802816 | tf_op jit(solution)/shard_map/jit(_take)/gather | solution.py:154
  70.7 14.2 %gather_fusion.3 = f32[4096,24]{1,0:T(8,128)S(1)} fusion(f32[24,16384]{0,1:T(8,128)} %copy.95, s32[4096]{0:T(1024)S(1)} %get-tuple-element.40), kind=kCustom, calls=%fused_computation.2.clone | custom fusion | bytes 802816 | tf_op jit(solution)/shard_map/jit(_take)/gather | solution.py:154
  85.4 14.2 %gather_fusion.4 = f32[4096,24]{1,0:T(8,128)S(1)} fusion(f32[24,16384]{0,1:T(8,128)} %copy.95, s32[4096]{0:T(1024)S(1)} %get-tuple-element.41), kind=kCustom, calls=%fused_computation.3.clone | custom fusion | bytes 802816 | tf_op jit(solution)/shard_map/jit(_take)/gather | solution.py:154
  99.6 1.3 copy.83
  103.2 7.5 all-to-all-start.1
  110.9 75.1 %all-to-all-done.1 = f32[4,24,32,128]{3,1,0,2:T(8,128)S(1)} async-done(((f32[4,24,32,128]{3,1,0,2:T(8,128)}), f32[4,24,32,128]{3,1,0,2:T(8,128)S(1)}, u32[]{:S(2)}, u32[]{:S(2)}) %all-to-all-start.1) | async-done | bytes 1572896 | tf_op jit(solution)/shard_map/all_to_all | solution.py:160
  186.0 2.2 collective-permute-start.1
  190.0 32.0 %collective-permute-done.1 = f32[4,24,32,128]{3,1,0,2:T(8,128)S(1)} collective-permute-done((f32[4,24,32,128]{3,1,0,2:T(8,128)S(1)}, f32[4,24,32,128]{3,1,0,2:T(8,128)S(1)}, u32[]{:S(2)}, u32[]{:S(2)}) %collective-permute-start.1) | collective-permute-done | bytes 1572896 | tf_op jit(solution)/shard_map/ppermute | solution.py:22
  221.9 2.1 copy.84
  224.0 2.4 reshape.638
  226.4 3.5 copy.85
  229.9 2.5 gather_fusion
  233.9 12.2 %scatter_fusion = f32[24,16384]{0,1:T(8,128)} fusion(f32[24,16384]{0,1:T(8,128)} %copy.95, s32[2048]{0:T(1024)S(1)} %bitcast.183, f32[2048,24]{1,0:T(8,128)S(1)} %copy.96), kind=kCustom, calls=%fused_computation.6 | custom fusion | bytes 598016 | tf_op jit(solution)/shard_map/scatter | solution.py:180
  246.1 5.1 copy.97
  251.5 4.6 collective-permute-start.2
  256.2 3.1 collective-permute-start.3
  260.3 2.3 fusion.116
  262.5 2.3 copy.100
  264.9 4.4 collective-permute-start.5
  269.3 2.3 copy.98
  273.0 6.6 slice_multiply_fusion
  279.5 5.2 copy.102
  284.8 1.8 copy.101
  286.6 1.8 copy.99
  288.4 3.5 fusion.4
  292.0 1.9 collective-permute-start.6
  293.9 4.5 collective-permute-start.7
  299.3 1.4 fusion.118
  300.7 1.6 copy.103
  303.6 1.6 copy.105
  305.2 6.4 collective-permute-start.9
  314.2 1.4 broadcast_divide_fusion
  315.5 1.9 collective-permute-start.10
  317.5 4.6 collective-permute-start.11
  324.9 6.7 collective-permute-start.13
  331.6 3.0 collective-permute-done.12
  334.6 6.8 collective-permute-done.13
  341.8 597.2 %all-gather = f32[256,1,4]{2,1,0:T(1,128)S(1)} all-gather(f32[1,1,4]{2,1,0:T(1,128)S(1)} %multiply_bitcast_fusion), channel_id=1, replica_groups=mesh['panel'=2,'lat'=8,'lon'=32] {'lat','lon'}, dimensions={0}, use_global_device_ids=true | all-gather | bytes 4112 | tf_op jit(solution)/shard_map/all_gather | solution.py:194
  941.5 46.6 %collective-permute-start.14 = (f32[4,1,128]{2,1,0:T(1,128)S(1)}, f32[4,1,128]{2,1,0:T(1,128)S(1)}, u32[]{:S(2)}, u32[]{:S(2)}) collective-permute-start(f32[4,1,128]{2,1,0:T(1,128)S(1)} %get-tuple-element.27), channel_id=1, source_target_pairs={{32,0},{64,32},{96,64},{128,96},{160,128},{192,160},{224,192},{33,... | collective-permute-start | bytes 6152 | tf_op jit(solution)/shard_map/ppermute | solution.py:33
  988.1 1.9 collective-permute-start.15
  992.6 5.5 collective-permute-start.17
  998.9 3.9 collective-permute-done.16
  (113 shorter events, 31.1 us)
Async XLA Ops:
  4.5 5.2 collective-permute-start
  9.7 31.5 %all-to-all-start = ((s32[32,1,128]{2,1,0:T(1,128)}), s32[32,1,128]{2,1,0:T(1,128)S(1)}, u32[]{:S(2)}, u32[]{:S(2)}) async-start(s32[32,1,128]{2,1,0:T(1,128)} %bitcast.6), calls=%async_computation | async-start | bytes 32768 | tf_op jit(solution)/shard_map/all_to_all | solution.py:150
  100.9 1.0 copy-start
  103.2 85.5 %copy-start.2 = (s32[1,1,2048]{2,1,0:T(1,128)S(1)}, s32[1,1,2048]{2,1,0:T(1,128)}, u32[]{:S(2)}) copy-start(s32[1,1,2048]{2,1,0:T(1,128)} %param.15) | copy-start | bytes 24580
  103.2 86.5 %copy-start.3 = (s32[1,1,2048]{2,1,0:T(1,128)S(1)}, s32[1,1,2048]{2,1,0:T(1,128)}, u32[]{:S(2)}) copy-start(s32[1,1,2048]{2,1,0:T(1,128)} %param.17) | copy-start | bytes 24580
  103.2 86.5 %copy-start.1 = (f32[1,1,2048]{2,1,0:T(1,128)S(1)}, f32[1,1,2048]{2,1,0:T(1,128)}, u32[]{:S(2)}) copy-start(f32[1,1,2048]{2,1,0:T(1,128)} %param.16) | copy-start | bytes 24580
  103.2 82.7 %all-to-all-start.1 = ((f32[4,24,32,128]{3,1,0,2:T(8,128)}), f32[4,24,32,128]{3,1,0,2:T(8,128)S(1)}, u32[]{:S(2)}, u32[]{:S(2)}) async-start(f32[4,24,32,128]{3,1,0,2:T(8,128)} %pad_maximum_fusion.9), calls=%async_computation.1 | async-start | bytes 3145728 | tf_op jit(solution)/shard_map/all_to_all | solution.py:160
  186.0 36.0 %collective-permute-start.1 = (f32[4,24,32,128]{3,1,0,2:T(8,128)S(1)}, f32[4,24,32,128]{3,1,0,2:T(8,128)S(1)}, u32[]{:S(2)}, u32[]{:S(2)}) collective-permute-start(f32[4,24,32,128]{3,1,0,2:T(8,128)S(1)} %all-to-all-done.1), channel_id=1, source_target_pairs={{0,256},{256,0},{1,257},{257,1},{2,258},{258,2},{3,259},{259,3},{4... | collective-permute-start | bytes 4718600 | tf_op jit(solution)/shard_map/ppermute | solution.py:22
  251.5 7.8 collective-permute-start.2
  256.2 3.9 collective-permute-start.3
  264.9 19.9 %collective-permute-start.5 = (f32[6,4,130,1]{2,1,3,0:T(4,128)S(1)}, f32[6,4,130,1]{2,1,3,0:T(4,128)S(1)}, u32[]{:S(2)}, u32[]{:S(2)}) collective-permute-start(f32[6,4,130,1]{2,1,3,0:T(4,128)S(1)} %copy.100), channel_id=1, source_target_pairs={{0,1},{1,2},{2,3},{3,4},{4,5},{5,6},{6,7},{7,8},{8,9},{9,10},{10,1... | collective-permute-start | bytes 37448 | tf_op jit(solution)/shard_map/ppermute | solution.py:32
  271.7 14.9 %collective-permute-start.4 = (f32[6,4,130,1]{2,1,3,0:T(4,128)S(1)}, f32[6,4,130,1]{2,1,3,0:T(4,128)S(1)}, u32[]{:S(2)}, u32[]{:S(2)}) collective-permute-start(f32[6,4,130,1]{2,1,3,0:T(4,128)S(1)} %copy.98), channel_id=1, source_target_pairs={{1,0},{2,1},{3,2},{4,3},{5,4},{6,5},{7,6},{8,7},{9,8},{10,9},{11,1... | collective-permute-start | bytes 37448 | tf_op jit(solution)/shard_map/ppermute | solution.py:33
  292.0 6.5 collective-permute-start.6
  293.9 5.2 collective-permute-start.7
  302.3 9.3 collective-permute-start.8
  305.2 7.7 collective-permute-start.9
  315.5 6.5 collective-permute-start.10
  317.5 5.3 collective-permute-start.11
  323.6 11.0 %collective-permute-start.12 = (f32[4,130,1]{2,1,0:T(8,128)}, f32[4,130,1]{2,1,0:T(8,128)S(1)}, u32[]{:S(2)}, u32[]{:S(2)}) collective-permute-start(f32[4,130,1]{2,1,0:T(8,128)} %get-tuple-element.23), channel_id=1, source_target_pairs={{1,0},{2,1},{3,2},{4,3},{5,4},{6,5},{7,6},{8,7},{9,8},{10,9},{11,1... | collective-permute-start | bytes 6248 | tf_op jit(solution)/shard_map/ppermute | solution.py:33
  324.9 16.5 %collective-permute-start.13 = (f32[4,130,1]{2,1,0:T(8,128)S(1)}, f32[4,130,1]{2,1,0:T(8,128)S(1)}, u32[]{:S(2)}, u32[]{:S(2)}) collective-permute-start(f32[4,130,1]{2,1,0:T(8,128)S(1)} %get-tuple-element.24), channel_id=1, source_target_pairs={{0,1},{1,2},{2,3},{3,4},{4,5},{5,6},{6,7},{7,8},{8,9},{9,10},{10,1... | collective-permute-start | bytes 6248 | tf_op jit(solution)/shard_map/ppermute | solution.py:32
  941.5 48.6 %collective-permute-start.14 = (f32[4,1,128]{2,1,0:T(1,128)S(1)}, f32[4,1,128]{2,1,0:T(1,128)S(1)}, u32[]{:S(2)}, u32[]{:S(2)}) collective-permute-start(f32[4,1,128]{2,1,0:T(1,128)S(1)} %get-tuple-element.27), channel_id=1, source_target_pairs={{32,0},{64,32},{96,64},{128,96},{160,128},{192,160},{224,192},{33,... | collective-permute-start | bytes 6152 | tf_op jit(solution)/shard_map/ppermute | solution.py:33
  988.1 3.1 collective-permute-start.15
  991.3 11.5 %collective-permute-start.16 = (f32[4,130,1]{2,1,0:T(8,128)S(1)}, f32[4,130,1]{2,1,0:T(8,128)S(1)}, u32[]{:S(2)}, u32[]{:S(2)}) collective-permute-start(f32[4,130,1]{2,1,0:T(8,128)S(1)} %get-tuple-element.21), channel_id=1, source_target_pairs={{1,0},{2,1},{3,2},{4,3},{5,4},{6,5},{7,6},{8,7},{9,8},{10,9},{11,1... | collective-permute-start | bytes 6248 | tf_op jit(solution)/shard_map/ppermute | solution.py:33
  992.6 11.1 %collective-permute-start.17 = (f32[4,130,1]{2,1,0:T(8,128)S(1)}, f32[4,130,1]{2,1,0:T(8,128)S(1)}, u32[]{:S(2)}, u32[]{:S(2)}) collective-permute-start(f32[4,130,1]{2,1,0:T(8,128)S(1)} %get-tuple-element.22), channel_id=1, source_target_pairs={{0,1},{1,2},{2,3},{3,4},{4,5},{5,6},{6,7},{7,8},{8,9},{9,10},{10,1... | collective-permute-start | bytes 6248 | tf_op jit(solution)/shard_map/ppermute | solution.py:32
where the time goes:
time: 1010 us
  blocking collectives  597 us (59%)
  waiting for transfers between devices  133 us (13%)
  starting transfers between devices  129 us (13%)
  local copies, waits for them, and re-layouts  122 us (12%)
  other arithmetic  20.7 us (2%)
    all_gather x1, blocking collectives, shards(): lax.all_gather(block_sum[:, None], ('lat', 'lon'), axis=1, tiled=True)  597 us
    all_to_all x1, waiting for transfers between devices, shards(): lax.all_to_all(served, 'lon', split_axis=2, concat_axis=2, tiled=True)  75.1 us
    ppermute x8, starting transfers between devices, padded_2(): after = lax.ppermute(leading, axis, down)  60.2 us
    gather x8, local copies, waits for them, and re-layouts, shards(): jnp.take(flat_cells, requests + offset, axis=1)  59.7 us
    ppermute x8, starting transfers between devices, padded_2(): before = lax.ppermute(last, axis, up)  37.1 us
    ppermute x2, waiting for transfers between devices, partner_2(): return lax.ppermute(block, axis, route)  33.2 us
  transfers between devices with their start and end apart: 20, of which 12 were waited for; matrix products, arithmetic and copies ran while one was open for 3% of the time, Pallas kernels for 0%

commit v1 on v0

--- a/solution.py
+++ b/solution.py
@@ -33,6 +33,20 @@
         after = lax.ppermute(leading, axis, down)
         shard = jnp.concatenate([before, shard, after], axis=dim)
     return shard
+
+
+def doubling_gather(block, axis):
+    count = lax.axis_size(axis)
+    index = lax.axis_index(axis)
+    step = 1
+    while step < count:
+        other = lax.ppermute(block, axis, [(i, i ^ step) for i in range(count)])
+        low = (index & step) == 0
+        block = jnp.where(
+            low, jnp.concatenate([block, other], 0), jnp.concatenate([other, block], 0)
+        )
+        step *= 2
+    return block
 
 
 def metric(row_index, total_rows):
@@ -191,14 +205,33 @@
     press_wide = padded_2(press_one, (("lat", 1), ("lon", 2)), 1)
     resid_one = -divergence + lap_shrink(press_wide, gain_own)
     block_sum = jnp.sum(resid_one, axis=(1, 2)) * (1.0 / math.sqrt(rows_dev * cols_dev))
-    gathered = lax.all_gather(block_sum[:, None], ("lat", "lon"), axis=1, tiled=True)
-    coarse = coarse_solve(gathered.reshape(levels, n_lat, n_lon), n_lat, n_lon)
+    gathered = doubling_gather(block_sum[None], "lon")
+    gathered = doubling_gather(gathered[None], "lat")
+    coarse = coarse_solve(jnp.transpose(gathered, (2, 0, 1)), n_lat, n_lon)
     start = jnp.zeros((), jnp.int32)
-    own_coarse = lax.dynamic_slice(coarse, (start, lat_pos, lon_pos), (levels, 1, 1)).reshape(
-        levels
-    )
+    near = lax.dynamic_slice(
+        jnp.pad(coarse, ((0, 0), (1, 1), (1, 1))), (start, lat_pos, lon_pos), (levels, 3, 3)
+    )
+    own_coarse = near[:, 1, 1]
     pressure = press_one + own_coarse[:, None, None]
-    press_rim = padded_2(pressure, (("lat", 1), ("lon", 2)), 1)
+    row_at = lax.broadcasted_iota(jnp.int32, (rows_dev + 2, cols_dev + 2), 0)
+    col_at = lax.broadcasted_iota(jnp.int32, (rows_dev + 2, cols_dev + 2), 1)
+    rim_coarse = jnp.where(
+        row_at == 0,
+        near[:, 0, 1][:, None, None],
+        jnp.where(
+            row_at == rows_dev + 1,
+            near[:, 2, 1][:, None, None],
+            jnp.where(
+                col_at == 0,
+                near[:, 1, 0][:, None, None],
+                jnp.where(
+                    col_at == cols_dev + 1, near[:, 1, 2][:, None, None], own_coarse[:, None, None]
+                ),
+            ),
+        ),
+    )
+    press_rim = press_wide + rim_coarse
     grad_rad, grad_lat, grad_lon = gradient(press_rim, inv_own)
     result = jnp.stack(
         [

time: 1010 us -> 414 us (0.41)
  blocking collectives: 597 us -> 0 us
  waiting for transfers between devices: 133 us -> 148 us
  starting transfers between devices: 129 us -> 116 us
    all_gather x1 -> x0, blocking collectives: 597 us -> none  [shards(): lax.all_gather(block_sum[:, None], ('lat', 'lon'), axis=1, tiled=True)]
    ppermute x8 -> x6, starting transfers between devices: 60.2 us -> 12.4 us  [padded_2(): after = lax.ppermute(leading, axis, down)]
    ppermute x0 -> x8, starting transfers between devices: none -> 41.6 us  [doubling_gather(): other = lax.ppermute(block, axis, [(i, i ^ step) for i in range(count)])]
    ppermute x0 -> x8, waiting for transfers between devices: none -> 18.2 us  [doubling_gather(): other = lax.ppermute(block, axis, [(i, i ^ step) for i in range(count)])]
    ppermute x8 -> x6, starting transfers between devices: 37.1 us -> 30.1 us  [padded_2(): before = lax.ppermute(last, axis, up)]
  transfers between devices with their start and end apart: 20 -> 24, of which waited for: 12 -> 17; matrix products, arithmetic and copies ran while one was open for 3% -> 7% of each run, Pallas kernels for 0% -> 0%
where the time goes in v1:
time: 414 us; the launch traced here: 411 us
  waiting for transfers between devices  148 us (36%)
  local copies, waits for them, and re-layouts  123 us (30%)
  starting transfers between devices  116 us (28%)
  other arithmetic  21.8 us (5%)
    all_to_all x1, waiting for transfers between devices, shards(): lax.all_to_all(served, 'lon', split_axis=2, concat_axis=2, tiled=True)  75.1 us
    gather x8, local copies, waits for them, and re-layouts, shards(): jnp.take(flat_cells, requests + offset, axis=1)  59.6 us
    ppermute x8, starting transfers between devices, doubling_gather(): other = lax.ppermute(block, axis, [(i, i ^ step) for i in range(count)])  41.6 us
    ppermute x2, waiting for transfers between devices, partner_2(): return lax.ppermute(block, axis, route)  33.2 us
    ppermute x6, starting transfers between devices, padded_2(): before = lax.ppermute(last, axis, up)  30.1 us
    ppermute x8, waiting for transfers between devices, doubling_gather(): other = lax.ppermute(block, axis, [(i, i ^ step) for i in range(count)])  18.2 us
    all_to_all x1, starting transfers between devices, shards(): lax.all_to_all(requests, 'lon', split_axis=0, concat_axis=0, tiled=True)  17.9 us
    scatter x2, local copies, waits for them, and re-layouts, shards(): flat_cells.at[:, dest_cell[0, 0]].set(rotated)  17.3 us
  transfers between devices with their start and end apart: 24, of which 17 were waited for; matrix products, arithmetic and copies ran while one was open for 7% of the time, Pallas kernels for 0%

profile of v1, /device:TPU:1, one launch (start us, length us, event | category | flops | bytes accessed | tf_op | source)
XLA Modules:
  0.0 411.4 jit_solution(13879906386483512133)
XLA Ops:
  4.5 3.9 collective-permute-start
  9.7 17.9 %all-to-all-start = ((s32[32,1,128]{2,1,0:T(1,128)}), s32[32,1,128]{2,1,0:T(1,128)S(1)}, u32[]{:S(2)}, u32[]{:S(2)}) async-start(s32[32,1,128]{2,1,0:T(1,128)} %bitcast.6), calls=%async_computation | async-start | bytes 32768 | tf_op jit(solution)/shard_map/all_to_all | solution.py:164
  27.6 2.3 copy.138
  29.9 4.7 %copy.101 = f32[24,16384]{0,1:T(8,128)} copy(f32[24,16384]{1,0:T(8,128)S(1)} %bitcast.161) | data formatting | bytes 3145728 | tf_op jit(solution)/shard_map/reshape;squeeze | solution.py:151
  34.6 6.6 %all-to-all-done = s32[32,1,128]{2,1,0:T(1,128)S(1)} async-done(((s32[32,1,128]{2,1,0:T(1,128)}), s32[32,1,128]{2,1,0:T(1,128)S(1)}, u32[]{:S(2)}, u32[]{:S(2)}) %all-to-all-start) | async-done | bytes 16416 | tf_op jit(solution)/shard_map/all_to_all | solution.py:164
  41.2 14.1 %gather_fusion.1 = f32[4096,24]{1,0:T(8,128)S(1)} fusion(f32[24,16384]{0,1:T(8,128)} %copy.101, s32[4096]{0:T(1024)S(1)} %get-tuple-element.39), kind=kCustom, calls=%fused_computation.clone | custom fusion | bytes 802816 | tf_op jit(solution)/shard_map/jit(_take)/gather | solution.py:168
  55.9 14.1 %gather_fusion.2 = f32[4096,24]{1,0:T(8,128)S(1)} fusion(f32[24,16384]{0,1:T(8,128)} %copy.101, s32[4096]{0:T(1024)S(1)} %get-tuple-element.40), kind=kCustom, calls=%fused_computation.1.clone | custom fusion | bytes 802816 | tf_op jit(solution)/shard_map/jit(_take)/gather | solution.py:168
  70.6 14.1 %gather_fusion.3 = f32[4096,24]{1,0:T(8,128)S(1)} fusion(f32[24,16384]{0,1:T(8,128)} %copy.101, s32[4096]{0:T(1024)S(1)} %get-tuple-element.41), kind=kCustom, calls=%fused_computation.2.clone | custom fusion | bytes 802816 | tf_op jit(solution)/shard_map/jit(_take)/gather | solution.py:168
  85.3 14.1 %gather_fusion.4 = f32[4096,24]{1,0:T(8,128)S(1)} fusion(f32[24,16384]{0,1:T(8,128)} %copy.101, s32[4096]{0:T(1024)S(1)} %get-tuple-element.42), kind=kCustom, calls=%fused_computation.3.clone | custom fusion | bytes 802816 | tf_op jit(solution)/shard_map/jit(_take)/gather | solution.py:168
  103.2 7.7 %all-to-all-start.1 = ((f32[4,24,32,128]{3,1,0,2:T(8,128)}), f32[4,24,32,128]{3,1,0,2:T(8,128)S(1)}, u32[]{:S(2)}, u32[]{:S(2)}) async-start(f32[4,24,32,128]{3,1,0,2:T(8,128)} %pad_maximum_fusion.9), calls=%async_computation.1 | async-start | bytes 3145728 | tf_op jit(solution)/shard_map/all_to_all | solution.py:174
  110.9 75.1 %all-to-all-done.1 = f32[4,24,32,128]{3,1,0,2:T(8,128)S(1)} async-done(((f32[4,24,32,128]{3,1,0,2:T(8,128)}), f32[4,24,32,128]{3,1,0,2:T(8,128)S(1)}, u32[]{:S(2)}, u32[]{:S(2)}) %all-to-all-start.1) | async-done | bytes 1572896 | tf_op jit(solution)/shard_map/all_to_all | solution.py:174
  186.0 2.2 collective-permute-start.1
  190.0 32.0 %collective-permute-done.1 = f32[4,24,32,128]{3,1,0,2:T(8,128)S(1)} collective-permute-done((f32[4,24,32,128]{3,1,0,2:T(8,128)S(1)}, f32[4,24,32,128]{3,1,0,2:T(8,128)S(1)}, u32[]{:S(2)}, u32[]{:S(2)}) %collective-permute-start.1) | collective-permute-done | bytes 1572896 | tf_op jit(solution)/shard_map/ppermute | solution.py:22
  222.0 2.1 copy.90
  224.0 2.4 reshape.738
  226.5 3.5 copy.91
  230.0 2.5 gather_fusion
  233.9 12.2 %scatter_fusion = f32[24,16384]{0,1:T(8,128)} fusion(f32[24,16384]{0,1:T(8,128)} %copy.101, s32[2048]{0:T(1024)S(1)} %bitcast.181, f32[2048,24]{1,0:T(8,128)S(1)} %copy.102), kind=kCustom, calls=%fused_computation.6 | custom fusion | bytes 598016 | tf_op jit(solution)/shard_map/scatter | solution.py:194
  246.1 5.1 %copy.103 = f32[24,16384]{1,0:T(8,128)S(1)} copy(f32[24,16384]{0,1:T(8,128)} %scatter_fusion) | data formatting | bytes 3145728 | tf_op jit(solution)/shard_map/scatter | solution.py:194
  251.5 4.6 %collective-permute-start.2 = (f32[6,4,1,128]{3,2,1,0:T(1,128)S(1)}, f32[6,4,1,128]{3,2,1,0:T(1,128)S(1)}, u32[]{:S(2)}, u32[]{:S(2)}) collective-permute-start(f32[6,4,1,128]{3,2,1,0:T(1,128)S(1)} %get-tuple-element.17), channel_id=1, source_target_pairs={{32,0},{64,32},{96,64},{128,96},{160,128},{192,160},{224,192},{33,... | collective-permute-start | bytes 36872 | tf_op jit(solution)/shard_map/ppermute | solution.py:33
  256.2 3.1 collective-permute-start.3
  260.3 2.3 fusion.126
  262.5 2.3 copy.104
  266.2 2.3 copy.106
  268.5 5.5 %collective-permute-start.5 = (f32[6,4,130,1]{2,1,3,0:T(4,128)S(1)}, f32[6,4,130,1]{2,1,3,0:T(4,128)S(1)}, u32[]{:S(2)}, u32[]{:S(2)}) collective-permute-start(f32[6,4,130,1]{2,1,3,0:T(4,128)S(1)} %copy.106), channel_id=1, source_target_pairs={{0,1},{1,2},{2,3},{3,4},{4,5},{5,6},{6,7},{7,8},{8,9},{9,10},{10,1... | collective-permute-start | bytes 37448 | tf_op jit(solution)/shard_map/ppermute | solution.py:32
  274.0 6.6 %slice_multiply_fusion = f32[4,16384]{0,1:T(8,128)} fusion(f32[24,16384]{0,1:T(8,128)} %scatter_fusion), kind=kLoop, calls=%fused_computation.7 | loop fusion | flops 65536 | bytes 524288 | tf_op jit(solution)/shard_map/mul | solution.py:201
  280.6 5.2 %copy.108 = f32[1,4,128,128]{3,2,1,0:T(8,128)S(1)} copy(f32[1,4,128,128]{1,3,2,0:T(8,128)} %bitcast.156) | data formatting | bytes 524288 | tf_op jit(solution)/shard_map/mul | solution.py:201
  289.4 3.5 fusion.4
  293.1 1.9 collective-permute-start.6
  295.0 4.8 %collective-permute-start.7 = (f32[3,4,1,128]{3,2,1,0:T(1,128)S(1)}, f32[3,4,1,128]{3,2,1,0:T(1,128)S(1)}, u32[]{:S(2)}, u32[]{:S(2)}) collective-permute-start(f32[3,4,1,128]{3,2,1,0:T(1,128)S(1)} %get-tuple-element.14), channel_id=1, source_target_pairs={{0,32},{32,64},{64,96},{96,128},{128,160},{160,192},{192,224},{1,3... | collective-permute-start | bytes 18440 | tf_op jit(solution)/shard_map/ppermute | solution.py:32
  306.6 6.0 %collective-permute-start.9 = (f32[3,4,130,1]{2,1,3,0:T(4,128)S(1)}, f32[3,4,130,1]{2,1,3,0:T(4,128)S(1)}, u32[]{:S(2)}, u32[]{:S(2)}) collective-permute-start(f32[3,4,130,1]{2,1,3,0:T(4,128)S(1)} %copy.111), channel_id=1, source_target_pairs={{0,1},{1,2},{2,3},{3,4},{4,5},{5,6},{6,7},{7,8},{8,9},{9,10},{10,1... | collective-permute-start | bytes 18728 | tf_op jit(solution)/shard_map/ppermute | solution.py:32
  315.1 2.1 broadcast_divide_fusion
  317.1 4.7 %collective-permute-start.10 = (f32[4,1,128]{2,1,0:T(1,128)S(1)}, f32[4,1,128]{2,1,0:T(1,128)S(1)}, u32[]{:S(2)}, u32[]{:S(2)}) collective-permute-start(f32[4,1,128]{2,1,0:T(1,128)S(1)} %get-tuple-element.29), channel_id=1, source_target_pairs={{0,32},{32,64},{64,96},{96,128},{128,160},{160,192},{192,224},{1,3... | collective-permute-start | bytes 6152 | tf_op jit(solution)/shard_map/ppermute | solution.py:32
  321.9 1.9 collective-permute-start.11
  323.8 2.9 collective-permute-done.11
  327.7 6.0 %collective-permute-start.12 = (f32[4,130,1]{2,1,0:T(8,128)}, f32[4,130,1]{2,1,0:T(8,128)S(1)}, u32[]{:S(2)}, u32[]{:S(2)}) collective-permute-start(f32[4,130,1]{2,1,0:T(8,128)} %get-tuple-element.27), channel_id=1, source_target_pairs={{0,1},{1,2},{2,3},{3,4},{4,5},{5,6},{6,7},{7,8},{8,9},{9,10},{10,1... | collective-permute-start | bytes 6248 | tf_op jit(solution)/shard_map/ppermute | solution.py:32
  335.1 4.1 collective-permute-done.12
  339.1 6.7 %collective-permute-done.13 = f32[4,130,1]{2,1,0:T(8,128)S(1)} collective-permute-done((f32[4,130,1]{2,1,0:T(8,128)}, f32[4,130,1]{2,1,0:T(8,128)S(1)}, u32[]{:S(2)}, u32[]{:S(2)}) %collective-permute-start.13) | collective-permute-done | bytes 2112 | tf_op jit(solution)/shard_map/ppermute | solution.py:33
  346.2 6.0 %collective-permute-start.14 = (f32[1,4]{1,0:T(1,128)S(1)}, f32[1,4]{1,0:T(1,128)S(1)}, u32[]{:S(2)}, u32[]{:S(2)}) collective-permute-start(f32[1,4]{1,0:T(1,128)S(1)} %multiply_bitcast_fusion), channel_id=1, source_target_pairs={{0,1},{1,0},{2,3},{3,2},{4,5},{5,4},{6,7},{7,6},{8,9},{9,8},{10,11... | collective-permute-start | bytes 56 | tf_op jit(solution)/shard_map/ppermute | solution.py:43
  353.2 6.1 %collective-permute-start.15 = (f32[2,4]{1,0:T(2,128)S(1)}, f32[2,4]{1,0:T(2,128)S(1)}, u32[]{:S(2)}, u32[]{:S(2)}) collective-permute-start(f32[2,4]{1,0:T(2,128)S(1)} %maximum_select_fusion.7), channel_id=1, source_target_pairs={{0,2},{1,3},{2,0},{3,1},{4,6},{5,7},{6,4},{7,5},{8,10},{9,11},{10,... | collective-permute-start | bytes 104 | tf_op jit(solution)/shard_map/ppermute | solution.py:43
  362.2 3.3 collective-permute-done.16
  365.5 3.7 collective-permute-start.17
  369.3 4.5 %collective-permute-done.17 = f32[8,4]{1,0:T(8,128)S(1)} collective-permute-done((f32[8,4]{1,0:T(8,128)S(1)}, f32[8,4]{1,0:T(8,128)S(1)}, u32[]{:S(2)}, u32[]{:S(2)}) %collective-permute-start.17) | collective-permute-done | bytes 160 | tf_op jit(solution)/shard_map/ppermute | solution.py:43
  373.9 7.2 %collective-permute-start.18 = (f32[16,4]{0,1:T(4,128)S(1)}, f32[16,4]{0,1:T(4,128)S(1)}, u32[]{:S(2)}, u32[]{:S(2)}) collective-permute-start(f32[16,4]{0,1:T(4,128)S(1)} %maximum_select_fusion.5), channel_id=1, source_target_pairs={{0,16},{1,17},{2,18},{3,19},{4,20},{5,21},{6,22},{7,23},{8,24},{9,... | collective-permute-start | bytes 776 | tf_op jit(solution)/shard_map/ppermute | solution.py:43
  381.1 5.9 %collective-permute-done.18 = f32[16,4]{0,1:T(4,128)S(1)} collective-permute-done((f32[16,4]{0,1:T(4,128)S(1)}, f32[16,4]{0,1:T(4,128)S(1)}, u32[]{:S(2)}, u32[]{:S(2)}) %collective-permute-start.18) | collective-permute-done | bytes 288 | tf_op jit(solution)/shard_map/ppermute | solution.py:43
  387.0 7.8 %collective-permute-start.19 = (f32[1,32,4]{1,2,0:T(4,128)S(1)}, f32[1,32,4]{1,2,0:T(4,128)S(1)}, u32[]{:S(2)}, u32[]{:S(2)}) collective-permute-start(f32[1,32,4]{1,2,0:T(4,128)S(1)} %maximum_select_fusion.6), channel_id=1, source_target_pairs={{0,32},{32,0},{64,96},{96,64},{128,160},{160,128},{192,224},{224,1... | collective-permute-start | bytes 1544 | tf_op jit(solution)/shard_map/ppermute | solution.py:43
  395.6 3.9 collective-permute-start.20
  400.5 5.0 %collective-permute-start.21 = (f32[4,32,4]{1,2,0:T(4,128)S(1)}, f32[4,32,4]{1,2,0:T(4,128)S(1)}, u32[]{:S(2)}, u32[]{:S(2)}) collective-permute-start(f32[4,32,4]{1,2,0:T(4,128)S(1)} %maximum_select_fusion.1), channel_id=1, source_target_pairs={{0,128},{32,160},{64,192},{96,224},{128,0},{160,32},{192,64},{224,... | collective-permute-start | bytes 6152 | tf_op jit(solution)/shard_map/ppermute | solution.py:43
  (130 shorter events, 43.5 us)
Async XLA Ops:
  4.5 5.2 %collective-permute-start = (s32[32,128]{1,0:T(8,128)S(1)}, s32[32,128]{1,0:T(8,128)}, u32[]{:S(2)}, u32[]{:S(2)}) collective-permute-start(s32[32,128]{1,0:T(8,128)S(1)} %reshape.737), channel_id=1, source_target_pairs={{0,256},{256,0},{1,257},{257,1},{2,258},{258,2},{3,259},{259,3},{4... | collective-permute-start | bytes 49160 | tf_op jit(solution)/shard_map/ppermute | solution.py:22
  9.7 31.5 %all-to-all-start = ((s32[32,1,128]{2,1,0:T(1,128)}), s32[32,1,128]{2,1,0:T(1,128)S(1)}, u32[]{:S(2)}, u32[]{:S(2)}) async-start(s32[32,1,128]{2,1,0:T(1,128)} %bitcast.6), calls=%async_computation | async-start | bytes 32768 | tf_op jit(solution)/shard_map/all_to_all | solution.py:164
  100.8 1.0 copy-start
  103.1 85.7 %copy-start.3 = (s32[1,1,2048]{2,1,0:T(1,128)S(1)}, s32[1,1,2048]{2,1,0:T(1,128)}, u32[]{:S(2)}) copy-start(s32[1,1,2048]{2,1,0:T(1,128)} %param.15) | copy-start | bytes 24580
  103.1 86.6 %copy-start.4 = (s32[1,1,2048]{2,1,0:T(1,128)S(1)}, s32[1,1,2048]{2,1,0:T(1,128)}, u32[]{:S(2)}) copy-start(s32[1,1,2048]{2,1,0:T(1,128)} %param.17) | copy-start | bytes 24580
  103.1 86.6 %copy-start.2 = (f32[1,1,2048]{2,1,0:T(1,128)S(1)}, f32[1,1,2048]{2,1,0:T(1,128)}, u32[]{:S(2)}) copy-start(f32[1,1,2048]{2,1,0:T(1,128)} %param.16) | copy-start | bytes 24580
  103.2 82.9 %all-to-all-start.1 = ((f32[4,24,32,128]{3,1,0,2:T(8,128)}), f32[4,24,32,128]{3,1,0,2:T(8,128)S(1)}, u32[]{:S(2)}, u32[]{:S(2)}) async-start(f32[4,24,32,128]{3,1,0,2:T(8,128)} %pad_maximum_fusion.9), calls=%async_computation.1 | async-start | bytes 3145728 | tf_op jit(solution)/shard_map/all_to_all | solution.py:174
  186.0 36.0 %collective-permute-start.1 = (f32[4,24,32,128]{3,1,0,2:T(8,128)S(1)}, f32[4,24,32,128]{3,1,0,2:T(8,128)S(1)}, u32[]{:S(2)}, u32[]{:S(2)}) collective-permute-start(f32[4,24,32,128]{3,1,0,2:T(8,128)S(1)} %all-to-all-done.1), channel_id=1, source_target_pairs={{0,256},{256,0},{1,257},{257,1},{2,258},{258,2},{3,259},{259,3},{4... | collective-permute-start | bytes 4718600 | tf_op jit(solution)/shard_map/ppermute | solution.py:22
  251.5 7.8 %collective-permute-start.2 = (f32[6,4,1,128]{3,2,1,0:T(1,128)S(1)}, f32[6,4,1,128]{3,2,1,0:T(1,128)S(1)}, u32[]{:S(2)}, u32[]{:S(2)}) collective-permute-start(f32[6,4,1,128]{3,2,1,0:T(1,128)S(1)} %get-tuple-element.17), channel_id=1, source_target_pairs={{32,0},{64,32},{96,64},{128,96},{160,128},{192,160},{224,192},{33,... | collective-permute-start | bytes 36872 | tf_op jit(solution)/shard_map/ppermute | solution.py:33
  256.2 3.9 collective-permute-start.3
  264.9 21.0 %collective-permute-start.4 = (f32[6,4,130,1]{2,1,3,0:T(4,128)S(1)}, f32[6,4,130,1]{2,1,3,0:T(4,128)S(1)}, u32[]{:S(2)}, u32[]{:S(2)}) collective-permute-start(f32[6,4,130,1]{2,1,3,0:T(4,128)S(1)} %copy.104), channel_id=1, source_target_pairs={{1,0},{2,1},{3,2},{4,3},{5,4},{6,5},{7,6},{8,7},{9,8},{10,9},{11,1... | collective-permute-start | bytes 37448 | tf_op jit(solution)/shard_map/ppermute | solution.py:33
  268.5 19.1 %collective-permute-start.5 = (f32[6,4,130,1]{2,1,3,0:T(4,128)S(1)}, f32[6,4,130,1]{2,1,3,0:T(4,128)S(1)}, u32[]{:S(2)}, u32[]{:S(2)}) collective-permute-start(f32[6,4,130,1]{2,1,3,0:T(4,128)S(1)} %copy.106), channel_id=1, source_target_pairs={{0,1},{1,2},{2,3},{3,4},{4,5},{5,6},{6,7},{7,8},{8,9},{9,10},{10,1... | collective-permute-start | bytes 37448 | tf_op jit(solution)/shard_map/ppermute | solution.py:32
  293.1 6.8 %collective-permute-start.6 = (f32[3,4,1,128]{3,2,1,0:T(1,128)S(1)}, f32[3,4,1,128]{3,2,1,0:T(1,128)S(1)}, u32[]{:S(2)}, u32[]{:S(2)}) collective-permute-start(f32[3,4,1,128]{3,2,1,0:T(1,128)S(1)} %get-tuple-element.15), channel_id=1, source_target_pairs={{32,0},{64,32},{96,64},{128,96},{160,128},{192,160},{224,192},{33,... | collective-permute-start | bytes 18440 | tf_op jit(solution)/shard_map/ppermute | solution.py:33
  295.0 5.5 %collective-permute-start.7 = (f32[3,4,1,128]{3,2,1,0:T(1,128)S(1)}, f32[3,4,1,128]{3,2,1,0:T(1,128)S(1)}, u32[]{:S(2)}, u32[]{:S(2)}) collective-permute-start(f32[3,4,1,128]{3,2,1,0:T(1,128)S(1)} %get-tuple-element.14), channel_id=1, source_target_pairs={{0,32},{32,64},{64,96},{96,128},{128,160},{160,192},{192,224},{1,3... | collective-permute-start | bytes 18440 | tf_op jit(solution)/shard_map/ppermute | solution.py:32
  303.7 8.9 %collective-permute-start.8 = (f32[3,4,130,1]{2,1,3,0:T(4,128)S(1)}, f32[3,4,130,1]{2,1,3,0:T(4,128)S(1)}, u32[]{:S(2)}, u32[]{:S(2)}) collective-permute-start(f32[3,4,130,1]{2,1,3,0:T(4,128)S(1)} %copy.109), channel_id=1, source_target_pairs={{1,0},{2,1},{3,2},{4,3},{5,4},{6,5},{7,6},{8,7},{9,8},{10,9},{11,1... | collective-permute-start | bytes 18728 | tf_op jit(solution)/shard_map/ppermute | solution.py:33
  306.6 7.3 %collective-permute-start.9 = (f32[3,4,130,1]{2,1,3,0:T(4,128)S(1)}, f32[3,4,130,1]{2,1,3,0:T(4,128)S(1)}, u32[]{:S(2)}, u32[]{:S(2)}) collective-permute-start(f32[3,4,130,1]{2,1,3,0:T(4,128)S(1)} %copy.111), channel_id=1, source_target_pairs={{0,1},{1,2},{2,3},{3,4},{4,5},{5,6},{6,7},{7,8},{8,9},{9,10},{10,1... | collective-permute-start | bytes 18728 | tf_op jit(solution)/shard_map/ppermute | solution.py:32
  317.1 28.6 %copy-start.1 = (f32[4,128,128]{2,1,0:T(8,128)S(1)}, f32[4,128,128]{2,1,0:T(8,128)}, u32[]{:S(2)}) copy-start(f32[4,128,128]{2,1,0:T(8,128)} %get-tuple-element.9) | copy-start | bytes 786436
  317.1 6.7 %collective-permute-start.10 = (f32[4,1,128]{2,1,0:T(1,128)S(1)}, f32[4,1,128]{2,1,0:T(1,128)S(1)}, u32[]{:S(2)}, u32[]{:S(2)}) collective-permute-start(f32[4,1,128]{2,1,0:T(1,128)S(1)} %get-tuple-element.29), channel_id=1, source_target_pairs={{0,32},{32,64},{64,96},{96,128},{128,160},{160,192},{192,224},{1,3... | collective-permute-start | bytes 6152 | tf_op jit(solution)/shard_map/ppermute | solution.py:32
  321.9 4.9 %collective-permute-start.11 = (f32[4,1,128]{2,1,0:T(1,128)S(1)}, f32[4,1,128]{2,1,0:T(1,128)S(1)}, u32[]{:S(2)}, u32[]{:S(2)}) collective-permute-start(f32[4,1,128]{2,1,0:T(1,128)S(1)} %get-tuple-element.30), channel_id=1, source_target_pairs={{32,0},{64,32},{96,64},{128,96},{160,128},{192,160},{224,192},{33,... | collective-permute-start | bytes 6152 | tf_op jit(solution)/shard_map/ppermute | solution.py:33
  327.7 11.4 %collective-permute-start.12 = (f32[4,130,1]{2,1,0:T(8,128)}, f32[4,130,1]{2,1,0:T(8,128)S(1)}, u32[]{:S(2)}, u32[]{:S(2)}) collective-permute-start(f32[4,130,1]{2,1,0:T(8,128)} %get-tuple-element.27), channel_id=1, source_target_pairs={{0,1},{1,2},{2,3},{3,4},{4,5},{5,6},{6,7},{7,8},{8,9},{9,10},{10,1... | collective-permute-start | bytes 6248 | tf_op jit(solution)/shard_map/ppermute | solution.py:32
  333.7 12.1 %collective-permute-start.13 = (f32[4,130,1]{2,1,0:T(8,128)}, f32[4,130,1]{2,1,0:T(8,128)S(1)}, u32[]{:S(2)}, u32[]{:S(2)}) collective-permute-start(f32[4,130,1]{2,1,0:T(8,128)} %get-tuple-element.28), channel_id=1, source_target_pairs={{1,0},{2,1},{3,2},{4,3},{5,4},{6,5},{7,6},{8,7},{9,8},{10,9},{11,1... | collective-permute-start | bytes 6248 | tf_op jit(solution)/shard_map/ppermute | solution.py:33
  346.2 7.0 %collective-permute-start.14 = (f32[1,4]{1,0:T(1,128)S(1)}, f32[1,4]{1,0:T(1,128)S(1)}, u32[]{:S(2)}, u32[]{:S(2)}) collective-permute-start(f32[1,4]{1,0:T(1,128)S(1)} %multiply_bitcast_fusion), channel_id=1, source_target_pairs={{0,1},{1,0},{2,3},{3,2},{4,5},{5,4},{6,7},{7,6},{8,9},{9,8},{10,11... | collective-permute-start | bytes 56 | tf_op jit(solution)/shard_map/ppermute | solution.py:43
  353.2 7.1 %collective-permute-start.15 = (f32[2,4]{1,0:T(2,128)S(1)}, f32[2,4]{1,0:T(2,128)S(1)}, u32[]{:S(2)}, u32[]{:S(2)}) collective-permute-start(f32[2,4]{1,0:T(2,128)S(1)} %maximum_select_fusion.7), channel_id=1, source_target_pairs={{0,2},{1,3},{2,0},{3,1},{4,6},{5,7},{6,4},{7,5},{8,10},{9,11},{10,... | collective-permute-start | bytes 104 | tf_op jit(solution)/shard_map/ppermute | solution.py:43
  360.3 5.2 %collective-permute-start.16 = (f32[4,4]{1,0:T(4,128)S(1)}, f32[4,4]{1,0:T(4,128)S(1)}, u32[]{:S(2)}, u32[]{:S(2)}) collective-permute-start(f32[4,4]{1,0:T(4,128)S(1)} %maximum_select_fusion.4), channel_id=1, source_target_pairs={{0,4},{1,5},{2,6},{3,7},{4,0},{5,1},{6,2},{7,3},{8,12},{9,13},{10,... | collective-permute-start | bytes 200 | tf_op jit(solution)/shard_map/ppermute | solution.py:43
  365.5 8.3 %collective-permute-start.17 = (f32[8,4]{1,0:T(8,128)S(1)}, f32[8,4]{1,0:T(8,128)S(1)}, u32[]{:S(2)}, u32[]{:S(2)}) collective-permute-start(f32[8,4]{1,0:T(8,128)S(1)} %maximum_select_fusion.2), channel_id=1, source_target_pairs={{0,8},{1,9},{2,10},{3,11},{4,12},{5,13},{6,14},{7,15},{8,0},{9,1},... | collective-permute-start | bytes 392 | tf_op jit(solution)/shard_map/ppermute | solution.py:43
  373.9 13.0 %collective-permute-start.18 = (f32[16,4]{0,1:T(4,128)S(1)}, f32[16,4]{0,1:T(4,128)S(1)}, u32[]{:S(2)}, u32[]{:S(2)}) collective-permute-start(f32[16,4]{0,1:T(4,128)S(1)} %maximum_select_fusion.5), channel_id=1, source_target_pairs={{0,16},{1,17},{2,18},{3,19},{4,20},{5,21},{6,22},{7,23},{8,24},{9,... | collective-permute-start | bytes 776 | tf_op jit(solution)/shard_map/ppermute | solution.py:43
  387.0 8.6 %collective-permute-start.19 = (f32[1,32,4]{1,2,0:T(4,128)S(1)}, f32[1,32,4]{1,2,0:T(4,128)S(1)}, u32[]{:S(2)}, u32[]{:S(2)}) collective-permute-start(f32[1,32,4]{1,2,0:T(4,128)S(1)} %maximum_select_fusion.6), channel_id=1, source_target_pairs={{0,32},{32,0},{64,96},{96,64},{128,160},{160,128},{192,224},{224,1... | collective-permute-start | bytes 1544 | tf_op jit(solution)/shard_map/ppermute | solution.py:43
  395.6 4.9 %collective-permute-start.20 = (f32[2,32,4]{1,2,0:T(4,128)S(1)}, f32[2,32,4]{1,2,0:T(4,128)S(1)}, u32[]{:S(2)}, u32[]{:S(2)}) collective-permute-start(f32[2,32,4]{1,2,0:T(4,128)S(1)} %maximum_select_fusion.3), channel_id=1, source_target_pairs={{0,64},{32,96},{64,0},{96,32},{128,192},{160,224},{192,128},{224,1... | collective-permute-start | bytes 3080 | tf_op jit(solution)/shard_map/ppermute | solution.py:43
  400.5 6.0 %collective-permute-start.21 = (f32[4,32,4]{1,2,0:T(4,128)S(1)}, f32[4,32,4]{1,2,0:T(4,128)S(1)}, u32[]{:S(2)}, u32[]{:S(2)}) collective-permute-start(f32[4,32,4]{1,2,0:T(4,128)S(1)} %maximum_select_fusion.1), channel_id=1, source_target_pairs={{0,128},{32,160},{64,192},{96,224},{128,0},{160,32},{192,64},{224,... | collective-permute-start | bytes 6152 | tf_op jit(solution)/shard_map/ppermute | solution.py:43

commit v2 on v1

--- a/solution.py
+++ b/solution.py
@@ -158,24 +158,21 @@
     base_cell = (src_row[0, 0] * cols_dev + src_col[0, 0]).reshape(blocks, block_cells)
     weight_ids = weight_id[0, 0].reshape(blocks, block_cells)
     empty = jnp.zeros((slot_count, block_cells), jnp.int32)
-    requests = partner_2(
-        empty.at[slot_of].set(base_cell).reshape(n_lon, capacity * block_cells), "panel", 0
-    )
+    asked = jnp.stack(
+        [empty.at[slot_of].set(base_cell), empty.at[slot_of].set(weight_ids)], axis=1
+    ).reshape(n_lon, capacity, 2, block_cells)
+    requests = partner_2(asked, "panel", 0)
     requests = lax.all_to_all(requests, "lon", split_axis=0, concat_axis=0, tiled=True)
-    served = jnp.stack(
-        tuple(
-            (
-                jnp.take(flat_cells, requests + offset, axis=1)
-                for offset in (0, 1, cols_dev, cols_dev + 1)
-            )
-        ),
-        axis=0,
-    )
-    served = lax.all_to_all(served, "lon", split_axis=2, concat_axis=2, tiled=True)
+    cells_asked = requests[:, :, 0, :]
+    frac_lat, frac_lon = fractions(requests[:, :, 1, :])
+    corners = [
+        jnp.take(flat_cells, cells_asked + offset, axis=1)
+        for offset in (0, 1, cols_dev, cols_dev + 1)
+    ]
+    served = bilinear(*corners, frac_lat, frac_lon)
+    served = lax.all_to_all(served, "lon", split_axis=1, concat_axis=1, tiled=True)
     served = partner_2(served, "panel", 0)
-    picked = served.reshape(4, channels, slot_count, block_cells)[:, :, slot_of, :]
-    frac_lat, frac_lon = fractions(weight_ids)
-    values = bilinear(picked[0], picked[1], picked[2], picked[3], frac_lat, frac_lon)
+    values = served.reshape(channels, slot_count, block_cells)[:, slot_of, :]
     values = values.reshape(6, levels, blocks * block_cells)
     turn = border_angle[0, 0]
     cos_angle = jnp.cos(turn)

time: 414 us -> 348 us (0.84)
  waiting for transfers between devices: 148 us -> 71.2 us
  starting transfers between devices: 116 us -> 126 us
    all_to_all x1, waiting for transfers between devices: 75.1 us -> 23 us  [shards(): lax.all_to_all(served, 'lon', split_axis=1, concat_axis=1, tiled=True)]
    ppermute x2, waiting for transfers between devices: 33.2 us -> 15.4 us  [partner_2(): return lax.ppermute(block, axis, route)]
    ppermute x8, starting transfers between devices: 41.6 us -> 48.8 us  [doubling_gather(): other = lax.ppermute(block, axis, [(i, i ^ step) for i in range(count)])]
    ppermute x8, waiting for transfers between devices: 18.2 us -> 11 us  [doubling_gather(): other = lax.ppermute(block, axis, [(i, i ^ step) for i in range(count)])]
    reshape x3 -> x0, local copies, waits for them, and re-layouts: 6.03 us -> none  [the longest x2 5.96 us: shards(): served.reshape(4, channels, slot_count, block_cells)[:, :, slot_of, :]]
  transfers between devices with their start and end apart: 24 -> 24, of which waited for: 17 -> 17; matrix products, arithmetic and copies ran while one was open for 7% -> 8% of each run, Pallas kernels for 0% -> 0%
where the time goes in v2:
time: 348 us; the launch traced here: 345 us
  starting transfers between devices  126 us (36%)
  local copies, waits for them, and re-layouts  119 us (34%)
  waiting for transfers between devices  71.2 us (20%)
  other arithmetic  25.5 us (7%)
    gather x8, local copies, waits for them, and re-layouts, shards(): jnp.take(flat_cells, cells_asked + offset, axis=1)  61.7 us
    ppermute x8, starting transfers between devices, doubling_gather(): other = lax.ppermute(block, axis, [(i, i ^ step) for i in range(count)])  48.8 us
    ppermute x6, starting transfers between devices, padded_2(): before = lax.ppermute(last, axis, up)  30.3 us
    all_to_all x1, waiting for transfers between devices, shards(): lax.all_to_all(served, 'lon', split_axis=1, concat_axis=1, tiled=True)  23 us
    all_to_all x1, starting transfers between devices, shards(): lax.all_to_all(requests, 'lon', split_axis=0, concat_axis=0, tiled=True)  17.9 us
    scatter x2, local copies, waits for them, and re-layouts, shards(): flat_cells.at[:, dest_cell[0, 0]].set(rotated)  17.3 us
    ppermute x6, starting transfers between devices, padded_2(): after = lax.ppermute(leading, axis, down)  15.5 us
    ppermute x2, waiting for transfers between devices, partner_2(): return lax.ppermute(block, axis, route)  15.4 us
  transfers between devices with their start and end apart: 24, of which 17 were waited for; matrix products, arithmetic and copies ran while one was open for 8% of the time, Pallas kernels for 0%

profile of v2, /device:TPU:1, one launch (start us, length us, event | category | flops | bytes accessed | tf_op | source)
XLA Modules:
  0.0 344.9 jit_solution(5541399308872923284)
XLA Ops:
  7.1 3.9 %collective-permute-start = (s32[32,2,2,64]{3,1,2,0:T(2,128)S(1)}, s32[32,2,2,64]{3,1,2,0:T(2,128)S(1)}, u32[]{:S(2)}, u32[]{:S(2)}) collective-permute-start(s32[32,2,2,64]{3,1,2,0:T(2,128)S(1)} %pad_add_fusion), channel_id=1, source_target_pairs={{0,256},{256,0},{1,257},{257,1},{2,258},{258,2},{3,259},{259,3},{4... | collective-permute-start | bytes 98312 | tf_op jit(solution)/shard_map/ppermute | solution.py:22
  11.1 1.6 collective-permute-done
  13.4 17.9 %all-to-all-start = ((s32[32,1,256]{2,1,0:T(1,128)}), s32[32,1,256]{2,1,0:T(1,128)S(1)}, u32[]{:S(2)}, u32[]{:S(2)}) async-start(s32[32,1,256]{2,1,0:T(1,128)} %reshape.856), calls=%async_computation | async-start | bytes 65536 | tf_op jit(solution)/shard_map/all_to_all | solution.py:165
  31.3 2.3 copy.277
  33.7 4.6 %copy.185 = f32[24,16384]{0,1:T(8,128)} copy(f32[24,16384]{1,0:T(8,128)S(1)} %bitcast.193) | data formatting | bytes 3145728 | tf_op jit(solution)/shard_map/reshape;squeeze | solution.py:151
  38.3 6.8 %all-to-all-done = s32[32,1,256]{2,1,0:T(1,128)S(1)} async-done(((s32[32,1,256]{2,1,0:T(1,128)}), s32[32,1,256]{2,1,0:T(1,128)S(1)}, u32[]{:S(2)}, u32[]{:S(2)}) %all-to-all-start) | async-done | bytes 32800 | tf_op jit(solution)/shard_map/all_to_all | solution.py:165
  46.8 14.1 %gather_fusion.1 = f32[4096,24]{1,0:T(8,128)S(1)} fusion(f32[24,16384]{0,1:T(8,128)} %copy.185, s32[4096]{0:T(1024)S(1)} %get-tuple-element.50), kind=kCustom, calls=%fused_computation.clone | custom fusion | bytes 802816 | tf_op jit(solution)/shard_map/jit(_take)/gather | solution.py:169
  61.6 14.2 %gather_fusion.2 = f32[4096,24]{1,0:T(8,128)S(1)} fusion(f32[24,16384]{0,1:T(8,128)} %copy.185, s32[4096]{0:T(1024)S(1)} %get-tuple-element.49), kind=kCustom, calls=%fused_computation.1.clone | custom fusion | bytes 802816 | tf_op jit(solution)/shard_map/jit(_take)/gather | solution.py:169
  77.5 14.1 %gather_fusion.3 = f32[4096,24]{1,0:T(8,128)S(1)} fusion(f32[24,16384]{0,1:T(8,128)} %copy.185, s32[4096]{0:T(1024)S(1)} %get-tuple-element.48), kind=kCustom, calls=%fused_computation.2.clone | custom fusion | bytes 802816 | tf_op jit(solution)/shard_map/jit(_take)/gather | solution.py:169
  93.1 14.1 %gather_fusion.4 = f32[4096,24]{1,0:T(8,128)S(1)} fusion(f32[24,16384]{0,1:T(8,128)} %copy.185, s32[4096]{0:T(1024)S(1)} %get-tuple-element.47), kind=kCustom, calls=%fused_computation.3.clone | custom fusion | bytes 802816 | tf_op jit(solution)/shard_map/jit(_take)/gather | solution.py:169
  109.1 2.2 fusion.133
  112.5 7.2 %all-to-all-start.1 = ((f32[32,1,3072]{2,1,0:T(1,128)}), f32[32,1,3072]{2,1,0:T(1,128)S(1)}, u32[]{:S(2)}, u32[]{:S(2)}) async-start(f32[32,1,3072]{2,1,0:T(1,128)} %reshape.858), calls=%async_computation.1 | async-start | bytes 786432 | tf_op jit(solution)/shard_map/all_to_all | solution.py:173
  120.2 23.0 %all-to-all-done.1 = f32[32,1,3072]{2,1,0:T(1,128)S(1)} async-done(((f32[32,1,3072]{2,1,0:T(1,128)}), f32[32,1,3072]{2,1,0:T(1,128)S(1)}, u32[]{:S(2)}, u32[]{:S(2)}) %all-to-all-start.1) | async-done | bytes 393248 | tf_op jit(solution)/shard_map/all_to_all | solution.py:173
  145.7 2.2 collective-permute-start.1
  148.0 13.7 %collective-permute-done.1 = f32[24,32,2,64]{3,1,2,0:T(8,128)S(1)} collective-permute-done((f32[24,32,2,64]{3,1,2,0:T(8,128)S(1)}, f32[24,32,2,64]{3,1,2,0:T(8,128)S(1)}, u32[]{:S(2)}, u32[]{:S(2)}) %collective-permute-start.1) | collective-permute-done | bytes 393248 | tf_op jit(solution)/shard_map/ppermute | solution.py:22
  164.0 12.1 %scatter_fusion = f32[24,16384]{0,1:T(8,128)} fusion(f32[24,16384]{0,1:T(8,128)} %copy.185, s32[2048]{0:T(1024)S(1)} %bitcast.217, f32[2048,24]{1,0:T(8,128)S(1)} %copy.186), kind=kCustom, calls=%fused_computation.7 | custom fusion | bytes 598016 | tf_op jit(solution)/shard_map/scatter | solution.py:191
  176.2 5.1 %copy.187 = f32[24,16384]{1,0:T(8,128)S(1)} copy(f32[24,16384]{0,1:T(8,128)} %scatter_fusion) | data formatting | bytes 3145728 | tf_op jit(solution)/shard_map/scatter | solution.py:191
  181.6 7.8 %collective-permute-start.2 = (f32[6,4,1,128]{3,2,1,0:T(1,128)S(1)}, f32[6,4,1,128]{3,2,1,0:T(1,128)S(1)}, u32[]{:S(2)}, u32[]{:S(2)}) collective-permute-start(f32[6,4,1,128]{3,2,1,0:T(1,128)S(1)} %get-tuple-element.17), channel_id=1, source_target_pairs={{32,0},{64,32},{96,64},{128,96},{160,128},{192,160},{224,192},{33,... | collective-permute-start | bytes 36872 | tf_op jit(solution)/shard_map/ppermute | solution.py:33
  189.4 3.1 collective-permute-start.3
  193.5 2.3 fusion.125
  195.7 2.3 copy.188
  199.4 2.3 copy.190
  201.7 5.5 %collective-permute-start.5 = (f32[6,4,130,1]{2,1,3,0:T(4,128)S(1)}, f32[6,4,130,1]{2,1,3,0:T(4,128)S(1)}, u32[]{:S(2)}, u32[]{:S(2)}) collective-permute-start(f32[6,4,130,1]{2,1,3,0:T(4,128)S(1)} %copy.190), channel_id=1, source_target_pairs={{0,1},{1,2},{2,3},{3,4},{4,5},{5,6},{6,7},{7,8},{8,9},{9,10},{10,1... | collective-permute-start | bytes 37448 | tf_op jit(solution)/shard_map/ppermute | solution.py:32
  207.2 6.6 %slice_multiply_fusion = f32[4,16384]{0,1:T(8,128)} fusion(f32[24,16384]{0,1:T(8,128)} %scatter_fusion), kind=kLoop, calls=%fused_computation.8 | loop fusion | flops 65536 | bytes 524288 | tf_op jit(solution)/shard_map/mul | solution.py:198
  213.8 5.2 %copy.192 = f32[1,4,128,128]{3,2,1,0:T(8,128)S(1)} copy(f32[1,4,128,128]{1,3,2,0:T(8,128)} %bitcast.188) | data formatting | bytes 524288 | tf_op jit(solution)/shard_map/mul | solution.py:198
  219.1 1.8 copy.189
  220.8 1.8 copy.191
  222.6 3.5 %fusion.4 = f32[6,4,128,128]{3,2,1,0:T(8,128)S(1)} fusion(f32[6,4,128,128]{3,2,1,0:T(8,128)S(1)} %bitcast.191, f32[6,4,130,1]{3,2,1,0:T(8,128)} %copy.191, f32[6,4,1,128]{3,2,1,0:T(1,128)S(1)} %collective-permute-done.2, f32[6,4,1,128]{3,2,1,0:T(1,128)S(1)} %collective-permute-done.3, f32[6,4,130,1]{3,2,1,0:T(8,128)} %copy.189, f32[128]{0:T(128)S(1)} %fusion.122, ...), kind=kLoop, calls=%fused_computation.20 | loop fusion | flops 7864320 | bytes 3457920 | tf_op jit(solution)/shard_map/add | solution.py:197
  226.3 1.9 collective-permute-start.6
  228.2 4.8 %collective-permute-start.7 = (f32[3,4,1,128]{3,2,1,0:T(1,128)S(1)}, f32[3,4,1,128]{3,2,1,0:T(1,128)S(1)}, u32[]{:S(2)}, u32[]{:S(2)}) collective-permute-start(f32[3,4,1,128]{3,2,1,0:T(1,128)S(1)} %get-tuple-element.14), channel_id=1, source_target_pairs={{0,32},{32,64},{64,96},{96,128},{128,160},{160,192},{192,224},{1,3... | collective-permute-start | bytes 18440 | tf_op jit(solution)/shard_map/ppermute | solution.py:32
  239.8 6.2 %collective-permute-start.9 = (f32[3,4,130,1]{2,1,3,0:T(4,128)S(1)}, f32[3,4,130,1]{2,1,3,0:T(4,128)S(1)}, u32[]{:S(2)}, u32[]{:S(2)}) collective-permute-start(f32[3,4,130,1]{2,1,3,0:T(4,128)S(1)} %copy.195), channel_id=1, source_target_pairs={{0,1},{1,2},{2,3},{3,4},{4,5},{5,6},{6,7},{7,8},{8,9},{9,10},{10,1... | collective-permute-start | bytes 18728 | tf_op jit(solution)/shard_map/ppermute | solution.py:32
  248.5 2.1 broadcast_divide_fusion
  250.6 4.7 %collective-permute-start.10 = (f32[4,1,128]{2,1,0:T(1,128)S(1)}, f32[4,1,128]{2,1,0:T(1,128)S(1)}, u32[]{:S(2)}, u32[]{:S(2)}) collective-permute-start(f32[4,1,128]{2,1,0:T(1,128)S(1)} %get-tuple-element.29), channel_id=1, source_target_pairs={{0,32},{32,64},{64,96},{96,128},{128,160},{160,192},{192,224},{1,3... | collective-permute-start | bytes 6152 | tf_op jit(solution)/shard_map/ppermute | solution.py:32
  255.3 1.9 collective-permute-start.11
  257.3 2.9 collective-permute-done.11
  261.1 6.0 %collective-permute-start.12 = (f32[4,130,1]{2,1,0:T(8,128)}, f32[4,130,1]{2,1,0:T(8,128)S(1)}, u32[]{:S(2)}, u32[]{:S(2)}) collective-permute-start(f32[4,130,1]{2,1,0:T(8,128)} %get-tuple-element.27), channel_id=1, source_target_pairs={{0,1},{1,2},{2,3},{3,4},{4,5},{5,6},{6,7},{7,8},{8,9},{9,10},{10,1... | collective-permute-start | bytes 6248 | tf_op jit(solution)/shard_map/ppermute | solution.py:32
  268.5 4.1 %collective-permute-done.12 = f32[4,130,1]{2,1,0:T(8,128)S(1)} collective-permute-done((f32[4,130,1]{2,1,0:T(8,128)}, f32[4,130,1]{2,1,0:T(8,128)S(1)}, u32[]{:S(2)}, u32[]{:S(2)}) %collective-permute-start.12) | collective-permute-done | bytes 2112 | tf_op jit(solution)/shard_map/ppermute | solution.py:32
  272.5 6.7 %collective-permute-done.13 = f32[4,130,1]{2,1,0:T(8,128)S(1)} collective-permute-done((f32[4,130,1]{2,1,0:T(8,128)}, f32[4,130,1]{2,1,0:T(8,128)S(1)}, u32[]{:S(2)}, u32[]{:S(2)}) %collective-permute-start.13) | collective-permute-done | bytes 2112 | tf_op jit(solution)/shard_map/ppermute | solution.py:33
  279.6 6.0 %collective-permute-start.14 = (f32[1,4]{1,0:T(1,128)S(1)}, f32[1,4]{1,0:T(1,128)S(1)}, u32[]{:S(2)}, u32[]{:S(2)}) collective-permute-start(f32[1,4]{1,0:T(1,128)S(1)} %multiply_bitcast_fusion), channel_id=1, source_target_pairs={{0,1},{1,0},{2,3},{3,2},{4,5},{5,4},{6,7},{7,6},{8,9},{9,8},{10,11... | collective-permute-start | bytes 56 | tf_op jit(solution)/shard_map/ppermute | solution.py:43
  286.6 6.1 %collective-permute-start.15 = (f32[2,4]{1,0:T(2,128)S(1)}, f32[2,4]{1,0:T(2,128)S(1)}, u32[]{:S(2)}, u32[]{:S(2)}) collective-permute-start(f32[2,4]{1,0:T(2,128)S(1)} %maximum_select_fusion.7), channel_id=1, source_target_pairs={{0,2},{1,3},{2,0},{3,1},{4,6},{5,7},{6,4},{7,5},{8,10},{9,11},{10,... | collective-permute-start | bytes 104 | tf_op jit(solution)/shard_map/ppermute | solution.py:43
  293.7 3.2 collective-permute-start.16
  296.9 2.0 collective-permute-done.16
  298.9 7.1 %collective-permute-start.17 = (f32[8,4]{1,0:T(8,128)S(1)}, f32[8,4]{1,0:T(8,128)S(1)}, u32[]{:S(2)}, u32[]{:S(2)}) collective-permute-start(f32[8,4]{1,0:T(8,128)S(1)} %maximum_select_fusion.2), channel_id=1, source_target_pairs={{0,8},{1,9},{2,10},{3,11},{4,12},{5,13},{6,14},{7,15},{8,0},{9,1},... | collective-permute-start | bytes 392 | tf_op jit(solution)/shard_map/ppermute | solution.py:43
  307.4 9.7 %collective-permute-start.18 = (f32[16,4]{0,1:T(4,128)S(1)}, f32[16,4]{0,1:T(4,128)S(1)}, u32[]{:S(2)}, u32[]{:S(2)}) collective-permute-start(f32[16,4]{0,1:T(4,128)S(1)} %maximum_select_fusion.5), channel_id=1, source_target_pairs={{0,16},{1,17},{2,18},{3,19},{4,20},{5,21},{6,22},{7,23},{8,24},{9,... | collective-permute-start | bytes 776 | tf_op jit(solution)/shard_map/ppermute | solution.py:43
  317.0 3.4 collective-permute-done.18
  320.5 7.8 %collective-permute-start.19 = (f32[1,32,4]{1,2,0:T(4,128)S(1)}, f32[1,32,4]{1,2,0:T(4,128)S(1)}, u32[]{:S(2)}, u32[]{:S(2)}) collective-permute-start(f32[1,32,4]{1,2,0:T(4,128)S(1)} %maximum_select_fusion.6), channel_id=1, source_target_pairs={{0,32},{32,0},{64,96},{96,64},{128,160},{160,128},{192,224},{224,1... | collective-permute-start | bytes 1544 | tf_op jit(solution)/shard_map/ppermute | solution.py:43
  329.1 3.9 %collective-permute-start.20 = (f32[2,32,4]{1,2,0:T(4,128)S(1)}, f32[2,32,4]{1,2,0:T(4,128)S(1)}, u32[]{:S(2)}, u32[]{:S(2)}) collective-permute-start(f32[2,32,4]{1,2,0:T(4,128)S(1)} %maximum_select_fusion.3), channel_id=1, source_target_pairs={{0,64},{32,96},{64,0},{96,32},{128,192},{160,224},{192,128},{224,1... | collective-permute-start | bytes 3080 | tf_op jit(solution)/shard_map/ppermute | solution.py:43
  334.0 5.0 %collective-permute-start.21 = (f32[4,32,4]{1,2,0:T(4,128)S(1)}, f32[4,32,4]{1,2,0:T(4,128)S(1)}, u32[]{:S(2)}, u32[]{:S(2)}) collective-permute-start(f32[4,32,4]{1,2,0:T(4,128)S(1)} %maximum_select_fusion.1), channel_id=1, source_target_pairs={{0,128},{32,160},{64,192},{96,224},{128,0},{160,32},{192,64},{224,... | collective-permute-start | bytes 6152 | tf_op jit(solution)/shard_map/ppermute | solution.py:43
  (150 shorter events, 46.5 us)
Async XLA Ops:
  7.1 5.6 %collective-permute-start = (s32[32,2,2,64]{3,1,2,0:T(2,128)S(1)}, s32[32,2,2,64]{3,1,2,0:T(2,128)S(1)}, u32[]{:S(2)}, u32[]{:S(2)}) collective-permute-start(s32[32,2,2,64]{3,1,2,0:T(2,128)S(1)} %pad_add_fusion), channel_id=1, source_target_pairs={{0,256},{256,0},{1,257},{257,1},{2,258},{258,2},{3,259},{259,3},{4... | collective-permute-start | bytes 98312 | tf_op jit(solution)/shard_map/ppermute | solution.py:22
  13.4 31.7 %all-to-all-start = ((s32[32,1,256]{2,1,0:T(1,128)}), s32[32,1,256]{2,1,0:T(1,128)S(1)}, u32[]{:S(2)}, u32[]{:S(2)}) async-start(s32[32,1,256]{2,1,0:T(1,128)} %reshape.856), calls=%async_computation | async-start | bytes 65536 | tf_op jit(solution)/shard_map/all_to_all | solution.py:165
  111.3 8.7 %copy-start.1 = (f32[1,1,2048]{2,1,0:T(1,128)S(1)}, f32[1,1,2048]{2,1,0:T(1,128)}, u32[]{:S(2)}) copy-start(f32[1,1,2048]{2,1,0:T(1,128)} %param.16) | copy-start | bytes 24580
  112.5 30.6 %all-to-all-start.1 = ((f32[32,1,3072]{2,1,0:T(1,128)}), f32[32,1,3072]{2,1,0:T(1,128)S(1)}, u32[]{:S(2)}, u32[]{:S(2)}) async-start(f32[32,1,3072]{2,1,0:T(1,128)} %reshape.858), calls=%async_computation.1 | async-start | bytes 786432 | tf_op jit(solution)/shard_map/all_to_all | solution.py:173
  145.3 2.7 copy-start.2
  145.7 16.0 %collective-permute-start.1 = (f32[24,32,2,64]{3,1,2,0:T(8,128)S(1)}, f32[24,32,2,64]{3,1,2,0:T(8,128)S(1)}, u32[]{:S(2)}, u32[]{:S(2)}) collective-permute-start(f32[24,32,2,64]{3,1,2,0:T(8,128)S(1)} %copy.177), channel_id=1, source_target_pairs={{0,256},{256,0},{1,257},{257,1},{2,258},{258,2},{3,259},{259,3},{4... | collective-permute-start | bytes 1179656 | tf_op jit(solution)/shard_map/ppermute | solution.py:22
  181.6 10.9 %collective-permute-start.2 = (f32[6,4,1,128]{3,2,1,0:T(1,128)S(1)}, f32[6,4,1,128]{3,2,1,0:T(1,128)S(1)}, u32[]{:S(2)}, u32[]{:S(2)}) collective-permute-start(f32[6,4,1,128]{3,2,1,0:T(1,128)S(1)} %get-tuple-element.17), channel_id=1, source_target_pairs={{32,0},{64,32},{96,64},{128,96},{160,128},{192,160},{224,192},{33,... | collective-permute-start | bytes 36872 | tf_op jit(solution)/shard_map/ppermute | solution.py:33
  189.4 3.9 %collective-permute-start.3 = (f32[6,4,1,128]{3,2,1,0:T(1,128)S(1)}, f32[6,4,1,128]{3,2,1,0:T(1,128)S(1)}, u32[]{:S(2)}, u32[]{:S(2)}) collective-permute-start(f32[6,4,1,128]{3,2,1,0:T(1,128)S(1)} %get-tuple-element.16), channel_id=1, source_target_pairs={{0,32},{32,64},{64,96},{96,128},{128,160},{160,192},{192,224},{1,3... | collective-permute-start | bytes 36872 | tf_op jit(solution)/shard_map/ppermute | solution.py:32
  198.1 21.0 %collective-permute-start.4 = (f32[6,4,130,1]{2,1,3,0:T(4,128)S(1)}, f32[6,4,130,1]{2,1,3,0:T(4,128)S(1)}, u32[]{:S(2)}, u32[]{:S(2)}) collective-permute-start(f32[6,4,130,1]{2,1,3,0:T(4,128)S(1)} %copy.188), channel_id=1, source_target_pairs={{1,0},{2,1},{3,2},{4,3},{5,4},{6,5},{7,6},{8,7},{9,8},{10,9},{11,1... | collective-permute-start | bytes 37448 | tf_op jit(solution)/shard_map/ppermute | solution.py:33
  201.7 19.1 %collective-permute-start.5 = (f32[6,4,130,1]{2,1,3,0:T(4,128)S(1)}, f32[6,4,130,1]{2,1,3,0:T(4,128)S(1)}, u32[]{:S(2)}, u32[]{:S(2)}) collective-permute-start(f32[6,4,130,1]{2,1,3,0:T(4,128)S(1)} %copy.190), channel_id=1, source_target_pairs={{0,1},{1,2},{2,3},{3,4},{4,5},{5,6},{6,7},{7,8},{8,9},{9,10},{10,1... | collective-permute-start | bytes 37448 | tf_op jit(solution)/shard_map/ppermute | solution.py:32
  226.3 6.8 %collective-permute-start.6 = (f32[3,4,1,128]{3,2,1,0:T(1,128)S(1)}, f32[3,4,1,128]{3,2,1,0:T(1,128)S(1)}, u32[]{:S(2)}, u32[]{:S(2)}) collective-permute-start(f32[3,4,1,128]{3,2,1,0:T(1,128)S(1)} %get-tuple-element.15), channel_id=1, source_target_pairs={{32,0},{64,32},{96,64},{128,96},{160,128},{192,160},{224,192},{33,... | collective-permute-start | bytes 18440 | tf_op jit(solution)/shard_map/ppermute | solution.py:33
  228.2 5.5 %collective-permute-start.7 = (f32[3,4,1,128]{3,2,1,0:T(1,128)S(1)}, f32[3,4,1,128]{3,2,1,0:T(1,128)S(1)}, u32[]{:S(2)}, u32[]{:S(2)}) collective-permute-start(f32[3,4,1,128]{3,2,1,0:T(1,128)S(1)} %get-tuple-element.14), channel_id=1, source_target_pairs={{0,32},{32,64},{64,96},{96,128},{128,160},{160,192},{192,224},{1,3... | collective-permute-start | bytes 18440 | tf_op jit(solution)/shard_map/ppermute | solution.py:32
  236.9 9.1 %collective-permute-start.8 = (f32[3,4,130,1]{2,1,3,0:T(4,128)S(1)}, f32[3,4,130,1]{2,1,3,0:T(4,128)S(1)}, u32[]{:S(2)}, u32[]{:S(2)}) collective-permute-start(f32[3,4,130,1]{2,1,3,0:T(4,128)S(1)} %copy.193), channel_id=1, source_target_pairs={{1,0},{2,1},{3,2},{4,3},{5,4},{6,5},{7,6},{8,7},{9,8},{10,9},{11,1... | collective-permute-start | bytes 18728 | tf_op jit(solution)/shard_map/ppermute | solution.py:33
  239.8 7.5 %collective-permute-start.9 = (f32[3,4,130,1]{2,1,3,0:T(4,128)S(1)}, f32[3,4,130,1]{2,1,3,0:T(4,128)S(1)}, u32[]{:S(2)}, u32[]{:S(2)}) collective-permute-start(f32[3,4,130,1]{2,1,3,0:T(4,128)S(1)} %copy.195), channel_id=1, source_target_pairs={{0,1},{1,2},{2,3},{3,4},{4,5},{5,6},{6,7},{7,8},{8,9},{9,10},{10,1... | collective-permute-start | bytes 18728 | tf_op jit(solution)/shard_map/ppermute | solution.py:32
  250.6 28.6 %copy-start = (f32[4,128,128]{2,1,0:T(8,128)S(1)}, f32[4,128,128]{2,1,0:T(8,128)}, u32[]{:S(2)}) copy-start(f32[4,128,128]{2,1,0:T(8,128)} %get-tuple-element.9) | copy-start | bytes 786436
  250.6 6.7 %collective-permute-start.10 = (f32[4,1,128]{2,1,0:T(1,128)S(1)}, f32[4,1,128]{2,1,0:T(1,128)S(1)}, u32[]{:S(2)}, u32[]{:S(2)}) collective-permute-start(f32[4,1,128]{2,1,0:T(1,128)S(1)} %get-tuple-element.29), channel_id=1, source_target_pairs={{0,32},{32,64},{64,96},{96,128},{128,160},{160,192},{192,224},{1,3... | collective-permute-start | bytes 6152 | tf_op jit(solution)/shard_map/ppermute | solution.py:32
  255.3 4.9 %collective-permute-start.11 = (f32[4,1,128]{2,1,0:T(1,128)S(1)}, f32[4,1,128]{2,1,0:T(1,128)S(1)}, u32[]{:S(2)}, u32[]{:S(2)}) collective-permute-start(f32[4,1,128]{2,1,0:T(1,128)S(1)} %get-tuple-element.30), channel_id=1, source_target_pairs={{32,0},{64,32},{96,64},{128,96},{160,128},{192,160},{224,192},{33,... | collective-permute-start | bytes 6152 | tf_op jit(solution)/shard_map/ppermute | solution.py:33
  261.1 11.4 %collective-permute-start.12 = (f32[4,130,1]{2,1,0:T(8,128)}, f32[4,130,1]{2,1,0:T(8,128)S(1)}, u32[]{:S(2)}, u32[]{:S(2)}) collective-permute-start(f32[4,130,1]{2,1,0:T(8,128)} %get-tuple-element.27), channel_id=1, source_target_pairs={{0,1},{1,2},{2,3},{3,4},{4,5},{5,6},{6,7},{7,8},{8,9},{9,10},{10,1... | collective-permute-start | bytes 6248 | tf_op jit(solution)/shard_map/ppermute | solution.py:32
  267.2 12.1 %collective-permute-start.13 = (f32[4,130,1]{2,1,0:T(8,128)}, f32[4,130,1]{2,1,0:T(8,128)S(1)}, u32[]{:S(2)}, u32[]{:S(2)}) collective-permute-start(f32[4,130,1]{2,1,0:T(8,128)} %get-tuple-element.28), channel_id=1, source_target_pairs={{1,0},{2,1},{3,2},{4,3},{5,4},{6,5},{7,6},{8,7},{9,8},{10,9},{11,1... | collective-permute-start | bytes 6248 | tf_op jit(solution)/shard_map/ppermute | solution.py:33
  279.6 7.0 %collective-permute-start.14 = (f32[1,4]{1,0:T(1,128)S(1)}, f32[1,4]{1,0:T(1,128)S(1)}, u32[]{:S(2)}, u32[]{:S(2)}) collective-permute-start(f32[1,4]{1,0:T(1,128)S(1)} %multiply_bitcast_fusion), channel_id=1, source_target_pairs={{0,1},{1,0},{2,3},{3,2},{4,5},{5,4},{6,7},{7,6},{8,9},{9,8},{10,11... | collective-permute-start | bytes 56 | tf_op jit(solution)/shard_map/ppermute | solution.py:43
  286.6 7.1 %collective-permute-start.15 = (f32[2,4]{1,0:T(2,128)S(1)}, f32[2,4]{1,0:T(2,128)S(1)}, u32[]{:S(2)}, u32[]{:S(2)}) collective-permute-start(f32[2,4]{1,0:T(2,128)S(1)} %maximum_select_fusion.7), channel_id=1, source_target_pairs={{0,2},{1,3},{2,0},{3,1},{4,6},{5,7},{6,4},{7,5},{8,10},{9,11},{10,... | collective-permute-start | bytes 104 | tf_op jit(solution)/shard_map/ppermute | solution.py:43
  293.7 5.2 %collective-permute-start.16 = (f32[4,4]{1,0:T(4,128)S(1)}, f32[4,4]{1,0:T(4,128)S(1)}, u32[]{:S(2)}, u32[]{:S(2)}) collective-permute-start(f32[4,4]{1,0:T(4,128)S(1)} %maximum_select_fusion.4), channel_id=1, source_target_pairs={{0,4},{1,5},{2,6},{3,7},{4,0},{5,1},{6,2},{7,3},{8,12},{9,13},{10,... | collective-permute-start | bytes 200 | tf_op jit(solution)/shard_map/ppermute | solution.py:43
  298.9 8.3 %collective-permute-start.17 = (f32[8,4]{1,0:T(8,128)S(1)}, f32[8,4]{1,0:T(8,128)S(1)}, u32[]{:S(2)}, u32[]{:S(2)}) collective-permute-start(f32[8,4]{1,0:T(8,128)S(1)} %maximum_select_fusion.2), channel_id=1, source_target_pairs={{0,8},{1,9},{2,10},{3,11},{4,12},{5,13},{6,14},{7,15},{8,0},{9,1},... | collective-permute-start | bytes 392 | tf_op jit(solution)/shard_map/ppermute | solution.py:43
  307.4 13.0 %collective-permute-start.18 = (f32[16,4]{0,1:T(4,128)S(1)}, f32[16,4]{0,1:T(4,128)S(1)}, u32[]{:S(2)}, u32[]{:S(2)}) collective-permute-start(f32[16,4]{0,1:T(4,128)S(1)} %maximum_select_fusion.5), channel_id=1, source_target_pairs={{0,16},{1,17},{2,18},{3,19},{4,20},{5,21},{6,22},{7,23},{8,24},{9,... | collective-permute-start | bytes 776 | tf_op jit(solution)/shard_map/ppermute | solution.py:43
  320.5 8.6 %collective-permute-start.19 = (f32[1,32,4]{1,2,0:T(4,128)S(1)}, f32[1,32,4]{1,2,0:T(4,128)S(1)}, u32[]{:S(2)}, u32[]{:S(2)}) collective-permute-start(f32[1,32,4]{1,2,0:T(4,128)S(1)} %maximum_select_fusion.6), channel_id=1, source_target_pairs={{0,32},{32,0},{64,96},{96,64},{128,160},{160,128},{192,224},{224,1... | collective-permute-start | bytes 1544 | tf_op jit(solution)/shard_map/ppermute | solution.py:43
  329.1 4.9 %collective-permute-start.20 = (f32[2,32,4]{1,2,0:T(4,128)S(1)}, f32[2,32,4]{1,2,0:T(4,128)S(1)}, u32[]{:S(2)}, u32[]{:S(2)}) collective-permute-start(f32[2,32,4]{1,2,0:T(4,128)S(1)} %maximum_select_fusion.3), channel_id=1, source_target_pairs={{0,64},{32,96},{64,0},{96,32},{128,192},{160,224},{192,128},{224,1... | collective-permute-start | bytes 3080 | tf_op jit(solution)/shard_map/ppermute | solution.py:43
  334.0 6.0 %collective-permute-start.21 = (f32[4,32,4]{1,2,0:T(4,128)S(1)}, f32[4,32,4]{1,2,0:T(4,128)S(1)}, u32[]{:S(2)}, u32[]{:S(2)}) collective-permute-start(f32[4,32,4]{1,2,0:T(4,128)S(1)} %maximum_select_fusion.1), channel_id=1, source_target_pairs={{0,128},{32,160},{64,192},{96,224},{128,0},{160,32},{192,64},{224,... | collective-permute-start | bytes 6152 | tf_op jit(solution)/shard_map/ppermute | solution.py:43

commit v3 on v2

--- a/solution.py
+++ b/solution.py
@@ -193,13 +193,35 @@
     inv_own, gain_own = metric(
         lat_pos * rows_dev + jnp.arange(-0, rows_dev + 0, dtype=jnp.int32), total_rows
     )
-    widened = padded_2(filled, (("lat", 2), ("lon", 3)), 1)
-    stepped = filled + diffusivity[None] * lap_shrink(widened, gain_own)
-    stepped = jnp.concatenate([stepped[0:1] + BUOYANCY * filled[3:4], stepped[1:]], axis=0)
-    velocity = padded_2(stepped[0:3], (("lat", 2), ("lon", 3)), 1)
-    divergence = diverge(velocity, inv_own)
-    press_one = -divergence / (4.0 + 2.0 * gain_own)[:, None]
-    press_wide = padded_2(press_one, (("lat", 1), ("lon", 2)), 1)
+    halo = 3
+    total_cols = cols_dev * n_lon
+    row_first = lat_pos * rows_dev
+    col_first = lon_pos * cols_dev
+
+    def inside(reach):
+        rows = row_first - reach + jnp.arange(rows_dev + 2 * reach, dtype=jnp.int32)
+        cols = col_first - reach + jnp.arange(cols_dev + 2 * reach, dtype=jnp.int32)
+        return ((rows >= 0) & (rows < total_rows))[:, None] & ((cols >= 0) & (cols < total_cols))[
+            None, :
+        ]
+
+    stack = jnp.concatenate([filled.reshape(channels, rows_dev, cols_dev), diffusivity], axis=0)
+    wide = padded_2(stack, (("lat", 1), ("lon", 2)), halo)
+    wide_fields = wide[:channels].reshape(6, levels, rows_dev + 2 * halo, cols_dev + 2 * halo)
+    wide_visc = wide[channels:]
+    inv_two, gain_two = metric(row_first + jnp.arange(-2, rows_dev + 2, dtype=jnp.int32), total_rows)
+    inv_one, gain_one = metric(row_first + jnp.arange(-1, rows_dev + 1, dtype=jnp.int32), total_rows)
+    centre = wide_fields[..., 1:-1, 1:-1]
+    stepped_wide = centre + wide_visc[None, :, 1:-1, 1:-1] * lap_shrink(wide_fields, gain_two)
+    stepped_wide = jnp.concatenate(
+        [stepped_wide[0:1] + BUOYANCY * centre[3:4], stepped_wide[1:]], axis=0
+    )
+    velocity = jnp.where(inside(2), stepped_wide[0:3], 0.0)
+    divergence_wide = diverge(velocity, inv_one)
+    press_wide = jnp.where(inside(1), -divergence_wide / (4.0 + 2.0 * gain_one)[:, None], 0.0)
+    divergence = divergence_wide[:, 1:-1, 1:-1]
+    press_one = press_wide[:, 1:-1, 1:-1]
+    stepped = stepped_wide[:, :, 2:-2, 2:-2]
     resid_one = -divergence + lap_shrink(press_wide, gain_own)
     block_sum = jnp.sum(resid_one, axis=(1, 2)) * (1.0 / math.sqrt(rows_dev * cols_dev))
     gathered = doubling_gather(block_sum[None], "lon")

time: 348 us -> 299 us (0.86)
  starting transfers between devices: 126 us -> 80.1 us
  local copies, waits for them, and re-layouts: 119 us -> 112 us
    ppermute x8, starting transfers between devices: 48.8 us -> 31.1 us  [doubling_gather(): other = lax.ppermute(block, axis, [(i, i ^ step) for i in range(count)])]
    ppermute x6 -> x2, starting transfers between devices: 30.3 us -> 14.2 us  [padded_2(): before = lax.ppermute(last, axis, up)]
    ppermute x8, waiting for transfers between devices: 11 us -> 24.7 us  [doubling_gather(): other = lax.ppermute(block, axis, [(i, i ^ step) for i in range(count)])]
    ppermute x6 -> x2, starting transfers between devices: 15.5 us -> 3.2 us  [padded_2(): after = lax.ppermute(leading, axis, down)]
    unnamed x15 -> x48, local copies, waits for them, and re-layouts: 5.4 us -> 13.2 us
    mul x1 -> x0, other arithmetic: 6.58 us -> none  [shards(): BUOYANCY * filled[3:4]]
    slice x5 -> x4, local copies, waits for them, and re-layouts: 7.78 us -> 1.47 us  [the longest x1 0.94 us: shards(): centre = wide_fields[..., 1:-1, 1:-1]]
    ppermute x6 -> x2, waiting for transfers between devices: 5.49 us -> 0.01 us  [padded_2(): before = lax.ppermute(last, axis, up)]
  transfers between devices with their start and end apart: 24 -> 16, of which waited for: 17 -> 14; matrix products, arithmetic and copies ran while one was open for 8% -> 5% of each run, Pallas kernels for 0% -> 0%
where the time goes in v3:
time: 299 us; the launch traced here: 296 us
  local copies, waits for them, and re-layouts  112 us (37%)
  starting transfers between devices  80.1 us (27%)
  waiting for transfers between devices  74.4 us (25%)
  other arithmetic  27.2 us (9%)
    gather x8, local copies, waits for them, and re-layouts, shards(): jnp.take(flat_cells, cells_asked + offset, axis=1)  61.7 us
    ppermute x8, starting transfers between devices, doubling_gather(): other = lax.ppermute(block, axis, [(i, i ^ step) for i in range(count)])  31.1 us
    ppermute x8, waiting for transfers between devices, doubling_gather(): other = lax.ppermute(block, axis, [(i, i ^ step) for i in range(count)])  24.7 us
    all_to_all x1, waiting for transfers between devices, shards(): lax.all_to_all(served, 'lon', split_axis=1, concat_axis=1, tiled=True)  21.6 us
    all_to_all x1, starting transfers between devices, shards(): lax.all_to_all(requests, 'lon', split_axis=0, concat_axis=0, tiled=True)  17.9 us
    ppermute x2, starting transfers between devices, padded_2(): before = lax.ppermute(last, axis, up)  14.2 us
    ppermute x2, waiting for transfers between devices, partner_2(): return lax.ppermute(block, axis, route)  14.1 us
    unnamed x48, local copies, waits for them, and re-layouts  13.2 us
  transfers between devices with their start and end apart: 16, of which 14 were waited for; matrix products, arithmetic and copies ran while one was open for 5% of the time, Pallas kernels for 0%

profile of v3, /device:TPU:1, one launch (start us, length us, event | category | flops | bytes accessed | tf_op | source)
XLA Modules:
  0.0 296.4 jit_solution(8331194930861884064)
XLA Ops:
  3.4 1.4 reduce.17
  7.1 3.9 %collective-permute-start = (s32[32,2,2,64]{3,1,2,0:T(2,128)S(1)}, s32[32,2,2,64]{3,1,2,0:T(2,128)S(1)}, u32[]{:S(2)}, u32[]{:S(2)}) collective-permute-start(s32[32,2,2,64]{3,1,2,0:T(2,128)S(1)} %pad_add_fusion), channel_id=1, source_target_pairs={{0,256},{256,0},{1,257},{257,1},{2,258},{258,2},{3,259},{259,3},{4... | collective-permute-start | bytes 98312 | tf_op jit(solution)/shard_map/ppermute | solution.py:22
  13.4 17.9 %all-to-all-start = ((s32[32,1,256]{2,1,0:T(1,128)}), s32[32,1,256]{2,1,0:T(1,128)S(1)}, u32[]{:S(2)}, u32[]{:S(2)}) async-start(s32[32,1,256]{2,1,0:T(1,128)} %reshape.881), calls=%async_computation | async-start | bytes 65536 | tf_op jit(solution)/shard_map/all_to_all | solution.py:165
  31.4 2.3 copy.289
  33.7 4.6 %copy.201 = f32[24,16384]{0,1:T(8,128)} copy(f32[24,16384]{1,0:T(8,128)S(1)} %bitcast.194) | data formatting | bytes 3145728 | tf_op jit(solution)/shard_map/reshape;squeeze | solution.py:151
  38.4 6.7 %all-to-all-done = s32[32,1,256]{2,1,0:T(1,128)S(1)} async-done(((s32[32,1,256]{2,1,0:T(1,128)}), s32[32,1,256]{2,1,0:T(1,128)S(1)}, u32[]{:S(2)}, u32[]{:S(2)}) %all-to-all-start) | async-done | bytes 32800 | tf_op jit(solution)/shard_map/all_to_all | solution.py:165
  46.8 14.1 %gather_fusion.1 = f32[4096,24]{1,0:T(8,128)S(1)} fusion(f32[24,16384]{0,1:T(8,128)} %copy.201, s32[4096]{0:T(1024)S(1)} %get-tuple-element.46), kind=kCustom, calls=%fused_computation.clone | custom fusion | bytes 802816 | tf_op jit(solution)/shard_map/jit(_take)/gather | solution.py:169
  61.5 14.1 %gather_fusion.2 = f32[4096,24]{1,0:T(8,128)S(1)} fusion(f32[24,16384]{0,1:T(8,128)} %copy.201, s32[4096]{0:T(1024)S(1)} %get-tuple-element.45), kind=kCustom, calls=%fused_computation.1.clone | custom fusion | bytes 802816 | tf_op jit(solution)/shard_map/jit(_take)/gather | solution.py:169
  75.7 1.5 copy.182
  77.4 14.1 %gather_fusion.3 = f32[4096,24]{1,0:T(8,128)S(1)} fusion(f32[24,16384]{0,1:T(8,128)} %copy.201, s32[4096]{0:T(1024)S(1)} %get-tuple-element.44), kind=kCustom, calls=%fused_computation.2.clone | custom fusion | bytes 802816 | tf_op jit(solution)/shard_map/jit(_take)/gather | solution.py:169
  91.6 1.6 copy.187
  93.1 14.1 %gather_fusion.4 = f32[4096,24]{1,0:T(8,128)S(1)} fusion(f32[24,16384]{0,1:T(8,128)} %copy.201, s32[4096]{0:T(1024)S(1)} %get-tuple-element.43), kind=kCustom, calls=%fused_computation.3.clone | custom fusion | bytes 802816 | tf_op jit(solution)/shard_map/jit(_take)/gather | solution.py:169
  107.3 1.5 copy.192
  109.1 2.2 fusion.122
  112.5 7.4 %all-to-all-start.1 = ((f32[32,1,3072]{2,1,0:T(1,128)}), f32[32,1,3072]{2,1,0:T(1,128)S(1)}, u32[]{:S(2)}, u32[]{:S(2)}) async-start(f32[32,1,3072]{2,1,0:T(1,128)} %reshape.883), calls=%async_computation.1 | async-start | bytes 786432 | tf_op jit(solution)/shard_map/all_to_all | solution.py:173
  121.8 21.6 %all-to-all-done.1 = f32[32,1,3072]{2,1,0:T(1,128)S(1)} async-done(((f32[32,1,3072]{2,1,0:T(1,128)}), f32[32,1,3072]{2,1,0:T(1,128)S(1)}, u32[]{:S(2)}, u32[]{:S(2)}) %all-to-all-start.1) | async-done | bytes 393248 | tf_op jit(solution)/shard_map/all_to_all | solution.py:173
  143.9 1.6 reduce.19
  146.0 2.2 collective-permute-start.1
  148.2 13.7 %collective-permute-done.1 = f32[24,32,2,64]{3,1,2,0:T(8,128)S(1)} collective-permute-done((f32[24,32,2,64]{3,1,2,0:T(8,128)S(1)}, f32[24,32,2,64]{3,1,2,0:T(8,128)S(1)}, u32[]{:S(2)}, u32[]{:S(2)}) %collective-permute-start.1) | collective-permute-done | bytes 393248 | tf_op jit(solution)/shard_map/ppermute | solution.py:22
  164.3 12.2 %scatter_fusion = f32[24,16384]{0,1:T(8,128)} fusion(f32[24,16384]{0,1:T(8,128)} %copy.201, s32[2048]{0:T(1024)S(1)} %bitcast.220, f32[2048,24]{1,0:T(8,128)S(1)} %copy.202), kind=kCustom, calls=%fused_computation.7 | custom fusion | bytes 598016 | tf_op jit(solution)/shard_map/scatter | solution.py:191
  176.4 5.4 %copy.203 = f32[24,128,128]{2,1,0:T(8,128)S(1)} copy(f32[24,128,128]{0,2,1:T(8,128)} %bitcast.190) | data formatting | bytes 3145728 | tf_op jit(solution)/shard_map/reshape;reshape | solution.py:208
  181.9 9.0 %collective-permute-start.2 = (f32[28,3,128]{2,1,0:T(4,128)S(1)}, f32[28,3,128]{2,1,0:T(4,128)S(1)}, u32[]{:S(2)}, u32[]{:S(2)}) collective-permute-start(f32[28,3,128]{2,1,0:T(4,128)S(1)} %get-tuple-element.14), channel_id=1, source_target_pairs={{0,32},{32,64},{64,96},{96,128},{128,160},{160,192},{192,224},{1,3... | collective-permute-start | bytes 129032 | tf_op jit(solution)/shard_map/ppermute | solution.py:32
  190.8 1.9 collective-permute-start.3
  193.3 3.0 %collective-permute-done.3 = f32[28,3,128]{2,1,0:T(4,128)S(1)} collective-permute-done((f32[28,3,128]{2,1,0:T(4,128)S(1)}, f32[28,3,128]{2,1,0:T(4,128)S(1)}, u32[]{:S(2)}, u32[]{:S(2)}) %collective-permute-start.3) | collective-permute-done | bytes 43040 | tf_op jit(solution)/shard_map/ppermute | solution.py:33
  197.1 1.9 fusion.118
  199.1 3.4 %copy.223 = f32[28,134,3]{1,0,2:T(8,128)} copy(f32[28,134,3]{2,1,0:T(8,128)} %get-tuple-element.12) | data formatting | bytes 90048
  202.4 5.3 %collective-permute-start.4 = (f32[28,134,3]{1,0,2:T(8,128)}, f32[28,134,3]{1,0,2:T(8,128)}, u32[]{:S(2)}, u32[]{:S(2)}) collective-permute-start(f32[28,134,3]{1,0,2:T(8,128)} %copy.223), channel_id=1, source_target_pairs={{0,1},{1,2},{2,3},{3,4},{4,5},{5,6},{6,7},{7,8},{8,9},{9,10},{10,1... | collective-permute-start | bytes 135080 | tf_op jit(solution)/shard_map/ppermute | solution.py:32
  207.7 1.8 copy.224
  209.6 1.3 collective-permute-start.5
  210.9 1.6 copy.206
  212.5 4.2 %collective-permute-done.5 = f32[28,134,3]{1,0,2:T(8,128)} collective-permute-done((f32[28,134,3]{1,0,2:T(8,128)}, f32[28,134,3]{1,0,2:T(8,128)}, u32[]{:S(2)}, u32[]{:S(2)}) %collective-permute-start.5) | collective-permute-done | bytes 45056 | tf_op jit(solution)/shard_map/ppermute | solution.py:33
  216.7 2.9 copy.207
  219.6 4.8 %pad_maximum_fusion = f32[28,134,134]{2,1,0:T(8,128)S(1)} fusion(f32[28,134,3]{2,1,0:T(8,128)} %copy.207, f32[28,3,128]{2,1,0:T(4,128)} %copy-done.8, f32[4,128,128]{2,1,0:T(8,128)} %bitcast.195, f32[24,128,128]{2,1,0:T(8,128)S(1)} %copy.203, f32[28,3,128]{2,1,0:T(4,128)} %copy-done.6, f32[28,134,3]{2,1,0:T(8,128)S(1)} %copy.206), kind=kLoop, calls=%fused_computation.10 | loop fusion | flops 2513840 | bytes 4022144 | tf_op jit(solution)/shard_map/concatenate | solution.py:34
  226.6 3.6 %fusion.4 = f32[6,4,132,132]{3,2,1,0:T(8,128)S(1)} fusion(f32[6,4,132,132]{3,2,1,0:T(8,128)S(1)} %slice.283, f32[6,4,134,134]{3,2,1,0:T(8,128)S(1)} %bitcast.192, f32[132]{0:T(256)S(1)} %divide_multiply_fusion, f32[4,132,132]{2,1,0:T(8,128)S(1)} %pad_maximum_fusion.3), kind=kLoop, calls=%fused_computation.15 | loop fusion | flops 5018112 | bytes 10315536 | tf_op jit(solution)/shard_map/add | solution.py:215
  233.8 2.7 collective-permute-start.6
  236.5 3.1 %collective-permute-done.6 = f32[1,4]{1,0:T(1,128)S(1)} collective-permute-done((f32[1,4]{1,0:T(1,128)S(1)}, f32[1,4]{1,0:T(1,128)S(1)}, u32[]{:S(2)}, u32[]{:S(2)}) %collective-permute-start.6) | collective-permute-done | bytes 48 | tf_op jit(solution)/shard_map/ppermute | solution.py:43
  239.6 1.9 collective-permute-start.7
  241.5 2.4 collective-permute-done.7
  243.9 2.1 collective-permute-start.8
  246.0 3.1 %collective-permute-done.8 = f32[4,4]{1,0:T(4,128)S(1)} collective-permute-done((f32[4,4]{1,0:T(4,128)S(1)}, f32[4,4]{1,0:T(4,128)S(1)}, u32[]{:S(2)}, u32[]{:S(2)}) %collective-permute-start.8) | collective-permute-done | bytes 96 | tf_op jit(solution)/shard_map/ppermute | solution.py:43
  249.1 2.3 collective-permute-start.9
  251.5 5.9 %collective-permute-done.9 = f32[8,4]{1,0:T(8,128)S(1)} collective-permute-done((f32[8,4]{1,0:T(8,128)S(1)}, f32[8,4]{1,0:T(8,128)S(1)}, u32[]{:S(2)}, u32[]{:S(2)}) %collective-permute-start.9) | collective-permute-done | bytes 160 | tf_op jit(solution)/shard_map/ppermute | solution.py:43
  257.5 5.2 %collective-permute-start.10 = (f32[16,4]{0,1:T(4,128)S(1)}, f32[16,4]{0,1:T(4,128)S(1)}, u32[]{:S(2)}, u32[]{:S(2)}) collective-permute-start(f32[16,4]{0,1:T(4,128)S(1)} %maximum_select_fusion.5), channel_id=1, source_target_pairs={{0,16},{1,17},{2,18},{3,19},{4,20},{5,21},{6,22},{7,23},{8,24},{9,... | collective-permute-start | bytes 776 | tf_op jit(solution)/shard_map/ppermute | solution.py:43
  262.8 7.8 %collective-permute-done.10 = f32[16,4]{0,1:T(4,128)S(1)} collective-permute-done((f32[16,4]{0,1:T(4,128)S(1)}, f32[16,4]{0,1:T(4,128)S(1)}, u32[]{:S(2)}, u32[]{:S(2)}) %collective-permute-start.10) | collective-permute-done | bytes 288 | tf_op jit(solution)/shard_map/ppermute | solution.py:43
  270.7 6.7 %collective-permute-start.11 = (f32[1,32,4]{1,2,0:T(4,128)S(1)}, f32[1,32,4]{1,2,0:T(4,128)S(1)}, u32[]{:S(2)}, u32[]{:S(2)}) collective-permute-start(f32[1,32,4]{1,2,0:T(4,128)S(1)} %maximum_select_fusion.6), channel_id=1, source_target_pairs={{0,32},{32,0},{64,96},{96,64},{128,160},{160,128},{192,224},{224,1... | collective-permute-start | bytes 1544 | tf_op jit(solution)/shard_map/ppermute | solution.py:43
  278.2 5.0 %collective-permute-start.12 = (f32[2,32,4]{1,2,0:T(4,128)S(1)}, f32[2,32,4]{1,2,0:T(4,128)S(1)}, u32[]{:S(2)}, u32[]{:S(2)}) collective-permute-start(f32[2,32,4]{1,2,0:T(4,128)S(1)} %maximum_select_fusion.3), channel_id=1, source_target_pairs={{0,64},{32,96},{64,0},{96,32},{128,192},{160,224},{192,128},{224,1... | collective-permute-start | bytes 3080 | tf_op jit(solution)/shard_map/ppermute | solution.py:43
  284.2 5.2 %collective-permute-start.13 = (f32[4,32,4]{1,2,0:T(4,128)S(1)}, f32[4,32,4]{1,2,0:T(4,128)S(1)}, u32[]{:S(2)}, u32[]{:S(2)}) collective-permute-start(f32[4,32,4]{1,2,0:T(4,128)S(1)} %maximum_select_fusion.1), channel_id=1, source_target_pairs={{0,128},{32,160},{64,192},{96,224},{128,0},{160,32},{192,64},{224,... | collective-permute-start | bytes 6152 | tf_op jit(solution)/shard_map/ppermute | solution.py:43
  295.2 1.2 maximum_bitcast_fusion
  (164 shorter events, 31.4 us)
Async XLA Ops:
  7.1 5.6 %collective-permute-start = (s32[32,2,2,64]{3,1,2,0:T(2,128)S(1)}, s32[32,2,2,64]{3,1,2,0:T(2,128)S(1)}, u32[]{:S(2)}, u32[]{:S(2)}) collective-permute-start(s32[32,2,2,64]{3,1,2,0:T(2,128)S(1)} %pad_add_fusion), channel_id=1, source_target_pairs={{0,256},{256,0},{1,257},{257,1},{2,258},{258,2},{3,259},{259,3},{4... | collective-permute-start | bytes 98312 | tf_op jit(solution)/shard_map/ppermute | solution.py:22
  13.4 31.7 %all-to-all-start = ((s32[32,1,256]{2,1,0:T(1,128)}), s32[32,1,256]{2,1,0:T(1,128)S(1)}, u32[]{:S(2)}, u32[]{:S(2)}) async-start(s32[32,1,256]{2,1,0:T(1,128)} %reshape.881), calls=%async_computation | async-start | bytes 65536 | tf_op jit(solution)/shard_map/all_to_all | solution.py:165
  109.1 12.5 %copy-start.12 = (f32[1,1,2048]{2,1,0:T(1,128)S(1)}, f32[1,1,2048]{2,1,0:T(1,128)}, u32[]{:S(2)}) copy-start(f32[1,1,2048]{2,1,0:T(1,128)} %param.16) | copy-start | bytes 24580
  112.5 35.7 %copy-start.13 = (s32[1,1,2048]{2,1,0:T(1,128)S(1)}, s32[1,1,2048]{2,1,0:T(1,128)}, u32[]{:S(2)}) copy-start(s32[1,1,2048]{2,1,0:T(1,128)} %param.17) | copy-start | bytes 24580
  112.5 30.9 %all-to-all-start.1 = ((f32[32,1,3072]{2,1,0:T(1,128)}), f32[32,1,3072]{2,1,0:T(1,128)S(1)}, u32[]{:S(2)}, u32[]{:S(2)}) async-start(f32[32,1,3072]{2,1,0:T(1,128)} %reshape.883), calls=%async_computation.1 | async-start | bytes 786432 | tf_op jit(solution)/shard_map/all_to_all | solution.py:173
  146.0 16.0 %collective-permute-start.1 = (f32[24,32,2,64]{3,1,2,0:T(8,128)S(1)}, f32[24,32,2,64]{3,1,2,0:T(8,128)S(1)}, u32[]{:S(2)}, u32[]{:S(2)}) collective-permute-start(f32[24,32,2,64]{3,1,2,0:T(8,128)S(1)} %copy.193), channel_id=1, source_target_pairs={{0,256},{256,0},{1,257},{257,1},{2,258},{258,2},{3,259},{259,3},{4... | collective-permute-start | bytes 1179656 | tf_op jit(solution)/shard_map/ppermute | solution.py:22
  176.4 5.4 %copy-start.3 = (f32[1,4,128,128]{3,2,1,0:T(8,128)S(1)}, f32[1,4,128,128]{3,2,1,0:T(8,128)}, u32[]{:S(2)}) copy-start(f32[1,4,128,128]{3,2,1,0:T(8,128)} %param.11) | copy-start | bytes 786436
  181.9 11.4 %collective-permute-start.2 = (f32[28,3,128]{2,1,0:T(4,128)S(1)}, f32[28,3,128]{2,1,0:T(4,128)S(1)}, u32[]{:S(2)}, u32[]{:S(2)}) collective-permute-start(f32[28,3,128]{2,1,0:T(4,128)S(1)} %get-tuple-element.14), channel_id=1, source_target_pairs={{0,32},{32,64},{64,96},{96,128},{128,160},{160,192},{192,224},{1,3... | collective-permute-start | bytes 129032 | tf_op jit(solution)/shard_map/ppermute | solution.py:32
  190.8 5.5 %collective-permute-start.3 = (f32[28,3,128]{2,1,0:T(4,128)S(1)}, f32[28,3,128]{2,1,0:T(4,128)S(1)}, u32[]{:S(2)}, u32[]{:S(2)}) collective-permute-start(f32[28,3,128]{2,1,0:T(4,128)S(1)} %get-tuple-element.15), channel_id=1, source_target_pairs={{32,0},{64,32},{96,64},{128,96},{160,128},{192,160},{224,192},{33,... | collective-permute-start | bytes 129032 | tf_op jit(solution)/shard_map/ppermute | solution.py:33
  193.3 3.0 %copy-start.6 = (f32[28,3,128]{2,1,0:T(4,128)}, f32[28,3,128]{2,1,0:T(4,128)S(1)}, u32[]{:S(2)}) copy-start(f32[28,3,128]{2,1,0:T(4,128)S(1)} %collective-permute-done.2) | copy-start | bytes 129028
  196.3 0.6 copy-start.8
  202.4 8.5 %collective-permute-start.4 = (f32[28,134,3]{1,0,2:T(8,128)}, f32[28,134,3]{1,0,2:T(8,128)}, u32[]{:S(2)}, u32[]{:S(2)}) collective-permute-start(f32[28,134,3]{1,0,2:T(8,128)} %copy.223), channel_id=1, source_target_pairs={{0,1},{1,2},{2,3},{3,4},{4,5},{5,6},{6,7},{7,8},{8,9},{9,10},{10,1... | collective-permute-start | bytes 135080 | tf_op jit(solution)/shard_map/ppermute | solution.py:32
  209.6 7.2 %collective-permute-start.5 = (f32[28,134,3]{1,0,2:T(8,128)}, f32[28,134,3]{1,0,2:T(8,128)}, u32[]{:S(2)}, u32[]{:S(2)}) collective-permute-start(f32[28,134,3]{1,0,2:T(8,128)} %copy.224), channel_id=1, source_target_pairs={{1,0},{2,1},{3,2},{4,3},{5,4},{6,5},{7,6},{8,7},{9,8},{10,9},{11,1... | collective-permute-start | bytes 135080 | tf_op jit(solution)/shard_map/ppermute | solution.py:33
  224.6 1.5 copy-start
  224.7 1.5 copy-start.4
  224.7 1.5 copy-start.7
  224.7 1.5 copy-start.9
  230.4 0.8 copy-start.5
  230.4 0.8 copy-start.11
  231.2 0.8 copy-start.10
  232.5 0.8 copy-start.1
  232.5 57.9 %copy-start.14 = (f32[4]{0:T(128)S(1)}, f32[4]{0:T(128)}, u32[]{:S(2)}) copy-start(f32[4]{0:T(128)} %get-tuple-element.49) | copy-start | bytes 52
  232.5 57.9 %copy-start.15 = (f32[4]{0:T(128)S(1)}, f32[4]{0:T(128)}, u32[]{:S(2)}) copy-start(f32[4]{0:T(128)} %get-tuple-element.50) | copy-start | bytes 52
  232.5 58.5 %copy-start.16 = (f32[32]{0:T(128)S(1)}, f32[32]{0:T(128)}, u32[]{:S(2)}) copy-start(f32[32]{0:T(128)} %get-tuple-element.54) | copy-start | bytes 388
  232.5 58.5 %copy-start.17 = (f32[32]{0:T(128)S(1)}, f32[32]{0:T(128)}, u32[]{:S(2)}) copy-start(f32[32]{0:T(128)} %get-tuple-element.55) | copy-start | bytes 388
  232.6 58.5 %copy-start.18 = (f32[32]{0:T(128)S(1)}, f32[32]{0:T(128)}, u32[]{:S(2)}) copy-start(f32[32]{0:T(128)} %get-tuple-element.56) | copy-start | bytes 388
  233.8 5.8 %collective-permute-start.6 = (f32[1,4]{1,0:T(1,128)S(1)}, f32[1,4]{1,0:T(1,128)S(1)}, u32[]{:S(2)}, u32[]{:S(2)}) collective-permute-start(f32[1,4]{1,0:T(1,128)S(1)} %multiply_bitcast_fusion), channel_id=1, source_target_pairs={{0,1},{1,0},{2,3},{3,2},{4,5},{5,4},{6,7},{7,6},{8,9},{9,8},{10,11... | collective-permute-start | bytes 56 | tf_op jit(solution)/shard_map/ppermute | solution.py:43
  239.6 4.3 %collective-permute-start.7 = (f32[2,4]{1,0:T(2,128)S(1)}, f32[2,4]{1,0:T(2,128)S(1)}, u32[]{:S(2)}, u32[]{:S(2)}) collective-permute-start(f32[2,4]{1,0:T(2,128)S(1)} %maximum_select_fusion.7), channel_id=1, source_target_pairs={{0,2},{1,3},{2,0},{3,1},{4,6},{5,7},{6,4},{7,5},{8,10},{9,11},{10,... | collective-permute-start | bytes 104 | tf_op jit(solution)/shard_map/ppermute | solution.py:43
  243.9 5.2 %collective-permute-start.8 = (f32[4,4]{1,0:T(4,128)S(1)}, f32[4,4]{1,0:T(4,128)S(1)}, u32[]{:S(2)}, u32[]{:S(2)}) collective-permute-start(f32[4,4]{1,0:T(4,128)S(1)} %maximum_select_fusion.4), channel_id=1, source_target_pairs={{0,4},{1,5},{2,6},{3,7},{4,0},{5,1},{6,2},{7,3},{8,12},{9,13},{10,... | collective-permute-start | bytes 200 | tf_op jit(solution)/shard_map/ppermute | solution.py:43
  249.1 8.3 %collective-permute-start.9 = (f32[8,4]{1,0:T(8,128)S(1)}, f32[8,4]{1,0:T(8,128)S(1)}, u32[]{:S(2)}, u32[]{:S(2)}) collective-permute-start(f32[8,4]{1,0:T(8,128)S(1)} %maximum_select_fusion.2), channel_id=1, source_target_pairs={{0,8},{1,9},{2,10},{3,11},{4,12},{5,13},{6,14},{7,15},{8,0},{9,1},... | collective-permute-start | bytes 392 | tf_op jit(solution)/shard_map/ppermute | solution.py:43
  257.5 13.0 %collective-permute-start.10 = (f32[16,4]{0,1:T(4,128)S(1)}, f32[16,4]{0,1:T(4,128)S(1)}, u32[]{:S(2)}, u32[]{:S(2)}) collective-permute-start(f32[16,4]{0,1:T(4,128)S(1)} %maximum_select_fusion.5), channel_id=1, source_target_pairs={{0,16},{1,17},{2,18},{3,19},{4,20},{5,21},{6,22},{7,23},{8,24},{9,... | collective-permute-start | bytes 776 | tf_op jit(solution)/shard_map/ppermute | solution.py:43
  270.7 7.5 %collective-permute-start.11 = (f32[1,32,4]{1,2,0:T(4,128)S(1)}, f32[1,32,4]{1,2,0:T(4,128)S(1)}, u32[]{:S(2)}, u32[]{:S(2)}) collective-permute-start(f32[1,32,4]{1,2,0:T(4,128)S(1)} %maximum_select_fusion.6), channel_id=1, source_target_pairs={{0,32},{32,0},{64,96},{96,64},{128,160},{160,128},{192,224},{224,1... | collective-permute-start | bytes 1544 | tf_op jit(solution)/shard_map/ppermute | solution.py:43
  278.2 6.0 %collective-permute-start.12 = (f32[2,32,4]{1,2,0:T(4,128)S(1)}, f32[2,32,4]{1,2,0:T(4,128)S(1)}, u32[]{:S(2)}, u32[]{:S(2)}) collective-permute-start(f32[2,32,4]{1,2,0:T(4,128)S(1)} %maximum_select_fusion.3), channel_id=1, source_target_pairs={{0,64},{32,96},{64,0},{96,32},{128,192},{160,224},{192,128},{224,1... | collective-permute-start | bytes 3080 | tf_op jit(solution)/shard_map/ppermute | solution.py:43
  284.2 6.2 %collective-permute-start.13 = (f32[4,32,4]{1,2,0:T(4,128)S(1)}, f32[4,32,4]{1,2,0:T(4,128)S(1)}, u32[]{:S(2)}, u32[]{:S(2)}) collective-permute-start(f32[4,32,4]{1,2,0:T(4,128)S(1)} %maximum_select_fusion.1), channel_id=1, source_target_pairs={{0,128},{32,160},{64,192},{96,224},{128,0},{160,32},{192,64},{224,... | collective-permute-start | bytes 6152 | tf_op jit(solution)/shard_map/ppermute | solution.py:43
  289.4 3.0 %copy-start.2 = (f32[4,130,130]{2,1,0:T(8,128)S(1)}, f32[4,130,130]{2,1,0:T(8,128)}, u32[]{:S(2)}) copy-start(f32[4,130,130]{2,1,0:T(8,128)} %copy-done.1) | copy-start | bytes 811204

commit v4 on v3

--- a/solution.py
+++ b/solution.py
@@ -3,6 +3,8 @@
 import jax
 import jax.numpy as jnp
 from jax import lax
+from jax.experimental import pallas as pl
+from jax.experimental.pallas import tpu as pltpu
 from jax.sharding import PartitionSpec as P
 
 CAP = 2
@@ -47,6 +49,26 @@
         )
         step *= 2
     return block
+
+
+def corner_gather(table, rows, width):
+    count = rows.shape[0]
+
+    def kernel(rows_ref, table_ref, out_ref):
+        def body(t, carry):
+            at = rows_ref[t]
+            for k, offset in enumerate((0, 1, width, width + 1)):
+                out_ref[k, pl.ds(t, 1), :] = table_ref[pl.ds(at + offset, 1), :]
+            return carry
+
+        lax.fori_loop(0, count, body, 0, unroll=16)
+
+    return pl.pallas_call(
+        kernel,
+        out_shape=jax.ShapeDtypeStruct((4, count, table.shape[1]), table.dtype),
+        in_specs=[pl.BlockSpec(memory_space=pltpu.SMEM), pl.BlockSpec(memory_space=pltpu.VMEM)],
+        out_specs=pl.BlockSpec(memory_space=pltpu.VMEM),
+    )(rows, table)
 
 
 def metric(row_index, total_rows):
@@ -163,17 +185,15 @@
     ).reshape(n_lon, capacity, 2, block_cells)
     requests = partner_2(asked, "panel", 0)
     requests = lax.all_to_all(requests, "lon", split_axis=0, concat_axis=0, tiled=True)
-    cells_asked = requests[:, :, 0, :]
-    frac_lat, frac_lon = fractions(requests[:, :, 1, :])
-    corners = [
-        jnp.take(flat_cells, cells_asked + offset, axis=1)
-        for offset in (0, 1, cols_dev, cols_dev + 1)
-    ]
-    served = bilinear(*corners, frac_lat, frac_lon)
-    served = lax.all_to_all(served, "lon", split_axis=1, concat_axis=1, tiled=True)
+    cells_asked = requests[:, :, 0, :].reshape(-1)
+    frac_lat, frac_lon = fractions(requests[:, :, 1, :].reshape(-1, 1))
+    corners = corner_gather(flat_cells.T, cells_asked, cols_dev)
+    served = bilinear(corners[0], corners[1], corners[2], corners[3], frac_lat, frac_lon)
+    served = served.reshape(n_lon, capacity, block_cells, channels)
+    served = lax.all_to_all(served, "lon", split_axis=0, concat_axis=0, tiled=True)
     served = partner_2(served, "panel", 0)
-    values = served.reshape(channels, slot_count, block_cells)[:, slot_of, :]
-    values = values.reshape(6, levels, blocks * block_cells)
+    values = served.reshape(slot_count, block_cells, channels)[slot_of]
+    values = values.reshape(blocks * block_cells, channels).T.reshape(6, levels, blocks * block_cells)
     turn = border_angle[0, 0]
     cos_angle = jnp.cos(turn)
     sin_angle = jnp.sin(turn)

time: 299 us -> 268 us (0.90)
  local copies, waits for them, and re-layouts: 112 us -> 64.9 us
  Pallas kernels: 0 us -> 15.4 us
    gather x9 -> x2, local copies, waits for them, and re-layouts: 62.3 us -> 0.66 us  [shards(): values = served.reshape(slot_count, block_cells, channels)[slot_of]]
    pallas_call x0 -> x1, Pallas kernels: none -> 15.4 us  [corner_gather(): pl.pallas_call(kernel, out_shape=jax.ShapeDtypeStruct((4, count, table.sh...]
    squeeze x4, local copies, waits for them, and re-layouts: 0.36 us -> 9.88 us  [the longest x1 3.14 us: shards(): corners[1]]
    slice x10 -> x2, local copies, waits for them, and re-layouts: 0.3 us -> 6.26 us  [the longest x1 6.24 us: shards(): corners[0]]
where the time goes in v4:
time: 268 us; the launch traced here: 266 us
  starting transfers between devices  80.1 us (30%)
  waiting for transfers between devices  74.2 us (28%)
  local copies, waits for them, and re-layouts  64.9 us (24%)
  other arithmetic  27.9 us (10%)
  Pallas kernels  15.4 us (6%)
    ppermute x8, starting transfers between devices, doubling_gather(): other = lax.ppermute(block, axis, [(i, i ^ step) for i in range(count)])  31.2 us
    ppermute x8, waiting for transfers between devices, doubling_gather(): other = lax.ppermute(block, axis, [(i, i ^ step) for i in range(count)])  24.6 us
    all_to_all x1, waiting for transfers between devices, shards(): lax.all_to_all(served, 'lon', split_axis=0, concat_axis=0, tiled=True)  21.6 us
    all_to_all x1, starting transfers between devices, shards(): lax.all_to_all(requests, 'lon', split_axis=0, concat_axis=0, tiled=True)  17.9 us
    pallas_call x1, Pallas kernels, corner_gather(): pl.pallas_call(kernel, out_shape=jax.ShapeDtypeStruct((4, count, table.sh...  15.4 us
    ppermute x2, starting transfers between devices, padded_2(): before = lax.ppermute(last, axis, up)  14.2 us
    ppermute x2, waiting for transfers between devices, partner_2(): return lax.ppermute(block, axis, route)  14.1 us
    unnamed x48, local copies, waits for them, and re-layouts  13.2 us
  transfers between devices with their start and end apart: 16, of which 14 were waited for; matrix products, arithmetic and copies ran while one was open for 5% of the time, Pallas kernels for 0%

profile of v4, /device:TPU:1, one launch (start us, length us, event | category | flops | bytes accessed | tf_op | source)
XLA Modules:
  0.0 265.6 jit_solution(10915726695829487561)
XLA Ops:
  3.4 1.4 reduce.17
  7.1 3.9 %collective-permute-start = (s32[32,2,2,64]{3,1,2,0:T(2,128)S(1)}, s32[32,2,2,64]{3,1,2,0:T(2,128)S(1)}, u32[]{:S(2)}, u32[]{:S(2)}) collective-permute-start(s32[32,2,2,64]{3,1,2,0:T(2,128)S(1)} %pad_add_fusion), channel_id=1, source_target_pairs={{0,256},{256,0},{1,257},{257,1},{2,258},{258,2},{3,259},{259,3},{4... | collective-permute-start | bytes 98312 | tf_op jit(solution)/shard_map/ppermute | solution.py:24
  13.4 17.9 %all-to-all-start = ((s32[32,1,256]{2,1,0:T(1,128)}), s32[32,1,256]{2,1,0:T(1,128)S(1)}, u32[]{:S(2)}, u32[]{:S(2)}) async-start(s32[32,1,256]{2,1,0:T(1,128)} %reshape.661), calls=%async_computation | async-start | bytes 65536 | tf_op jit(solution)/shard_map/all_to_all | solution.py:187
  31.4 2.3 copy.179
  33.7 4.6 %copy.109 = f32[24,16384]{0,1:T(8,128)} copy(f32[24,16384]{1,0:T(8,128)S(1)} %bitcast.174) | data formatting | bytes 3145728 | tf_op jit(solution)/shard_map/reshape;squeeze | solution.py:173
  38.4 6.7 %all-to-all-done = s32[32,1,256]{2,1,0:T(1,128)S(1)} async-done(((s32[32,1,256]{2,1,0:T(1,128)}), s32[32,1,256]{2,1,0:T(1,128)S(1)}, u32[]{:S(2)}, u32[]{:S(2)}) %all-to-all-start) | async-done | bytes 32800 | tf_op jit(solution)/shard_map/all_to_all | solution.py:187
  47.2 15.4 %shard_map.95 = f32[4,4096,24]{2,1,0:T(8,128)} custom-call(s32[4096]{0:T(1024)} %reshape_squeeze.15.rows_ref, f32[16384,24]{1,0:T(8,128)} %bitcast.168), custom_call_target="tpu_custom_call" | custom-call | tf_op jit(solution)/shard_map/pallas_call | solution.py:66
  62.5 6.2 %fusion.117 = (f32[1,4096,24]{2,1,0:T(8,128)}, f32[1,4096,24]{2,1,0:T(8,128)S(1)}, f32[1,4096,24]{2,1,0:T(8,128)}, f32[1,4096,24]{2,1,0:T(8,128)}) fusion(f32[4,4096,24]{2,1,0:T(8,128)} %shard_map.95), kind=kLoop, calls=%fused_computation.225 | loop fusion | bytes 3145728 | tf_op jit(solution)/shard_map/slice | solution.py:191
  68.8 2.2 copy.101
  71.0 3.1 %copy.103 = f32[32,2,64,24]{2,3,1,0:T(8,128)} copy(f32[32,2,64,24]{3,2,1,0:T(8,128)} %bitcast.172) | data formatting | bytes 786432 | tf_op jit(solution)/shard_map/squeeze | solution.py:191
  74.1 3.1 %copy.105 = f32[32,2,64,24]{2,3,1,0:T(8,128)} copy(f32[32,2,64,24]{3,2,1,0:T(8,128)} %bitcast.171) | data formatting | bytes 786432 | tf_op jit(solution)/shard_map/squeeze | solution.py:191
  77.2 1.5 copy.107
  78.9 1.9 fusion.121
  82.0 7.3 %all-to-all-start.1 = ((f32[32,1,3072]{2,1,0:T(1,128)}), f32[32,1,3072]{2,1,0:T(1,128)S(1)}, u32[]{:S(2)}, u32[]{:S(2)}) async-start(f32[32,1,3072]{2,1,0:T(1,128)} %reshape.663), calls=%async_computation.1 | async-start | bytes 786432 | tf_op jit(solution)/shard_map/all_to_all | solution.py:193
  91.1 21.6 %all-to-all-done.1 = f32[32,1,3072]{2,1,0:T(1,128)S(1)} async-done(((f32[32,1,3072]{2,1,0:T(1,128)}), f32[32,1,3072]{2,1,0:T(1,128)S(1)}, u32[]{:S(2)}, u32[]{:S(2)}) %all-to-all-start.1) | async-done | bytes 393248 | tf_op jit(solution)/shard_map/all_to_all | solution.py:193
  113.3 1.6 reduce.19
  115.1 2.2 collective-permute-start.1
  117.3 13.7 %collective-permute-done.1 = f32[32,2,64,24]{2,3,1,0:T(8,128)S(1)} collective-permute-done((f32[32,2,64,24]{2,3,1,0:T(8,128)S(1)}, f32[32,2,64,24]{2,3,1,0:T(8,128)S(1)}, u32[]{:S(2)}, u32[]{:S(2)}) %collective-permute-start.1) | collective-permute-done | bytes 393248 | tf_op jit(solution)/shard_map/ppermute | solution.py:24
  132.4 12.1 %scatter_fusion = f32[24,16384]{0,1:T(8,128)} fusion(f32[24,16384]{0,1:T(8,128)} %copy.109, s32[2048]{0:T(1024)S(1)} %bitcast.201, f32[2048,24]{1,0:T(8,128)S(1)} %copy.110), kind=kCustom, calls=%fused_computation.3 | custom fusion | bytes 598016 | tf_op jit(solution)/shard_map/scatter | solution.py:211
  144.6 5.4 %copy.111 = f32[24,128,128]{2,1,0:T(8,128)S(1)} copy(f32[24,128,128]{0,2,1:T(8,128)} %bitcast.169) | data formatting | bytes 3145728 | tf_op jit(solution)/shard_map/reshape;reshape | solution.py:228
  150.0 9.0 %collective-permute-start.2 = (f32[28,3,128]{2,1,0:T(4,128)S(1)}, f32[28,3,128]{2,1,0:T(4,128)S(1)}, u32[]{:S(2)}, u32[]{:S(2)}) collective-permute-start(f32[28,3,128]{2,1,0:T(4,128)S(1)} %get-tuple-element.17), channel_id=1, source_target_pairs={{0,32},{32,64},{64,96},{96,128},{128,160},{160,192},{192,224},{1,3... | collective-permute-start | bytes 129032 | tf_op jit(solution)/shard_map/ppermute | solution.py:34
  159.0 2.1 collective-permute-start.3
  161.7 2.8 %collective-permute-done.3 = f32[28,3,128]{2,1,0:T(4,128)S(1)} collective-permute-done((f32[28,3,128]{2,1,0:T(4,128)S(1)}, f32[28,3,128]{2,1,0:T(4,128)S(1)}, u32[]{:S(2)}, u32[]{:S(2)}) %collective-permute-start.3) | collective-permute-done | bytes 43040 | tf_op jit(solution)/shard_map/ppermute | solution.py:35
  165.3 1.9 fusion.118
  167.2 3.4 %copy.130 = f32[28,134,3]{1,0,2:T(8,128)} copy(f32[28,134,3]{2,1,0:T(8,128)} %get-tuple-element.15) | data formatting | bytes 90048
  170.6 5.3 %collective-permute-start.4 = (f32[28,134,3]{1,0,2:T(8,128)}, f32[28,134,3]{1,0,2:T(8,128)}, u32[]{:S(2)}, u32[]{:S(2)}) collective-permute-start(f32[28,134,3]{1,0,2:T(8,128)} %copy.130), channel_id=1, source_target_pairs={{0,1},{1,2},{2,3},{3,4},{4,5},{5,6},{6,7},{7,8},{8,9},{9,10},{10,1... | collective-permute-start | bytes 135080 | tf_op jit(solution)/shard_map/ppermute | solution.py:34
  175.8 1.8 copy.131
  177.7 1.3 collective-permute-start.5
  179.0 1.6 copy.114
  180.6 4.2 %collective-permute-done.5 = f32[28,134,3]{1,0,2:T(8,128)} collective-permute-done((f32[28,134,3]{1,0,2:T(8,128)}, f32[28,134,3]{1,0,2:T(8,128)}, u32[]{:S(2)}, u32[]{:S(2)}) %collective-permute-start.5) | collective-permute-done | bytes 45056 | tf_op jit(solution)/shard_map/ppermute | solution.py:35
  184.9 2.9 %copy.115 = f32[28,134,3]{2,1,0:T(8,128)} copy(f32[28,134,3]{1,0,2:T(8,128)} %collective-permute-done.5) | data formatting | bytes 90048 | tf_op jit(solution)/shard_map/ppermute | solution.py:35
  187.7 4.8 %pad_maximum_fusion = f32[28,134,134]{2,1,0:T(8,128)S(1)} fusion(f32[28,134,3]{2,1,0:T(8,128)} %copy.115, f32[28,3,128]{2,1,0:T(4,128)} %copy-done.8, f32[4,128,128]{2,1,0:T(8,128)} %bitcast.175, f32[24,128,128]{2,1,0:T(8,128)S(1)} %copy.111, f32[28,3,128]{2,1,0:T(4,128)} %copy-done.6, f32[28,134,3]{2,1,0:T(8,128)S(1)} %copy.114), kind=kLoop, calls=%fused_computation.6 | loop fusion | flops 2513840 | bytes 4022144 | tf_op jit(solution)/shard_map/concatenate | solution.py:36
  194.7 3.6 %fusion.4 = f32[6,4,132,132]{3,2,1,0:T(8,128)S(1)} fusion(f32[6,4,132,132]{3,2,1,0:T(8,128)S(1)} %slice.295, f32[6,4,134,134]{3,2,1,0:T(8,128)S(1)} %bitcast.166, f32[132]{0:T(256)S(1)} %divide_multiply_fusion, f32[4,132,132]{2,1,0:T(8,128)S(1)} %pad_maximum_fusion.3), kind=kLoop, calls=%fused_computation.11 | loop fusion | flops 5018112 | bytes 10315536 | tf_op jit(solution)/shard_map/add | solution.py:235
  201.9 2.7 %collective-permute-start.6 = (f32[1,4]{1,0:T(1,128)S(1)}, f32[1,4]{1,0:T(1,128)S(1)}, u32[]{:S(2)}, u32[]{:S(2)}) collective-permute-start(f32[1,4]{1,0:T(1,128)S(1)} %multiply_bitcast_fusion), channel_id=1, source_target_pairs={{0,1},{1,0},{2,3},{3,2},{4,5},{5,4},{6,7},{7,6},{8,9},{9,8},{10,11... | collective-permute-start | bytes 56 | tf_op jit(solution)/shard_map/ppermute | solution.py:45
  204.6 3.1 %collective-permute-done.6 = f32[1,4]{1,0:T(1,128)S(1)} collective-permute-done((f32[1,4]{1,0:T(1,128)S(1)}, f32[1,4]{1,0:T(1,128)S(1)}, u32[]{:S(2)}, u32[]{:S(2)}) %collective-permute-start.6) | collective-permute-done | bytes 48 | tf_op jit(solution)/shard_map/ppermute | solution.py:45
  207.6 1.9 collective-permute-start.7
  209.6 2.4 collective-permute-done.7
  212.0 2.2 collective-permute-start.8
  214.1 3.1 %collective-permute-done.8 = f32[4,4]{1,0:T(4,128)S(1)} collective-permute-done((f32[4,4]{1,0:T(4,128)S(1)}, f32[4,4]{1,0:T(4,128)S(1)}, u32[]{:S(2)}, u32[]{:S(2)}) %collective-permute-start.8) | collective-permute-done | bytes 96 | tf_op jit(solution)/shard_map/ppermute | solution.py:45
  217.2 2.3 collective-permute-start.9
  219.6 5.9 %collective-permute-done.9 = f32[8,4]{1,0:T(8,128)S(1)} collective-permute-done((f32[8,4]{1,0:T(8,128)S(1)}, f32[8,4]{1,0:T(8,128)S(1)}, u32[]{:S(2)}, u32[]{:S(2)}) %collective-permute-start.9) | collective-permute-done | bytes 160 | tf_op jit(solution)/shard_map/ppermute | solution.py:45
  225.6 5.2 %collective-permute-start.10 = (f32[16,4]{0,1:T(4,128)S(1)}, f32[16,4]{0,1:T(4,128)S(1)}, u32[]{:S(2)}, u32[]{:S(2)}) collective-permute-start(f32[16,4]{0,1:T(4,128)S(1)} %maximum_select_fusion.5), channel_id=1, source_target_pairs={{0,16},{1,17},{2,18},{3,19},{4,20},{5,21},{6,22},{7,23},{8,24},{9,... | collective-permute-start | bytes 776 | tf_op jit(solution)/shard_map/ppermute | solution.py:45
  230.9 7.8 %collective-permute-done.10 = f32[16,4]{0,1:T(4,128)S(1)} collective-permute-done((f32[16,4]{0,1:T(4,128)S(1)}, f32[16,4]{0,1:T(4,128)S(1)}, u32[]{:S(2)}, u32[]{:S(2)}) %collective-permute-start.10) | collective-permute-done | bytes 288 | tf_op jit(solution)/shard_map/ppermute | solution.py:45
  238.7 6.7 %collective-permute-start.11 = (f32[1,32,4]{1,2,0:T(4,128)S(1)}, f32[1,32,4]{1,2,0:T(4,128)S(1)}, u32[]{:S(2)}, u32[]{:S(2)}) collective-permute-start(f32[1,32,4]{1,2,0:T(4,128)S(1)} %maximum_select_fusion.6), channel_id=1, source_target_pairs={{0,32},{32,0},{64,96},{96,64},{128,160},{160,128},{192,224},{224,1... | collective-permute-start | bytes 1544 | tf_op jit(solution)/shard_map/ppermute | solution.py:45
  246.3 5.0 %collective-permute-start.12 = (f32[2,32,4]{1,2,0:T(4,128)S(1)}, f32[2,32,4]{1,2,0:T(4,128)S(1)}, u32[]{:S(2)}, u32[]{:S(2)}) collective-permute-start(f32[2,32,4]{1,2,0:T(4,128)S(1)} %maximum_select_fusion.3), channel_id=1, source_target_pairs={{0,64},{32,96},{64,0},{96,32},{128,192},{160,224},{192,128},{224,1... | collective-permute-start | bytes 3080 | tf_op jit(solution)/shard_map/ppermute | solution.py:45
  252.3 5.2 %collective-permute-start.13 = (f32[4,32,4]{1,2,0:T(4,128)S(1)}, f32[4,32,4]{1,2,0:T(4,128)S(1)}, u32[]{:S(2)}, u32[]{:S(2)}) collective-permute-start(f32[4,32,4]{1,2,0:T(4,128)S(1)} %maximum_select_fusion.1), channel_id=1, source_target_pairs={{0,128},{32,160},{64,192},{96,224},{128,0},{160,32},{192,64},{224,... | collective-permute-start | bytes 6152 | tf_op jit(solution)/shard_map/ppermute | solution.py:45
  260.5 1.9 add_bitcast_fusion
  264.3 1.2 maximum_bitcast_fusion
  (134 shorter events, 28.9 us)
Async XLA Ops:
  7.1 5.6 %collective-permute-start = (s32[32,2,2,64]{3,1,2,0:T(2,128)S(1)}, s32[32,2,2,64]{3,1,2,0:T(2,128)S(1)}, u32[]{:S(2)}, u32[]{:S(2)}) collective-permute-start(s32[32,2,2,64]{3,1,2,0:T(2,128)S(1)} %pad_add_fusion), channel_id=1, source_target_pairs={{0,256},{256,0},{1,257},{257,1},{2,258},{258,2},{3,259},{259,3},{4... | collective-permute-start | bytes 98312 | tf_op jit(solution)/shard_map/ppermute | solution.py:24
  13.4 31.7 %all-to-all-start = ((s32[32,1,256]{2,1,0:T(1,128)}), s32[32,1,256]{2,1,0:T(1,128)S(1)}, u32[]{:S(2)}, u32[]{:S(2)}) async-start(s32[32,1,256]{2,1,0:T(1,128)} %reshape.661), calls=%async_computation | async-start | bytes 65536 | tf_op jit(solution)/shard_map/all_to_all | solution.py:187
  78.9 12.0 %copy-start.12 = (f32[1,1,2048]{2,1,0:T(1,128)S(1)}, f32[1,1,2048]{2,1,0:T(1,128)}, u32[]{:S(2)}) copy-start(f32[1,1,2048]{2,1,0:T(1,128)} %param.14) | copy-start | bytes 24580
  80.8 36.5 %copy-start.13 = (s32[1,1,2048]{2,1,0:T(1,128)S(1)}, s32[1,1,2048]{2,1,0:T(1,128)}, u32[]{:S(2)}) copy-start(s32[1,1,2048]{2,1,0:T(1,128)} %param.15) | copy-start | bytes 24580
  82.0 30.7 %all-to-all-start.1 = ((f32[32,1,3072]{2,1,0:T(1,128)}), f32[32,1,3072]{2,1,0:T(1,128)S(1)}, u32[]{:S(2)}, u32[]{:S(2)}) async-start(f32[32,1,3072]{2,1,0:T(1,128)} %reshape.663), calls=%async_computation.1 | async-start | bytes 786432 | tf_op jit(solution)/shard_map/all_to_all | solution.py:193
  115.1 16.0 %collective-permute-start.1 = (f32[32,2,64,24]{2,3,1,0:T(8,128)S(1)}, f32[32,2,64,24]{2,3,1,0:T(8,128)S(1)}, u32[]{:S(2)}, u32[]{:S(2)}) collective-permute-start(f32[32,2,64,24]{2,3,1,0:T(8,128)S(1)} %bitcast.188), channel_id=1, source_target_pairs={{0,256},{256,0},{1,257},{257,1},{2,258},{258,2},{3,259},{259,3},{4... | collective-permute-start | bytes 1179656 | tf_op jit(solution)/shard_map/ppermute | solution.py:24
  144.6 5.4 %copy-start.3 = (f32[1,4,128,128]{3,2,1,0:T(8,128)S(1)}, f32[1,4,128,128]{3,2,1,0:T(8,128)}, u32[]{:S(2)}) copy-start(f32[1,4,128,128]{3,2,1,0:T(8,128)} %param.9) | copy-start | bytes 786436
  150.0 11.7 %collective-permute-start.2 = (f32[28,3,128]{2,1,0:T(4,128)S(1)}, f32[28,3,128]{2,1,0:T(4,128)S(1)}, u32[]{:S(2)}, u32[]{:S(2)}) collective-permute-start(f32[28,3,128]{2,1,0:T(4,128)S(1)} %get-tuple-element.17), channel_id=1, source_target_pairs={{0,32},{32,64},{64,96},{96,128},{128,160},{160,192},{192,224},{1,3... | collective-permute-start | bytes 129032 | tf_op jit(solution)/shard_map/ppermute | solution.py:34
  159.0 5.5 %collective-permute-start.3 = (f32[28,3,128]{2,1,0:T(4,128)S(1)}, f32[28,3,128]{2,1,0:T(4,128)S(1)}, u32[]{:S(2)}, u32[]{:S(2)}) collective-permute-start(f32[28,3,128]{2,1,0:T(4,128)S(1)} %get-tuple-element.18), channel_id=1, source_target_pairs={{32,0},{64,32},{96,64},{128,96},{160,128},{192,160},{224,192},{33,... | collective-permute-start | bytes 129032 | tf_op jit(solution)/shard_map/ppermute | solution.py:35
  161.7 2.8 %copy-start.6 = (f32[28,3,128]{2,1,0:T(4,128)}, f32[28,3,128]{2,1,0:T(4,128)S(1)}, u32[]{:S(2)}) copy-start(f32[28,3,128]{2,1,0:T(4,128)S(1)} %collective-permute-done.2) | copy-start | bytes 129028
  164.5 0.6 copy-start.8
  170.6 8.5 %collective-permute-start.4 = (f32[28,134,3]{1,0,2:T(8,128)}, f32[28,134,3]{1,0,2:T(8,128)}, u32[]{:S(2)}, u32[]{:S(2)}) collective-permute-start(f32[28,134,3]{1,0,2:T(8,128)} %copy.130), channel_id=1, source_target_pairs={{0,1},{1,2},{2,3},{3,4},{4,5},{5,6},{6,7},{7,8},{8,9},{9,10},{10,1... | collective-permute-start | bytes 135080 | tf_op jit(solution)/shard_map/ppermute | solution.py:34
  177.7 7.2 %collective-permute-start.5 = (f32[28,134,3]{1,0,2:T(8,128)}, f32[28,134,3]{1,0,2:T(8,128)}, u32[]{:S(2)}, u32[]{:S(2)}) collective-permute-start(f32[28,134,3]{1,0,2:T(8,128)} %copy.131), channel_id=1, source_target_pairs={{1,0},{2,1},{3,2},{4,3},{5,4},{6,5},{7,6},{8,7},{9,8},{10,9},{11,1... | collective-permute-start | bytes 135080 | tf_op jit(solution)/shard_map/ppermute | solution.py:35
  192.7 1.5 copy-start
  192.8 1.5 copy-start.4
  192.8 1.5 copy-start.7
  192.8 1.5 copy-start.9
  198.5 1.0 copy-start.5
  198.5 0.8 copy-start.11
  199.3 0.8 copy-start.10
  200.6 0.8 copy-start.1
  200.6 57.9 %copy-start.14 = (f32[4]{0:T(128)S(1)}, f32[4]{0:T(128)}, u32[]{:S(2)}) copy-start(f32[4]{0:T(128)} %get-tuple-element.34) | copy-start | bytes 52
  200.6 57.9 %copy-start.15 = (f32[4]{0:T(128)S(1)}, f32[4]{0:T(128)}, u32[]{:S(2)}) copy-start(f32[4]{0:T(128)} %get-tuple-element.35) | copy-start | bytes 52
  200.6 58.5 %copy-start.16 = (f32[32]{0:T(128)S(1)}, f32[32]{0:T(128)}, u32[]{:S(2)}) copy-start(f32[32]{0:T(128)} %get-tuple-element.39) | copy-start | bytes 388
  200.6 58.5 %copy-start.17 = (f32[32]{0:T(128)S(1)}, f32[32]{0:T(128)}, u32[]{:S(2)}) copy-start(f32[32]{0:T(128)} %get-tuple-element.40) | copy-start | bytes 388
  200.6 58.5 %copy-start.18 = (f32[32]{0:T(128)S(1)}, f32[32]{0:T(128)}, u32[]{:S(2)}) copy-start(f32[32]{0:T(128)} %get-tuple-element.41) | copy-start | bytes 388
  201.9 5.8 %collective-permute-start.6 = (f32[1,4]{1,0:T(1,128)S(1)}, f32[1,4]{1,0:T(1,128)S(1)}, u32[]{:S(2)}, u32[]{:S(2)}) collective-permute-start(f32[1,4]{1,0:T(1,128)S(1)} %multiply_bitcast_fusion), channel_id=1, source_target_pairs={{0,1},{1,0},{2,3},{3,2},{4,5},{5,4},{6,7},{7,6},{8,9},{9,8},{10,11... | collective-permute-start | bytes 56 | tf_op jit(solution)/shard_map/ppermute | solution.py:45
  207.6 4.3 %collective-permute-start.7 = (f32[2,4]{1,0:T(2,128)S(1)}, f32[2,4]{1,0:T(2,128)S(1)}, u32[]{:S(2)}, u32[]{:S(2)}) collective-permute-start(f32[2,4]{1,0:T(2,128)S(1)} %maximum_select_fusion.7), channel_id=1, source_target_pairs={{0,2},{1,3},{2,0},{3,1},{4,6},{5,7},{6,4},{7,5},{8,10},{9,11},{10,... | collective-permute-start | bytes 104 | tf_op jit(solution)/shard_map/ppermute | solution.py:45
  212.0 5.2 %collective-permute-start.8 = (f32[4,4]{1,0:T(4,128)S(1)}, f32[4,4]{1,0:T(4,128)S(1)}, u32[]{:S(2)}, u32[]{:S(2)}) collective-permute-start(f32[4,4]{1,0:T(4,128)S(1)} %maximum_select_fusion.4), channel_id=1, source_target_pairs={{0,4},{1,5},{2,6},{3,7},{4,0},{5,1},{6,2},{7,3},{8,12},{9,13},{10,... | collective-permute-start | bytes 200 | tf_op jit(solution)/shard_map/ppermute | solution.py:45
  217.2 8.3 %collective-permute-start.9 = (f32[8,4]{1,0:T(8,128)S(1)}, f32[8,4]{1,0:T(8,128)S(1)}, u32[]{:S(2)}, u32[]{:S(2)}) collective-permute-start(f32[8,4]{1,0:T(8,128)S(1)} %maximum_select_fusion.2), channel_id=1, source_target_pairs={{0,8},{1,9},{2,10},{3,11},{4,12},{5,13},{6,14},{7,15},{8,0},{9,1},... | collective-permute-start | bytes 392 | tf_op jit(solution)/shard_map/ppermute | solution.py:45
  225.6 13.0 %collective-permute-start.10 = (f32[16,4]{0,1:T(4,128)S(1)}, f32[16,4]{0,1:T(4,128)S(1)}, u32[]{:S(2)}, u32[]{:S(2)}) collective-permute-start(f32[16,4]{0,1:T(4,128)S(1)} %maximum_select_fusion.5), channel_id=1, source_target_pairs={{0,16},{1,17},{2,18},{3,19},{4,20},{5,21},{6,22},{7,23},{8,24},{9,... | collective-permute-start | bytes 776 | tf_op jit(solution)/shard_map/ppermute | solution.py:45
  238.7 7.5 %collective-permute-start.11 = (f32[1,32,4]{1,2,0:T(4,128)S(1)}, f32[1,32,4]{1,2,0:T(4,128)S(1)}, u32[]{:S(2)}, u32[]{:S(2)}) collective-permute-start(f32[1,32,4]{1,2,0:T(4,128)S(1)} %maximum_select_fusion.6), channel_id=1, source_target_pairs={{0,32},{32,0},{64,96},{96,64},{128,160},{160,128},{192,224},{224,1... | collective-permute-start | bytes 1544 | tf_op jit(solution)/shard_map/ppermute | solution.py:45
  246.3 6.0 %collective-permute-start.12 = (f32[2,32,4]{1,2,0:T(4,128)S(1)}, f32[2,32,4]{1,2,0:T(4,128)S(1)}, u32[]{:S(2)}, u32[]{:S(2)}) collective-permute-start(f32[2,32,4]{1,2,0:T(4,128)S(1)} %maximum_select_fusion.3), channel_id=1, source_target_pairs={{0,64},{32,96},{64,0},{96,32},{128,192},{160,224},{192,128},{224,1... | collective-permute-start | bytes 3080 | tf_op jit(solution)/shard_map/ppermute | solution.py:45
  252.3 6.2 %collective-permute-start.13 = (f32[4,32,4]{1,2,0:T(4,128)S(1)}, f32[4,32,4]{1,2,0:T(4,128)S(1)}, u32[]{:S(2)}, u32[]{:S(2)}) collective-permute-start(f32[4,32,4]{1,2,0:T(4,128)S(1)} %maximum_select_fusion.1), channel_id=1, source_target_pairs={{0,128},{32,160},{64,192},{96,224},{128,0},{160,32},{192,64},{224,... | collective-permute-start | bytes 6152 | tf_op jit(solution)/shard_map/ppermute | solution.py:45
  257.5 4.9 %copy-start.2 = (f32[4,130,130]{2,1,0:T(8,128)S(1)}, f32[4,130,130]{2,1,0:T(8,128)}, u32[]{:S(2)}) copy-start(f32[4,130,130]{2,1,0:T(8,128)} %copy-done.1) | copy-start | bytes 811204

commit v5 on v4

--- a/solution.py
+++ b/solution.py
@@ -51,24 +51,30 @@
     return block
 
 
-def corner_gather(table, rows, width):
+def corner_blend(table, rows, weights, width):
     count = rows.shape[0]
 
-    def kernel(rows_ref, table_ref, out_ref):
+    def kernel(rows_ref, weights_ref, table_ref, out_ref):
         def body(t, carry):
             at = rows_ref[t]
-            for k, offset in enumerate((0, 1, width, width + 1)):
-                out_ref[k, pl.ds(t, 1), :] = table_ref[pl.ds(at + offset, 1), :]
+            total = weights_ref[0, t] * table_ref[pl.ds(at, 1), :]
+            for k, offset in enumerate((1, width, width + 1)):
+                total = total + weights_ref[k + 1, t] * table_ref[pl.ds(at + offset, 1), :]
+            out_ref[pl.ds(t, 1), :] = total
             return carry
 
         lax.fori_loop(0, count, body, 0, unroll=16)
 
     return pl.pallas_call(
         kernel,
-        out_shape=jax.ShapeDtypeStruct((4, count, table.shape[1]), table.dtype),
-        in_specs=[pl.BlockSpec(memory_space=pltpu.SMEM), pl.BlockSpec(memory_space=pltpu.VMEM)],
+        out_shape=jax.ShapeDtypeStruct((count, table.shape[1]), table.dtype),
+        in_specs=[
+            pl.BlockSpec(memory_space=pltpu.SMEM),
+            pl.BlockSpec(memory_space=pltpu.SMEM),
+            pl.BlockSpec(memory_space=pltpu.VMEM),
+        ],
         out_specs=pl.BlockSpec(memory_space=pltpu.VMEM),
-    )(rows, table)
+    )(rows, weights, table)
 
 
 def metric(row_index, total_rows):
@@ -186,9 +192,17 @@
     requests = partner_2(asked, "panel", 0)
     requests = lax.all_to_all(requests, "lon", split_axis=0, concat_axis=0, tiled=True)
     cells_asked = requests[:, :, 0, :].reshape(-1)
-    frac_lat, frac_lon = fractions(requests[:, :, 1, :].reshape(-1, 1))
-    corners = corner_gather(flat_cells.T, cells_asked, cols_dev)
-    served = bilinear(corners[0], corners[1], corners[2], corners[3], frac_lat, frac_lon)
+    frac_lat, frac_lon = fractions(requests[:, :, 1, :].reshape(-1))
+    weights = jnp.stack(
+        [
+            (1.0 - frac_lat) * (1.0 - frac_lon),
+            (1.0 - frac_lat) * frac_lon,
+            frac_lat * (1.0 - frac_lon),
+            frac_lat * frac_lon,
+        ],
+        axis=0,
+    )
+    served = corner_blend(flat_cells.T, cells_asked, weights, cols_dev)
     served = served.reshape(n_lon, capacity, block_cells, channels)
     served = lax.all_to_all(served, "lon", split_axis=0, concat_axis=0, tiled=True)
     served = partner_2(served, "panel", 0)

time: 268 us -> 263 us (0.981)
  local copies, waits for them, and re-layouts: 64.9 us -> 50.8 us
  Pallas kernels: 15.4 us -> 24.8 us
    squeeze x4 -> x0, local copies, waits for them, and re-layouts: 9.88 us -> none  [the longest x1 3.14 us: shards(): corners[1]]
    pallas_call x1, Pallas kernels: 15.4 us -> 24.8 us  [corner_blend(): pl.pallas_call(kernel, out_shape=jax.ShapeDtypeStruct((count, table.shape...]
    slice x2 -> x1, local copies, waits for them, and re-layouts: 6.26 us -> 0.02 us  [shards(): frac_lat, frac_lon = fractions(requests[:, :, 1, :].reshape(-1))]
    unnamed x48 -> x46, local copies, waits for them, and re-layouts: 13.2 us -> 13 us
  transfers between devices with their start and end apart: 16 -> 16, of which waited for: 14 -> 14; matrix products, arithmetic and copies ran while one was open for 5% -> 6% of each run, Pallas kernels for 0% -> 0%
where the time goes in v5:
time: 263 us; the launch traced here: 261 us
  starting transfers between devices  80.1 us (30%)
  waiting for transfers between devices  74.3 us (28%)
  local copies, waits for them, and re-layouts  50.8 us (19%)
  other arithmetic  27.8 us (11%)
  Pallas kernels  24.8 us (9%)
    ppermute x8, starting transfers between devices, doubling_gather(): other = lax.ppermute(block, axis, [(i, i ^ step) for i in range(count)])  31.1 us
    pallas_call x1, Pallas kernels, corner_blend(): pl.pallas_call(kernel, out_shape=jax.ShapeDtypeStruct((count, table.shape...  24.8 us
    ppermute x8, waiting for transfers between devices, doubling_gather(): other = lax.ppermute(block, axis, [(i, i ^ step) for i in range(count)])  24.7 us
    all_to_all x1, waiting for transfers between devices, shards(): lax.all_to_all(served, 'lon', split_axis=0, concat_axis=0, tiled=True)  21.6 us
    all_to_all x1, starting transfers between devices, shards(): lax.all_to_all(requests, 'lon', split_axis=0, concat_axis=0, tiled=True)  17.9 us
    ppermute x2, starting transfers between devices, padded_2(): before = lax.ppermute(last, axis, up)  14.2 us
    ppermute x2, waiting for transfers between devices, partner_2(): return lax.ppermute(block, axis, route)  14.2 us
    unnamed x46, local copies, waits for them, and re-layouts  13 us
  transfers between devices with their start and end apart: 16, of which 14 were waited for; matrix products, arithmetic and copies ran while one was open for 6% of the time, Pallas kernels for 0%

profile of v5, /device:TPU:1, one launch (start us, length us, event | category | flops | bytes accessed | tf_op | source)
XLA Modules:
  0.0 260.8 jit_solution(4598113508037582534)
XLA Ops:
  3.4 1.4 reduce.17
  7.1 3.9 %collective-permute-start = (s32[32,2,2,64]{3,1,2,0:T(2,128)S(1)}, s32[32,2,2,64]{3,1,2,0:T(2,128)S(1)}, u32[]{:S(2)}, u32[]{:S(2)}) collective-permute-start(s32[32,2,2,64]{3,1,2,0:T(2,128)S(1)} %pad_add_fusion), channel_id=1, source_target_pairs={{0,256},{256,0},{1,257},{257,1},{2,258},{258,2},{3,259},{259,3},{4... | collective-permute-start | bytes 98312 | tf_op jit(solution)/shard_map/ppermute | solution.py:24
  13.4 17.9 %all-to-all-start = ((s32[32,1,256]{2,1,0:T(1,128)}), s32[32,1,256]{2,1,0:T(1,128)S(1)}, u32[]{:S(2)}, u32[]{:S(2)}) async-start(s32[32,1,256]{2,1,0:T(1,128)} %reshape.642), calls=%async_computation | async-start | bytes 65536 | tf_op jit(solution)/shard_map/all_to_all | solution.py:193
  31.4 2.3 copy.106
  33.7 4.6 %copy.76 = f32[24,16384]{0,1:T(8,128)} copy(f32[24,16384]{1,0:T(8,128)S(1)} %bitcast.129) | data formatting | bytes 3145728 | tf_op jit(solution)/shard_map/reshape;squeeze | solution.py:179
  38.4 6.7 %all-to-all-done = s32[32,1,256]{2,1,0:T(1,128)S(1)} async-done(((s32[32,1,256]{2,1,0:T(1,128)}), s32[32,1,256]{2,1,0:T(1,128)S(1)}, u32[]{:S(2)}, u32[]{:S(2)}) %all-to-all-start) | async-done | bytes 32800 | tf_op jit(solution)/shard_map/all_to_all | solution.py:193
  48.2 24.8 %shard_map.95 = f32[4096,24]{1,0:T(8,128)} custom-call(s32[4096]{0:T(1024)} %reshape_squeeze.14.rows_ref, f32[4,4096]{1,0:T(4,128)} %pad_maximum_fusion.4.weights_ref, f32[16384,24]{1,0:T(8,128)} %bitcast.126), custom_call_target="tpu_custom_call" | custom-call | tf_op jit(solution)/shard_map/pallas_call | solution.py:68
  73.0 2.2 copy.74
  75.2 1.2 reshape.644
  76.5 7.3 %all-to-all-start.1 = ((f32[32,1,3072]{2,1,0:T(1,128)}), f32[32,1,3072]{2,1,0:T(1,128)S(1)}, u32[]{:S(2)}, u32[]{:S(2)}) async-start(f32[32,1,3072]{2,1,0:T(1,128)} %reshape.644), calls=%async_computation.1 | async-start | bytes 786432 | tf_op jit(solution)/shard_map/all_to_all | solution.py:207
  85.6 21.6 %all-to-all-done.1 = f32[32,1,3072]{2,1,0:T(1,128)S(1)} async-done(((f32[32,1,3072]{2,1,0:T(1,128)}), f32[32,1,3072]{2,1,0:T(1,128)S(1)}, u32[]{:S(2)}, u32[]{:S(2)}) %all-to-all-start.1) | async-done | bytes 393248 | tf_op jit(solution)/shard_map/all_to_all | solution.py:207
  107.7 1.6 reduce.19
  109.5 2.2 collective-permute-start.1
  111.8 13.7 %collective-permute-done.1 = f32[32,2,64,24]{2,3,1,0:T(8,128)S(1)} collective-permute-done((f32[32,2,64,24]{2,3,1,0:T(8,128)S(1)}, f32[32,2,64,24]{2,3,1,0:T(8,128)S(1)}, u32[]{:S(2)}, u32[]{:S(2)}) %collective-permute-start.1) | collective-permute-done | bytes 393248 | tf_op jit(solution)/shard_map/ppermute | solution.py:24
  126.9 12.1 %scatter_fusion = f32[24,16384]{0,1:T(8,128)} fusion(f32[24,16384]{0,1:T(8,128)} %copy.76, s32[2048]{0:T(1024)S(1)} %bitcast.157, f32[2048,24]{1,0:T(8,128)S(1)} %copy.77), kind=kCustom, calls=%fused_computation.3 | custom fusion | bytes 598016 | tf_op jit(solution)/shard_map/scatter | solution.py:225
  139.0 5.4 %copy.78 = f32[24,128,128]{2,1,0:T(8,128)S(1)} copy(f32[24,128,128]{0,2,1:T(8,128)} %bitcast.127) | data formatting | bytes 3145728 | tf_op jit(solution)/shard_map/reshape;reshape | solution.py:242
  144.5 9.0 %collective-permute-start.2 = (f32[28,3,128]{2,1,0:T(4,128)S(1)}, f32[28,3,128]{2,1,0:T(4,128)S(1)}, u32[]{:S(2)}, u32[]{:S(2)}) collective-permute-start(f32[28,3,128]{2,1,0:T(4,128)S(1)} %get-tuple-element.16), channel_id=1, source_target_pairs={{0,32},{32,64},{64,96},{96,128},{128,160},{160,192},{192,224},{1,3... | collective-permute-start | bytes 129032 | tf_op jit(solution)/shard_map/ppermute | solution.py:34
  153.4 1.9 collective-permute-start.3
  155.9 3.0 %collective-permute-done.3 = f32[28,3,128]{2,1,0:T(4,128)S(1)} collective-permute-done((f32[28,3,128]{2,1,0:T(4,128)S(1)}, f32[28,3,128]{2,1,0:T(4,128)S(1)}, u32[]{:S(2)}, u32[]{:S(2)}) %collective-permute-start.3) | collective-permute-done | bytes 43040 | tf_op jit(solution)/shard_map/ppermute | solution.py:35
  159.7 1.9 fusion.111
  161.6 3.4 %copy.96 = f32[28,134,3]{1,0,2:T(8,128)} copy(f32[28,134,3]{2,1,0:T(8,128)} %get-tuple-element.14) | data formatting | bytes 90048
  165.0 5.3 %collective-permute-start.4 = (f32[28,134,3]{1,0,2:T(8,128)}, f32[28,134,3]{1,0,2:T(8,128)}, u32[]{:S(2)}, u32[]{:S(2)}) collective-permute-start(f32[28,134,3]{1,0,2:T(8,128)} %copy.96), channel_id=1, source_target_pairs={{0,1},{1,2},{2,3},{3,4},{4,5},{5,6},{6,7},{7,8},{8,9},{9,10},{10,1... | collective-permute-start | bytes 135080 | tf_op jit(solution)/shard_map/ppermute | solution.py:34
  170.3 1.8 copy.97
  172.1 1.5 collective-permute-start.5
  173.7 1.6 copy.81
  175.2 4.1 %collective-permute-done.5 = f32[28,134,3]{1,0,2:T(8,128)} collective-permute-done((f32[28,134,3]{1,0,2:T(8,128)}, f32[28,134,3]{1,0,2:T(8,128)}, u32[]{:S(2)}, u32[]{:S(2)}) %collective-permute-start.5) | collective-permute-done | bytes 45056 | tf_op jit(solution)/shard_map/ppermute | solution.py:35
  179.3 2.9 %copy.82 = f32[28,134,3]{2,1,0:T(8,128)} copy(f32[28,134,3]{1,0,2:T(8,128)} %collective-permute-done.5) | data formatting | bytes 90048 | tf_op jit(solution)/shard_map/ppermute | solution.py:35
  182.2 4.8 %pad_maximum_fusion = f32[28,134,134]{2,1,0:T(8,128)S(1)} fusion(f32[28,134,3]{2,1,0:T(8,128)} %copy.82, f32[28,3,128]{2,1,0:T(4,128)} %copy-done.7, f32[4,128,128]{2,1,0:T(8,128)} %bitcast.130, f32[24,128,128]{2,1,0:T(8,128)S(1)} %copy.78, f32[28,3,128]{2,1,0:T(4,128)} %copy-done.5, f32[28,134,3]{2,1,0:T(8,128)S(1)} %copy.81), kind=kLoop, calls=%fused_computation.6 | loop fusion | flops 2513840 | bytes 4022144 | tf_op jit(solution)/shard_map/concatenate | solution.py:36
  187.3 0.9 slice.275
  189.1 3.6 %fusion.4 = f32[6,4,132,132]{3,2,1,0:T(8,128)S(1)} fusion(f32[6,4,132,132]{3,2,1,0:T(8,128)S(1)} %slice.275, f32[6,4,134,134]{3,2,1,0:T(8,128)S(1)} %bitcast.124, f32[132]{0:T(256)S(1)} %divide_multiply_fusion, f32[4,132,132]{2,1,0:T(8,128)S(1)} %pad_maximum_fusion.3), kind=kLoop, calls=%fused_computation.11 | loop fusion | flops 5018112 | bytes 10315536 | tf_op jit(solution)/shard_map/add | solution.py:249
  196.1 2.7 %collective-permute-start.6 = (f32[1,4]{1,0:T(1,128)S(1)}, f32[1,4]{1,0:T(1,128)S(1)}, u32[]{:S(2)}, u32[]{:S(2)}) collective-permute-start(f32[1,4]{1,0:T(1,128)S(1)} %multiply_bitcast_fusion), channel_id=1, source_target_pairs={{0,1},{1,0},{2,3},{3,2},{4,5},{5,4},{6,7},{7,6},{8,9},{9,8},{10,11... | collective-permute-start | bytes 56 | tf_op jit(solution)/shard_map/ppermute | solution.py:45
  198.8 3.1 %collective-permute-done.6 = f32[1,4]{1,0:T(1,128)S(1)} collective-permute-done((f32[1,4]{1,0:T(1,128)S(1)}, f32[1,4]{1,0:T(1,128)S(1)}, u32[]{:S(2)}, u32[]{:S(2)}) %collective-permute-start.6) | collective-permute-done | bytes 48 | tf_op jit(solution)/shard_map/ppermute | solution.py:45
  201.9 1.9 collective-permute-start.7
  203.8 2.4 collective-permute-done.7
  206.2 2.2 collective-permute-start.8
  208.4 3.1 %collective-permute-done.8 = f32[4,4]{1,0:T(4,128)S(1)} collective-permute-done((f32[4,4]{1,0:T(4,128)S(1)}, f32[4,4]{1,0:T(4,128)S(1)}, u32[]{:S(2)}, u32[]{:S(2)}) %collective-permute-start.8) | collective-permute-done | bytes 96 | tf_op jit(solution)/shard_map/ppermute | solution.py:45
  211.4 2.3 collective-permute-start.9
  213.8 5.9 %collective-permute-done.9 = f32[8,4]{1,0:T(8,128)S(1)} collective-permute-done((f32[8,4]{1,0:T(8,128)S(1)}, f32[8,4]{1,0:T(8,128)S(1)}, u32[]{:S(2)}, u32[]{:S(2)}) %collective-permute-start.9) | collective-permute-done | bytes 160 | tf_op jit(solution)/shard_map/ppermute | solution.py:45
  219.9 5.2 %collective-permute-start.10 = (f32[16,4]{0,1:T(4,128)S(1)}, f32[16,4]{0,1:T(4,128)S(1)}, u32[]{:S(2)}, u32[]{:S(2)}) collective-permute-start(f32[16,4]{0,1:T(4,128)S(1)} %maximum_select_fusion.5), channel_id=1, source_target_pairs={{0,16},{1,17},{2,18},{3,19},{4,20},{5,21},{6,22},{7,23},{8,24},{9,... | collective-permute-start | bytes 776 | tf_op jit(solution)/shard_map/ppermute | solution.py:45
  225.1 7.8 %collective-permute-done.10 = f32[16,4]{0,1:T(4,128)S(1)} collective-permute-done((f32[16,4]{0,1:T(4,128)S(1)}, f32[16,4]{0,1:T(4,128)S(1)}, u32[]{:S(2)}, u32[]{:S(2)}) %collective-permute-start.10) | collective-permute-done | bytes 288 | tf_op jit(solution)/shard_map/ppermute | solution.py:45
  233.0 6.7 %collective-permute-start.11 = (f32[1,32,4]{1,2,0:T(4,128)S(1)}, f32[1,32,4]{1,2,0:T(4,128)S(1)}, u32[]{:S(2)}, u32[]{:S(2)}) collective-permute-start(f32[1,32,4]{1,2,0:T(4,128)S(1)} %maximum_select_fusion.6), channel_id=1, source_target_pairs={{0,32},{32,0},{64,96},{96,64},{128,160},{160,128},{192,224},{224,1... | collective-permute-start | bytes 1544 | tf_op jit(solution)/shard_map/ppermute | solution.py:45
  240.5 5.0 %collective-permute-start.12 = (f32[2,32,4]{1,2,0:T(4,128)S(1)}, f32[2,32,4]{1,2,0:T(4,128)S(1)}, u32[]{:S(2)}, u32[]{:S(2)}) collective-permute-start(f32[2,32,4]{1,2,0:T(4,128)S(1)} %maximum_select_fusion.3), channel_id=1, source_target_pairs={{0,64},{32,96},{64,0},{96,32},{128,192},{160,224},{192,128},{224,1... | collective-permute-start | bytes 3080 | tf_op jit(solution)/shard_map/ppermute | solution.py:45
  245.5 1.0 collective-permute-done.12
  246.5 5.2 %collective-permute-start.13 = (f32[4,32,4]{1,2,0:T(4,128)S(1)}, f32[4,32,4]{1,2,0:T(4,128)S(1)}, u32[]{:S(2)}, u32[]{:S(2)}) collective-permute-start(f32[4,32,4]{1,2,0:T(4,128)S(1)} %maximum_select_fusion.1), channel_id=1, source_target_pairs={{0,128},{32,160},{64,192},{96,224},{128,0},{160,32},{192,64},{224,... | collective-permute-start | bytes 6152 | tf_op jit(solution)/shard_map/ppermute | solution.py:45
  254.8 1.9 add_bitcast_fusion
  256.7 1.2 select_add_fusion
  258.4 1.2 fusion.25
  259.6 1.2 maximum_bitcast_fusion
  (126 shorter events, 25.0 us)
Async XLA Ops:
  7.1 5.6 %collective-permute-start = (s32[32,2,2,64]{3,1,2,0:T(2,128)S(1)}, s32[32,2,2,64]{3,1,2,0:T(2,128)S(1)}, u32[]{:S(2)}, u32[]{:S(2)}) collective-permute-start(s32[32,2,2,64]{3,1,2,0:T(2,128)S(1)} %pad_add_fusion), channel_id=1, source_target_pairs={{0,256},{256,0},{1,257},{257,1},{2,258},{258,2},{3,259},{259,3},{4... | collective-permute-start | bytes 98312 | tf_op jit(solution)/shard_map/ppermute | solution.py:24
  13.4 31.7 %all-to-all-start = ((s32[32,1,256]{2,1,0:T(1,128)}), s32[32,1,256]{2,1,0:T(1,128)S(1)}, u32[]{:S(2)}, u32[]{:S(2)}) async-start(s32[32,1,256]{2,1,0:T(1,128)} %reshape.642), calls=%async_computation | async-start | bytes 65536 | tf_op jit(solution)/shard_map/all_to_all | solution.py:193
  73.0 12.3 %copy-start.11 = (f32[1,1,2048]{2,1,0:T(1,128)S(1)}, f32[1,1,2048]{2,1,0:T(1,128)}, u32[]{:S(2)}) copy-start(f32[1,1,2048]{2,1,0:T(1,128)} %param.14) | copy-start | bytes 24580
  73.0 38.7 %copy-start.12 = (s32[1,1,2048]{2,1,0:T(1,128)S(1)}, s32[1,1,2048]{2,1,0:T(1,128)}, u32[]{:S(2)}) copy-start(s32[1,1,2048]{2,1,0:T(1,128)} %param.15) | copy-start | bytes 24580
  76.5 30.8 %all-to-all-start.1 = ((f32[32,1,3072]{2,1,0:T(1,128)}), f32[32,1,3072]{2,1,0:T(1,128)S(1)}, u32[]{:S(2)}, u32[]{:S(2)}) async-start(f32[32,1,3072]{2,1,0:T(1,128)} %reshape.644), calls=%async_computation.1 | async-start | bytes 786432 | tf_op jit(solution)/shard_map/all_to_all | solution.py:207
  109.5 16.0 %collective-permute-start.1 = (f32[32,2,64,24]{2,3,1,0:T(8,128)S(1)}, f32[32,2,64,24]{2,3,1,0:T(8,128)S(1)}, u32[]{:S(2)}, u32[]{:S(2)}) collective-permute-start(f32[32,2,64,24]{2,3,1,0:T(8,128)S(1)} %bitcast.144), channel_id=1, source_target_pairs={{0,256},{256,0},{1,257},{257,1},{2,258},{258,2},{3,259},{259,3},{4... | collective-permute-start | bytes 1179656 | tf_op jit(solution)/shard_map/ppermute | solution.py:24
  139.0 5.4 %copy-start.2 = (f32[1,4,128,128]{3,2,1,0:T(8,128)S(1)}, f32[1,4,128,128]{3,2,1,0:T(8,128)}, u32[]{:S(2)}) copy-start(f32[1,4,128,128]{3,2,1,0:T(8,128)} %param.9) | copy-start | bytes 786436
  144.5 11.4 %collective-permute-start.2 = (f32[28,3,128]{2,1,0:T(4,128)S(1)}, f32[28,3,128]{2,1,0:T(4,128)S(1)}, u32[]{:S(2)}, u32[]{:S(2)}) collective-permute-start(f32[28,3,128]{2,1,0:T(4,128)S(1)} %get-tuple-element.16), channel_id=1, source_target_pairs={{0,32},{32,64},{64,96},{96,128},{128,160},{160,192},{192,224},{1,3... | collective-permute-start | bytes 129032 | tf_op jit(solution)/shard_map/ppermute | solution.py:34
  153.4 5.5 %collective-permute-start.3 = (f32[28,3,128]{2,1,0:T(4,128)S(1)}, f32[28,3,128]{2,1,0:T(4,128)S(1)}, u32[]{:S(2)}, u32[]{:S(2)}) collective-permute-start(f32[28,3,128]{2,1,0:T(4,128)S(1)} %get-tuple-element.17), channel_id=1, source_target_pairs={{32,0},{64,32},{96,64},{128,96},{160,128},{192,160},{224,192},{33,... | collective-permute-start | bytes 129032 | tf_op jit(solution)/shard_map/ppermute | solution.py:35
  155.9 3.0 %copy-start.5 = (f32[28,3,128]{2,1,0:T(4,128)}, f32[28,3,128]{2,1,0:T(4,128)S(1)}, u32[]{:S(2)}) copy-start(f32[28,3,128]{2,1,0:T(4,128)S(1)} %collective-permute-done.2) | copy-start | bytes 129028
  158.9 0.6 copy-start.7
  165.0 8.6 %collective-permute-start.4 = (f32[28,134,3]{1,0,2:T(8,128)}, f32[28,134,3]{1,0,2:T(8,128)}, u32[]{:S(2)}, u32[]{:S(2)}) collective-permute-start(f32[28,134,3]{1,0,2:T(8,128)} %copy.96), channel_id=1, source_target_pairs={{0,1},{1,2},{2,3},{3,4},{4,5},{5,6},{6,7},{7,8},{8,9},{9,10},{10,1... | collective-permute-start | bytes 135080 | tf_op jit(solution)/shard_map/ppermute | solution.py:34
  172.1 7.2 %collective-permute-start.5 = (f32[28,134,3]{1,0,2:T(8,128)}, f32[28,134,3]{1,0,2:T(8,128)}, u32[]{:S(2)}, u32[]{:S(2)}) collective-permute-start(f32[28,134,3]{1,0,2:T(8,128)} %copy.97), channel_id=1, source_target_pairs={{1,0},{2,1},{3,2},{4,3},{5,4},{6,5},{7,6},{8,7},{9,8},{10,9},{11,1... | collective-permute-start | bytes 135080 | tf_op jit(solution)/shard_map/ppermute | solution.py:35
  187.2 1.5 copy-start
  187.2 1.5 copy-start.3
  187.2 1.5 copy-start.6
  187.2 1.5 copy-start.8
  192.7 0.8 copy-start.10
  192.9 0.8 copy-start.4
  193.5 0.8 copy-start.9
  194.2 58.5 %copy-start.13 = (f32[4]{0:T(128)S(1)}, f32[4]{0:T(128)}, u32[]{:S(2)}) copy-start(f32[4]{0:T(128)} %get-tuple-element.32) | copy-start | bytes 52
  194.2 58.5 %copy-start.14 = (f32[4]{0:T(128)S(1)}, f32[4]{0:T(128)}, u32[]{:S(2)}) copy-start(f32[4]{0:T(128)} %get-tuple-element.33) | copy-start | bytes 52
  194.2 59.1 %copy-start.15 = (f32[32]{0:T(128)S(1)}, f32[32]{0:T(128)}, u32[]{:S(2)}) copy-start(f32[32]{0:T(128)} %get-tuple-element.37) | copy-start | bytes 388
  194.2 59.1 %copy-start.16 = (f32[32]{0:T(128)S(1)}, f32[32]{0:T(128)}, u32[]{:S(2)}) copy-start(f32[32]{0:T(128)} %get-tuple-element.38) | copy-start | bytes 388
  194.3 59.1 %copy-start.17 = (f32[32]{0:T(128)S(1)}, f32[32]{0:T(128)}, u32[]{:S(2)}) copy-start(f32[32]{0:T(128)} %get-tuple-element.39) | copy-start | bytes 388
  194.8 0.8 copy-start.1
  196.1 5.8 %collective-permute-start.6 = (f32[1,4]{1,0:T(1,128)S(1)}, f32[1,4]{1,0:T(1,128)S(1)}, u32[]{:S(2)}, u32[]{:S(2)}) collective-permute-start(f32[1,4]{1,0:T(1,128)S(1)} %multiply_bitcast_fusion), channel_id=1, source_target_pairs={{0,1},{1,0},{2,3},{3,2},{4,5},{5,4},{6,7},{7,6},{8,9},{9,8},{10,11... | collective-permute-start | bytes 56 | tf_op jit(solution)/shard_map/ppermute | solution.py:45
  201.9 4.3 %collective-permute-start.7 = (f32[2,4]{1,0:T(2,128)S(1)}, f32[2,4]{1,0:T(2,128)S(1)}, u32[]{:S(2)}, u32[]{:S(2)}) collective-permute-start(f32[2,4]{1,0:T(2,128)S(1)} %maximum_select_fusion.7), channel_id=1, source_target_pairs={{0,2},{1,3},{2,0},{3,1},{4,6},{5,7},{6,4},{7,5},{8,10},{9,11},{10,... | collective-permute-start | bytes 104 | tf_op jit(solution)/shard_map/ppermute | solution.py:45
  206.2 5.2 %collective-permute-start.8 = (f32[4,4]{1,0:T(4,128)S(1)}, f32[4,4]{1,0:T(4,128)S(1)}, u32[]{:S(2)}, u32[]{:S(2)}) collective-permute-start(f32[4,4]{1,0:T(4,128)S(1)} %maximum_select_fusion.4), channel_id=1, source_target_pairs={{0,4},{1,5},{2,6},{3,7},{4,0},{5,1},{6,2},{7,3},{8,12},{9,13},{10,... | collective-permute-start | bytes 200 | tf_op jit(solution)/shard_map/ppermute | solution.py:45
  211.4 8.3 %collective-permute-start.9 = (f32[8,4]{1,0:T(8,128)S(1)}, f32[8,4]{1,0:T(8,128)S(1)}, u32[]{:S(2)}, u32[]{:S(2)}) collective-permute-start(f32[8,4]{1,0:T(8,128)S(1)} %maximum_select_fusion.2), channel_id=1, source_target_pairs={{0,8},{1,9},{2,10},{3,11},{4,12},{5,13},{6,14},{7,15},{8,0},{9,1},... | collective-permute-start | bytes 392 | tf_op jit(solution)/shard_map/ppermute | solution.py:45
  219.9 13.0 %collective-permute-start.10 = (f32[16,4]{0,1:T(4,128)S(1)}, f32[16,4]{0,1:T(4,128)S(1)}, u32[]{:S(2)}, u32[]{:S(2)}) collective-permute-start(f32[16,4]{0,1:T(4,128)S(1)} %maximum_select_fusion.5), channel_id=1, source_target_pairs={{0,16},{1,17},{2,18},{3,19},{4,20},{5,21},{6,22},{7,23},{8,24},{9,... | collective-permute-start | bytes 776 | tf_op jit(solution)/shard_map/ppermute | solution.py:45
  233.0 7.5 %collective-permute-start.11 = (f32[1,32,4]{1,2,0:T(4,128)S(1)}, f32[1,32,4]{1,2,0:T(4,128)S(1)}, u32[]{:S(2)}, u32[]{:S(2)}) collective-permute-start(f32[1,32,4]{1,2,0:T(4,128)S(1)} %maximum_select_fusion.6), channel_id=1, source_target_pairs={{0,32},{32,0},{64,96},{96,64},{128,160},{160,128},{192,224},{224,1... | collective-permute-start | bytes 1544 | tf_op jit(solution)/shard_map/ppermute | solution.py:45
  240.5 6.0 %collective-permute-start.12 = (f32[2,32,4]{1,2,0:T(4,128)S(1)}, f32[2,32,4]{1,2,0:T(4,128)S(1)}, u32[]{:S(2)}, u32[]{:S(2)}) collective-permute-start(f32[2,32,4]{1,2,0:T(4,128)S(1)} %maximum_select_fusion.3), channel_id=1, source_target_pairs={{0,64},{32,96},{64,0},{96,32},{128,192},{160,224},{192,128},{224,1... | collective-permute-start | bytes 3080 | tf_op jit(solution)/shard_map/ppermute | solution.py:45
  246.5 6.2 %collective-permute-start.13 = (f32[4,32,4]{1,2,0:T(4,128)S(1)}, f32[4,32,4]{1,2,0:T(4,128)S(1)}, u32[]{:S(2)}, u32[]{:S(2)}) collective-permute-start(f32[4,32,4]{1,2,0:T(4,128)S(1)} %maximum_select_fusion.1), channel_id=1, source_target_pairs={{0,128},{32,160},{64,192},{96,224},{128,0},{160,32},{192,64},{224,... | collective-permute-start | bytes 6152 | tf_op jit(solution)/shard_map/ppermute | solution.py:45

commit v6 on v5

--- a/solution.py
+++ b/solution.py
@@ -37,18 +37,11 @@
     return shard
 
 
-def doubling_gather(block, axis):
+def gather_by_exchange(block, axis):
     count = lax.axis_size(axis)
-    index = lax.axis_index(axis)
-    step = 1
-    while step < count:
-        other = lax.ppermute(block, axis, [(i, i ^ step) for i in range(count)])
-        low = (index & step) == 0
-        block = jnp.where(
-            low, jnp.concatenate([block, other], 0), jnp.concatenate([other, block], 0)
-        )
-        step *= 2
-    return block
+    repeated = jnp.broadcast_to(block[None], (count,) + block.shape)
+    gathered = lax.all_to_all(repeated, axis, split_axis=0, concat_axis=0, tiled=True)
+    return gathered.reshape((count * block.shape[0],) + block.shape[1:])
 
 
 def corner_blend(table, rows, weights, width):
@@ -258,8 +251,8 @@
     stepped = stepped_wide[:, :, 2:-2, 2:-2]
     resid_one = -divergence + lap_shrink(press_wide, gain_own)
     block_sum = jnp.sum(resid_one, axis=(1, 2)) * (1.0 / math.sqrt(rows_dev * cols_dev))
-    gathered = doubling_gather(block_sum[None], "lon")
-    gathered = doubling_gather(gathered[None], "lat")
+    gathered = gather_by_exchange(block_sum[None], "lon")
+    gathered = gather_by_exchange(gathered[None], "lat")
     coarse = coarse_solve(jnp.transpose(gathered, (2, 0, 1)), n_lat, n_lon)
     start = jnp.zeros((), jnp.int32)
     near = lax.dynamic_slice(

time: 263 us -> 241 us (0.916)
  starting transfers between devices: 80.1 us -> 63.1 us
  waiting for transfers between devices: 74.3 us -> 66.4 us
    ppermute x8 -> x0, starting transfers between devices: 31.1 us -> none  [doubling_gather(): other = lax.ppermute(block, axis, [(i, i ^ step) for i in range(count)])]
    ppermute x8 -> x0, waiting for transfers between devices: 24.7 us -> none  [doubling_gather(): other = lax.ppermute(block, axis, [(i, i ^ step) for i in range(count)])]
    all_to_all x0 -> x2, waiting for transfers between devices: none -> 16.9 us  [gather_by_exchange(): lax.all_to_all(repeated, axis, split_axis=0, concat_axis=0, tiled=True)]
    all_to_all x0 -> x2, starting transfers between devices: none -> 14.9 us  [gather_by_exchange(): lax.all_to_all(repeated, axis, split_axis=0, concat_axis=0, tiled=True)]
    unnamed x46 -> x57, local copies, waits for them, and re-layouts: 13 us -> 13.8 us
  transfers between devices with their start and end apart: 16 -> 10, of which waited for: 14 -> 7; matrix products, arithmetic and copies ran while one was open for 6% -> 7% of each run, Pallas kernels for 0% -> 0%
where the time goes in v6:
time: 241 us; the launch traced here: 239 us
  waiting for transfers between devices  66.4 us (28%)
  starting transfers between devices  63.1 us (26%)
  local copies, waits for them, and re-layouts  53.1 us (22%)
  other arithmetic  29.1 us (12%)
  Pallas kernels  24.8 us (10%)
    pallas_call x1, Pallas kernels, corner_blend(): pl.pallas_call(kernel, out_shape=jax.ShapeDtypeStruct((count, table.shape...  24.8 us
    all_to_all x1, waiting for transfers between devices, shards(): lax.all_to_all(served, 'lon', split_axis=0, concat_axis=0, tiled=True)  21.7 us
    all_to_all x1, starting transfers between devices, shards(): lax.all_to_all(requests, 'lon', split_axis=0, concat_axis=0, tiled=True)  17.4 us
    all_to_all x2, waiting for transfers between devices, gather_by_exchange(): lax.all_to_all(repeated, axis, split_axis=0, concat_axis=0, tiled=True)  16.9 us
    all_to_all x2, starting transfers between devices, gather_by_exchange(): lax.all_to_all(repeated, axis, split_axis=0, concat_axis=0, tiled=True)  14.9 us
    ppermute x2, starting transfers between devices, padded_2(): before = lax.ppermute(last, axis, up)  14.1 us
    ppermute x2, waiting for transfers between devices, partner_2(): return lax.ppermute(block, axis, route)  14 us
    unnamed x57, local copies, waits for them, and re-layouts  13.8 us
  transfers between devices with their start and end apart: 10, of which 7 were waited for; matrix products, arithmetic and copies ran while one was open for 7% of the time, Pallas kernels for 0%

profile of v6, /device:TPU:1, one launch (start us, length us, event | category | flops | bytes accessed | tf_op | source)
XLA Modules:
  0.0 239.5 jit_solution(5475762059513835884)
XLA Ops:
  0.6 0.7 fusion.49
  1.4 0.8 select_reduce_fusion
  3.4 1.4 reduce.17
  4.9 0.7 add_reduce_fusion
  7.1 3.9 %collective-permute-start = (s32[32,2,2,64]{3,1,2,0:T(2,128)S(1)}, s32[32,2,2,64]{3,1,2,0:T(2,128)S(1)}, u32[]{:S(2)}, u32[]{:S(2)}) collective-permute-start(s32[32,2,2,64]{3,1,2,0:T(2,128)S(1)} %pad_add_fusion), channel_id=1, source_target_pairs={{0,256},{256,0},{1,257},{257,1},{2,258},{258,2},{3,259},{259,3},{4... | collective-permute-start | bytes 98312 | tf_op jit(solution)/shard_map/ppermute | solution.py:24
  13.3 0.7 reshape.542
  14.0 17.4 %all-to-all-start = ((s32[32,1,256]{2,1,0:T(1,128)}), s32[32,1,256]{2,1,0:T(1,128)S(1)}, u32[]{:S(2)}, u32[]{:S(2)}) async-start(s32[32,1,256]{2,1,0:T(1,128)} %reshape.542), calls=%async_computation | async-start | bytes 65536 | tf_op jit(solution)/shard_map/all_to_all | solution.py:186
  31.5 2.3 copy.94
  33.8 4.6 %copy.67 = f32[24,16384]{0,1:T(8,128)} copy(f32[24,16384]{1,0:T(8,128)S(1)} %bitcast.135) | data formatting | bytes 3145728 | tf_op jit(solution)/shard_map/reshape;squeeze | solution.py:172
  38.5 6.7 %all-to-all-done = s32[32,1,256]{2,1,0:T(1,128)S(1)} async-done(((s32[32,1,256]{2,1,0:T(1,128)}), s32[32,1,256]{2,1,0:T(1,128)S(1)}, u32[]{:S(2)}, u32[]{:S(2)}) %all-to-all-start) | async-done | bytes 32800 | tf_op jit(solution)/shard_map/all_to_all | solution.py:186
  45.7 0.7 reduce.18
  46.8 0.7 reshape_squeeze.14.rows_ref
  47.5 0.7 pad_maximum_fusion.4.weights_ref
  48.2 24.8 %shard_map.95 = f32[4096,24]{1,0:T(8,128)} custom-call(s32[4096]{0:T(1024)} %reshape_squeeze.14.rows_ref, f32[4,4096]{1,0:T(4,128)} %pad_maximum_fusion.4.weights_ref, f32[16384,24]{1,0:T(8,128)} %bitcast.132), custom_call_target="tpu_custom_call" | custom-call | tf_op jit(solution)/shard_map/pallas_call | solution.py:61
  73.1 2.2 copy.65
  75.3 1.2 reshape.544
  76.5 7.3 %all-to-all-start.1 = ((f32[32,1,3072]{2,1,0:T(1,128)}), f32[32,1,3072]{2,1,0:T(1,128)S(1)}, u32[]{:S(2)}, u32[]{:S(2)}) async-start(f32[32,1,3072]{2,1,0:T(1,128)} %reshape.544), calls=%async_computation.1 | async-start | bytes 786432 | tf_op jit(solution)/shard_map/all_to_all | solution.py:200
  84.0 0.7 broadcast_and_fusion
  84.7 0.7 broadcast_and_fusion.1
  85.7 21.7 %all-to-all-done.1 = f32[32,1,3072]{2,1,0:T(1,128)S(1)} async-done(((f32[32,1,3072]{2,1,0:T(1,128)}), f32[32,1,3072]{2,1,0:T(1,128)S(1)}, u32[]{:S(2)}, u32[]{:S(2)}) %all-to-all-start.1) | async-done | bytes 393248 | tf_op jit(solution)/shard_map/all_to_all | solution.py:200
  107.9 1.5 reduce.19
  109.6 2.1 collective-permute-start.1
  111.7 14.0 %collective-permute-done.1 = f32[32,2,64,24]{2,3,1,0:T(8,128)S(1)} collective-permute-done((f32[32,2,64,24]{2,3,1,0:T(8,128)S(1)}, f32[32,2,64,24]{2,3,1,0:T(8,128)S(1)}, u32[]{:S(2)}, u32[]{:S(2)}) %collective-permute-start.1) | collective-permute-done | bytes 393248 | tf_op jit(solution)/shard_map/ppermute | solution.py:24
  127.1 12.2 %scatter_fusion = f32[24,16384]{0,1:T(8,128)} fusion(f32[24,16384]{0,1:T(8,128)} %copy.67, s32[2048]{0:T(1024)S(1)} %bitcast.163, f32[2048,24]{1,0:T(8,128)S(1)} %copy.68), kind=kCustom, calls=%fused_computation.3 | custom fusion | bytes 598016 | tf_op jit(solution)/shard_map/scatter | solution.py:218
  139.2 5.4 %copy.69 = f32[24,128,128]{2,1,0:T(8,128)S(1)} copy(f32[24,128,128]{0,2,1:T(8,128)} %bitcast.133) | data formatting | bytes 3145728 | tf_op jit(solution)/shard_map/reshape;reshape | solution.py:235
  144.7 8.9 %collective-permute-start.2 = (f32[28,3,128]{2,1,0:T(4,128)S(1)}, f32[28,3,128]{2,1,0:T(4,128)S(1)}, u32[]{:S(2)}, u32[]{:S(2)}) collective-permute-start(f32[28,3,128]{2,1,0:T(4,128)S(1)} %get-tuple-element.16), channel_id=1, source_target_pairs={{0,32},{32,64},{64,96},{96,128},{128,160},{160,192},{192,224},{1,3... | collective-permute-start | bytes 129032 | tf_op jit(solution)/shard_map/ppermute | solution.py:34
  153.5 1.9 collective-permute-start.3
  155.5 3.5 %collective-permute-done.3 = f32[28,3,128]{2,1,0:T(4,128)S(1)} collective-permute-done((f32[28,3,128]{2,1,0:T(4,128)S(1)}, f32[28,3,128]{2,1,0:T(4,128)S(1)}, u32[]{:S(2)}, u32[]{:S(2)}) %collective-permute-start.3) | collective-permute-done | bytes 43040 | tf_op jit(solution)/shard_map/ppermute | solution.py:35
  159.8 1.9 fusion.103
  161.8 3.4 %copy.84 = f32[28,134,3]{1,0,2:T(8,128)} copy(f32[28,134,3]{2,1,0:T(8,128)} %get-tuple-element.14) | data formatting | bytes 90048
  165.1 5.2 %collective-permute-start.4 = (f32[28,134,3]{1,0,2:T(8,128)}, f32[28,134,3]{1,0,2:T(8,128)}, u32[]{:S(2)}, u32[]{:S(2)}) collective-permute-start(f32[28,134,3]{1,0,2:T(8,128)} %copy.84), channel_id=1, source_target_pairs={{0,1},{1,2},{2,3},{3,4},{4,5},{5,6},{6,7},{7,8},{8,9},{9,10},{10,1... | collective-permute-start | bytes 135080 | tf_op jit(solution)/shard_map/ppermute | solution.py:34
  170.3 1.8 copy.85
  172.2 1.5 collective-permute-start.5
  174.2 1.6 copy.72
  175.7 3.6 %collective-permute-done.5 = f32[28,134,3]{1,0,2:T(8,128)} collective-permute-done((f32[28,134,3]{1,0,2:T(8,128)}, f32[28,134,3]{1,0,2:T(8,128)}, u32[]{:S(2)}, u32[]{:S(2)}) %collective-permute-start.5) | collective-permute-done | bytes 45056 | tf_op jit(solution)/shard_map/ppermute | solution.py:35
  179.4 2.9 %copy.73 = f32[28,134,3]{2,1,0:T(8,128)} copy(f32[28,134,3]{1,0,2:T(8,128)} %collective-permute-done.5) | data formatting | bytes 90048 | tf_op jit(solution)/shard_map/ppermute | solution.py:35
  182.2 4.8 %pad_maximum_fusion = f32[28,134,134]{2,1,0:T(8,128)S(1)} fusion(f32[28,134,3]{2,1,0:T(8,128)} %copy.73, f32[28,3,128]{2,1,0:T(4,128)} %copy-done.8, f32[4,128,128]{2,1,0:T(8,128)} %bitcast.136, f32[24,128,128]{2,1,0:T(8,128)S(1)} %copy.69, f32[28,3,128]{2,1,0:T(4,128)} %copy-done.6, f32[28,134,3]{2,1,0:T(8,128)S(1)} %copy.72), kind=kLoop, calls=%fused_computation.6 | loop fusion | flops 2513840 | bytes 4022144 | tf_op jit(solution)/shard_map/concatenate | solution.py:36
  187.3 0.9 slice.275
  189.2 3.6 %fusion.4 = f32[6,4,132,132]{3,2,1,0:T(8,128)S(1)} fusion(f32[6,4,132,132]{3,2,1,0:T(8,128)S(1)} %slice.275, f32[6,4,134,134]{3,2,1,0:T(8,128)S(1)} %bitcast.130, f32[132]{0:T(256)S(1)} %divide_multiply_fusion, f32[4,132,132]{2,1,0:T(8,128)S(1)} %pad_maximum_fusion.3), kind=kLoop, calls=%fused_computation.11 | loop fusion | flops 5018112 | bytes 10315536 | tf_op jit(solution)/shard_map/add | solution.py:242
  196.8 8.1 %all-to-all-start.2 = ((f32[32,1,4]{2,1,0:T(1,128)}), f32[32,1,4]{2,1,0:T(1,128)S(1)}, u32[]{:S(2)}, u32[]{:S(2)}) async-start(f32[32,1,4]{2,1,0:T(1,128)} %broadcast_in_dim.159), calls=%async_computation.2 | async-start | bytes 32768 | tf_op jit(solution)/shard_map/all_to_all | solution.py:43
  204.9 13.6 %all-to-all-done.2 = f32[32,1,4]{2,1,0:T(1,128)S(1)} async-done(((f32[32,1,4]{2,1,0:T(1,128)}), f32[32,1,4]{2,1,0:T(1,128)S(1)}, u32[]{:S(2)}, u32[]{:S(2)}) %all-to-all-start.2) | async-done | bytes 544 | tf_op jit(solution)/shard_map/all_to_all | solution.py:43
  219.3 6.8 %all-to-all-start.3 = ((f32[8,1,128]{2,1,0:T(1,128)}), f32[8,1,128]{2,1,0:T(1,128)S(1)}, u32[]{:S(2)}, u32[]{:S(2)}) async-start(f32[8,1,128]{2,1,0:T(1,128)} %reshape.546), calls=%async_computation.3 | async-start | bytes 8192 | tf_op jit(solution)/shard_map/all_to_all | solution.py:43
  226.2 1.2 slice.302
  227.3 3.3 %all-to-all-done.3 = f32[8,1,128]{2,1,0:T(1,128)S(1)} async-done(((f32[8,1,128]{2,1,0:T(1,128)}), f32[8,1,128]{2,1,0:T(1,128)S(1)}, u32[]{:S(2)}, u32[]{:S(2)}) %all-to-all-start.3) | async-done | bytes 4128 | tf_op jit(solution)/shard_map/all_to_all | solution.py:43
  233.4 1.9 add_bitcast_fusion
  235.3 1.2 select_add_fusion
  237.0 1.2 fusion.25
  238.2 1.2 maximum_bitcast_fusion
  (119 shorter events, 19.0 us)
Async XLA Ops:
  7.1 6.2 %collective-permute-start = (s32[32,2,2,64]{3,1,2,0:T(2,128)S(1)}, s32[32,2,2,64]{3,1,2,0:T(2,128)S(1)}, u32[]{:S(2)}, u32[]{:S(2)}) collective-permute-start(s32[32,2,2,64]{3,1,2,0:T(2,128)S(1)} %pad_add_fusion), channel_id=1, source_target_pairs={{0,256},{256,0},{1,257},{257,1},{2,258},{258,2},{3,259},{259,3},{4... | collective-permute-start | bytes 98312 | tf_op jit(solution)/shard_map/ppermute | solution.py:24
  14.0 31.1 %all-to-all-start = ((s32[32,1,256]{2,1,0:T(1,128)}), s32[32,1,256]{2,1,0:T(1,128)S(1)}, u32[]{:S(2)}, u32[]{:S(2)}) async-start(s32[32,1,256]{2,1,0:T(1,128)} %reshape.542), calls=%async_computation | async-start | bytes 65536 | tf_op jit(solution)/shard_map/all_to_all | solution.py:186
  73.1 12.4 %copy-start.12 = (f32[1,1,2048]{2,1,0:T(1,128)S(1)}, f32[1,1,2048]{2,1,0:T(1,128)}, u32[]{:S(2)}) copy-start(f32[1,1,2048]{2,1,0:T(1,128)} %param.14) | copy-start | bytes 24580
  73.1 38.6 %copy-start.13 = (s32[1,1,2048]{2,1,0:T(1,128)S(1)}, s32[1,1,2048]{2,1,0:T(1,128)}, u32[]{:S(2)}) copy-start(s32[1,1,2048]{2,1,0:T(1,128)} %param.15) | copy-start | bytes 24580
  76.5 30.9 %all-to-all-start.1 = ((f32[32,1,3072]{2,1,0:T(1,128)}), f32[32,1,3072]{2,1,0:T(1,128)S(1)}, u32[]{:S(2)}, u32[]{:S(2)}) async-start(f32[32,1,3072]{2,1,0:T(1,128)} %reshape.544), calls=%async_computation.1 | async-start | bytes 786432 | tf_op jit(solution)/shard_map/all_to_all | solution.py:200
  109.6 16.1 %collective-permute-start.1 = (f32[32,2,64,24]{2,3,1,0:T(8,128)S(1)}, f32[32,2,64,24]{2,3,1,0:T(8,128)S(1)}, u32[]{:S(2)}, u32[]{:S(2)}) collective-permute-start(f32[32,2,64,24]{2,3,1,0:T(8,128)S(1)} %bitcast.150), channel_id=1, source_target_pairs={{0,256},{256,0},{1,257},{257,1},{2,258},{258,2},{3,259},{259,3},{4... | collective-permute-start | bytes 1179656 | tf_op jit(solution)/shard_map/ppermute | solution.py:24
  139.2 5.4 %copy-start.2 = (f32[1,4,128,128]{3,2,1,0:T(8,128)S(1)}, f32[1,4,128,128]{3,2,1,0:T(8,128)}, u32[]{:S(2)}) copy-start(f32[1,4,128,128]{3,2,1,0:T(8,128)} %param.9) | copy-start | bytes 786436
  144.7 10.9 %collective-permute-start.2 = (f32[28,3,128]{2,1,0:T(4,128)S(1)}, f32[28,3,128]{2,1,0:T(4,128)S(1)}, u32[]{:S(2)}, u32[]{:S(2)}) collective-permute-start(f32[28,3,128]{2,1,0:T(4,128)S(1)} %get-tuple-element.16), channel_id=1, source_target_pairs={{0,32},{32,64},{64,96},{96,128},{128,160},{160,192},{192,224},{1,3... | collective-permute-start | bytes 129032 | tf_op jit(solution)/shard_map/ppermute | solution.py:34
  153.5 5.5 %collective-permute-start.3 = (f32[28,3,128]{2,1,0:T(4,128)S(1)}, f32[28,3,128]{2,1,0:T(4,128)S(1)}, u32[]{:S(2)}, u32[]{:S(2)}) collective-permute-start(f32[28,3,128]{2,1,0:T(4,128)S(1)} %get-tuple-element.17), channel_id=1, source_target_pairs={{32,0},{64,32},{96,64},{128,96},{160,128},{192,160},{224,192},{33,... | collective-permute-start | bytes 129032 | tf_op jit(solution)/shard_map/ppermute | solution.py:35
  155.5 3.5 %copy-start.6 = (f32[28,3,128]{2,1,0:T(4,128)}, f32[28,3,128]{2,1,0:T(4,128)S(1)}, u32[]{:S(2)}) copy-start(f32[28,3,128]{2,1,0:T(4,128)S(1)} %collective-permute-done.2) | copy-start | bytes 129028
  159.0 0.6 copy-start.8
  165.1 9.0 %collective-permute-start.4 = (f32[28,134,3]{1,0,2:T(8,128)}, f32[28,134,3]{1,0,2:T(8,128)}, u32[]{:S(2)}, u32[]{:S(2)}) collective-permute-start(f32[28,134,3]{1,0,2:T(8,128)} %copy.84), channel_id=1, source_target_pairs={{0,1},{1,2},{2,3},{3,4},{4,5},{5,6},{6,7},{7,8},{8,9},{9,10},{10,1... | collective-permute-start | bytes 135080 | tf_op jit(solution)/shard_map/ppermute | solution.py:34
  172.2 7.2 %collective-permute-start.5 = (f32[28,134,3]{1,0,2:T(8,128)}, f32[28,134,3]{1,0,2:T(8,128)}, u32[]{:S(2)}, u32[]{:S(2)}) collective-permute-start(f32[28,134,3]{1,0,2:T(8,128)} %copy.85), channel_id=1, source_target_pairs={{1,0},{2,1},{3,2},{4,3},{5,4},{6,5},{7,6},{8,7},{9,8},{10,9},{11,1... | collective-permute-start | bytes 135080 | tf_op jit(solution)/shard_map/ppermute | solution.py:35
  187.3 1.5 copy-start
  187.3 1.5 copy-start.3
  187.3 1.5 copy-start.7
  187.3 1.5 copy-start.9
  192.8 0.8 copy-start.11
  193.0 0.8 copy-start.4
  193.5 0.8 copy-start.10
  194.3 37.0 %copy-start.18 = (f32[4]{0:T(128)S(1)}, f32[4]{0:T(128)}, u32[]{:S(2)}) copy-start(f32[4]{0:T(128)} %get-tuple-element.32) | copy-start | bytes 52
  194.3 37.0 %copy-start.19 = (f32[4]{0:T(128)S(1)}, f32[4]{0:T(128)}, u32[]{:S(2)}) copy-start(f32[4]{0:T(128)} %get-tuple-element.33) | copy-start | bytes 52
  194.3 37.0 %copy-start.21 = (f32[4]{0:T(128)S(1)}, f32[4]{0:T(128)}, u32[]{:S(2)}) copy-start(f32[4]{0:T(128)} %iota_multiply_fusion.2) | copy-start | bytes 52
  194.3 37.4 %copy-start.14 = (f32[8]{0:T(128)S(1)}, f32[8]{0:T(128)}, u32[]{:S(2)}) copy-start(f32[8]{0:T(128)} %get-tuple-element.34) | copy-start | bytes 100
  194.3 37.4 %copy-start.15 = (f32[8]{0:T(128)S(1)}, f32[8]{0:T(128)}, u32[]{:S(2)}) copy-start(f32[8]{0:T(128)} %get-tuple-element.35) | copy-start | bytes 100
  194.3 37.7 %copy-start.16 = (f32[32]{0:T(128)S(1)}, f32[32]{0:T(128)}, u32[]{:S(2)}) copy-start(f32[32]{0:T(128)} %get-tuple-element.38) | copy-start | bytes 388
  194.3 37.7 %copy-start.17 = (f32[32]{0:T(128)S(1)}, f32[32]{0:T(128)}, u32[]{:S(2)}) copy-start(f32[32]{0:T(128)} %get-tuple-element.39) | copy-start | bytes 388
  194.3 37.7 %copy-start.20 = (f32[32]{0:T(128)S(1)}, f32[32]{0:T(128)}, u32[]{:S(2)}) copy-start(f32[32]{0:T(128)} %get-tuple-element.37) | copy-start | bytes 388
  194.9 0.8 copy-start.1
  196.8 21.7 %all-to-all-start.2 = ((f32[32,1,4]{2,1,0:T(1,128)}), f32[32,1,4]{2,1,0:T(1,128)S(1)}, u32[]{:S(2)}, u32[]{:S(2)}) async-start(f32[32,1,4]{2,1,0:T(1,128)} %broadcast_in_dim.159), calls=%async_computation.2 | async-start | bytes 32768 | tf_op jit(solution)/shard_map/all_to_all | solution.py:43
  219.3 11.3 %all-to-all-start.3 = ((f32[8,1,128]{2,1,0:T(1,128)}), f32[8,1,128]{2,1,0:T(1,128)S(1)}, u32[]{:S(2)}, u32[]{:S(2)}) async-start(f32[8,1,128]{2,1,0:T(1,128)} %reshape.546), calls=%async_computation.3 | async-start | bytes 8192 | tf_op jit(solution)/shard_map/all_to_all | solution.py:43
  231.3 6.9 %copy-start.5 = (f32[3,4,128,128]{3,2,1,0:T(8,128)S(1)}, f32[3,4,128,128]{3,2,1,0:T(8,128)}, u32[]{:S(2)}) copy-start(f32[3,4,128,128]{3,2,1,0:T(8,128)} %slice.302) | copy-start | bytes 2359300

commit v7 on v6

--- a/solution.py
+++ b/solution.py
@@ -183,6 +183,7 @@
         [empty.at[slot_of].set(base_cell), empty.at[slot_of].set(weight_ids)], axis=1
     ).reshape(n_lon, capacity, 2, block_cells)
     requests = partner_2(asked, "panel", 0)
+    slot_mirror = partner_2(slot_of, "panel", 0)
     requests = lax.all_to_all(requests, "lon", split_axis=0, concat_axis=0, tiled=True)
     cells_asked = requests[:, :, 0, :].reshape(-1)
     frac_lat, frac_lon = fractions(requests[:, :, 1, :].reshape(-1))
@@ -198,8 +199,8 @@
     served = corner_blend(flat_cells.T, cells_asked, weights, cols_dev)
     served = served.reshape(n_lon, capacity, block_cells, channels)
     served = lax.all_to_all(served, "lon", split_axis=0, concat_axis=0, tiled=True)
-    served = partner_2(served, "panel", 0)
-    values = served.reshape(slot_count, block_cells, channels)[slot_of]
+    served = served.reshape(slot_count, block_cells, channels)[slot_mirror]
+    values = partner_2(served, "panel", 0)
     values = values.reshape(blocks * block_cells, channels).T.reshape(6, levels, blocks * block_cells)
     turn = border_angle[0, 0]
     cos_angle = jnp.cos(turn)

time: 241 us -> 237 us (0.983)
  waiting for transfers between devices: 66.4 us -> 59.6 us
    ppermute x2 -> x3, waiting for transfers between devices: 14 us -> 6.23 us  [partner_2(): return lax.ppermute(block, axis, route)]
    ppermute x2 -> x3, starting transfers between devices: 6.02 us -> 8.08 us  [partner_2(): return lax.ppermute(block, axis, route)]
  transfers between devices with their start and end apart: 10 -> 11, of which waited for: 7 -> 7; matrix products, arithmetic and copies ran while one was open for 7% -> 10% of each run, Pallas kernels for 0% -> 11%
where the time goes in v7:
time: 237 us; the launch traced here: 236 us
  starting transfers between devices  65.2 us (28%)
  waiting for transfers between devices  59.6 us (25%)
  local copies, waits for them, and re-layouts  53.1 us (22%)
  other arithmetic  30.2 us (13%)
  Pallas kernels  24.8 us (10%)
    pallas_call x1, Pallas kernels, corner_blend(): pl.pallas_call(kernel, out_shape=jax.ShapeDtypeStruct((count, table.shape...  24.8 us
    all_to_all x1, waiting for transfers between devices, shards(): lax.all_to_all(served, 'lon', split_axis=0, concat_axis=0, tiled=True)  22.8 us
    all_to_all x1, starting transfers between devices, shards(): lax.all_to_all(requests, 'lon', split_axis=0, concat_axis=0, tiled=True)  17.9 us
    all_to_all x2, waiting for transfers between devices, gather_by_exchange(): lax.all_to_all(repeated, axis, split_axis=0, concat_axis=0, tiled=True)  16.9 us
    all_to_all x2, starting transfers between devices, gather_by_exchange(): lax.all_to_all(repeated, axis, split_axis=0, concat_axis=0, tiled=True)  14.4 us
    ppermute x2, starting transfers between devices, padded_2(): before = lax.ppermute(last, axis, up)  14.1 us
    unnamed x57, local copies, waits for them, and re-layouts  13.7 us
    scatter x1, local copies, waits for them, and re-layouts, shards(): flat_cells.at[:, dest_cell[0, 0]].set(rotated)  12.2 us
  transfers between devices with their start and end apart: 11, of which 7 were waited for; matrix products, arithmetic and copies ran while one was open for 10% of the time, Pallas kernels for 11%

profile of v7, /device:TPU:1, one launch (start us, length us, event | category | flops | bytes accessed | tf_op | source)
XLA Modules:
  0.0 235.9 jit_solution(5676168183005020740)
XLA Ops:
  0.6 0.7 fusion.49
  1.4 0.8 select_reduce_fusion
  3.4 1.4 reduce.17
  4.9 0.7 add_reduce_fusion
  7.1 3.9 %collective-permute-start = (s32[32,2,2,64]{3,1,2,0:T(2,128)S(1)}, s32[32,2,2,64]{3,1,2,0:T(2,128)S(1)}, u32[]{:S(2)}, u32[]{:S(2)}) collective-permute-start(s32[32,2,2,64]{3,1,2,0:T(2,128)S(1)} %pad_add_fusion), channel_id=1, source_target_pairs={{0,256},{256,0},{1,257},{257,1},{2,258},{258,2},{3,259},{259,3},{4... | collective-permute-start | bytes 98312 | tf_op jit(solution)/shard_map/ppermute | solution.py:24
  11.7 1.9 collective-permute-start.1
  16.7 0.7 reshape.543
  17.4 17.9 %all-to-all-start = ((s32[32,1,256]{2,1,0:T(1,128)}), s32[32,1,256]{2,1,0:T(1,128)S(1)}, u32[]{:S(2)}, u32[]{:S(2)}) async-start(s32[32,1,256]{2,1,0:T(1,128)} %reshape.543), calls=%async_computation | async-start | bytes 65536 | tf_op jit(solution)/shard_map/all_to_all | solution.py:187
  35.4 2.3 copy.94
  37.7 4.6 %copy.67 = f32[24,16384]{0,1:T(8,128)} copy(f32[24,16384]{1,0:T(8,128)S(1)} %bitcast.136) | data formatting | bytes 3145728 | tf_op jit(solution)/shard_map/reshape;squeeze | solution.py:172
  42.4 6.7 %all-to-all-done = s32[32,1,256]{2,1,0:T(1,128)S(1)} async-done(((s32[32,1,256]{2,1,0:T(1,128)}), s32[32,1,256]{2,1,0:T(1,128)S(1)}, u32[]{:S(2)}, u32[]{:S(2)}) %all-to-all-start) | async-done | bytes 32800 | tf_op jit(solution)/shard_map/all_to_all | solution.py:187
  49.6 0.7 reduce.18
  51.5 0.7 pad_maximum_fusion.4.weights_ref
  52.2 24.8 %shard_map.95 = f32[4096,24]{1,0:T(8,128)} custom-call(s32[4096]{0:T(1024)} %reshape_squeeze.14.rows_ref, f32[4,4096]{1,0:T(4,128)} %pad_maximum_fusion.4.weights_ref, f32[16384,24]{1,0:T(8,128)} %bitcast.133), custom_call_target="tpu_custom_call" | custom-call | tf_op jit(solution)/shard_map/pallas_call | solution.py:61
  77.0 2.2 copy.65
  79.2 1.2 reshape.545
  80.5 7.3 %all-to-all-start.1 = ((f32[32,1,3072]{2,1,0:T(1,128)}), f32[32,1,3072]{2,1,0:T(1,128)S(1)}, u32[]{:S(2)}, u32[]{:S(2)}) async-start(f32[32,1,3072]{2,1,0:T(1,128)} %reshape.545), calls=%async_computation.1 | async-start | bytes 786432 | tf_op jit(solution)/shard_map/all_to_all | solution.py:201
  87.8 0.7 broadcast_and_fusion.1
  88.9 22.8 %all-to-all-done.1 = f32[32,1,3072]{2,1,0:T(1,128)S(1)} async-done(((f32[32,1,3072]{2,1,0:T(1,128)}), f32[32,1,3072]{2,1,0:T(1,128)S(1)}, u32[]{:S(2)}, u32[]{:S(2)}) %all-to-all-start.1) | async-done | bytes 393248 | tf_op jit(solution)/shard_map/all_to_all | solution.py:201
  112.2 1.6 reduce.19
  114.6 2.2 collective-permute-start.2
  116.9 6.2 %collective-permute-done.2 = f32[32,64,24]{1,2,0:T(8,128)S(1)} collective-permute-done((f32[32,64,24]{1,2,0:T(8,128)S(1)}, f32[32,64,24]{1,2,0:T(8,128)S(1)}, u32[]{:S(2)}, u32[]{:S(2)}) %collective-permute-start.2) | collective-permute-done | bytes 196640 | tf_op jit(solution)/shard_map/ppermute | solution.py:24
  123.9 12.2 %scatter_fusion = f32[24,16384]{0,1:T(8,128)} fusion(f32[24,16384]{0,1:T(8,128)} %copy.67, s32[2048]{0:T(1024)S(1)} %bitcast.163, f32[2048,24]{1,0:T(8,128)S(1)} %copy.68), kind=kCustom, calls=%fused_computation.3 | custom fusion | bytes 598016 | tf_op jit(solution)/shard_map/scatter | solution.py:219
  136.1 5.4 %copy.69 = f32[24,128,128]{2,1,0:T(8,128)S(1)} copy(f32[24,128,128]{0,2,1:T(8,128)} %bitcast.134) | data formatting | bytes 3145728 | tf_op jit(solution)/shard_map/reshape;reshape | solution.py:236
  141.5 8.8 %collective-permute-start.3 = (f32[28,3,128]{2,1,0:T(4,128)S(1)}, f32[28,3,128]{2,1,0:T(4,128)S(1)}, u32[]{:S(2)}, u32[]{:S(2)}) collective-permute-start(f32[28,3,128]{2,1,0:T(4,128)S(1)} %get-tuple-element.16), channel_id=1, source_target_pairs={{0,32},{32,64},{64,96},{96,128},{128,160},{160,192},{192,224},{1,3... | collective-permute-start | bytes 129032 | tf_op jit(solution)/shard_map/ppermute | solution.py:34
  150.4 1.9 collective-permute-start.4
  152.4 3.5 %collective-permute-done.4 = f32[28,3,128]{2,1,0:T(4,128)S(1)} collective-permute-done((f32[28,3,128]{2,1,0:T(4,128)S(1)}, f32[28,3,128]{2,1,0:T(4,128)S(1)}, u32[]{:S(2)}, u32[]{:S(2)}) %collective-permute-start.4) | collective-permute-done | bytes 43040 | tf_op jit(solution)/shard_map/ppermute | solution.py:35
  156.7 1.9 fusion.103
  158.6 3.4 %copy.84 = f32[28,134,3]{1,0,2:T(8,128)} copy(f32[28,134,3]{2,1,0:T(8,128)} %get-tuple-element.14) | data formatting | bytes 90048
  162.0 5.2 %collective-permute-start.5 = (f32[28,134,3]{1,0,2:T(8,128)}, f32[28,134,3]{1,0,2:T(8,128)}, u32[]{:S(2)}, u32[]{:S(2)}) collective-permute-start(f32[28,134,3]{1,0,2:T(8,128)} %copy.84), channel_id=1, source_target_pairs={{0,1},{1,2},{2,3},{3,4},{4,5},{5,6},{6,7},{7,8},{8,9},{9,10},{10,1... | collective-permute-start | bytes 135080 | tf_op jit(solution)/shard_map/ppermute | solution.py:34
  167.2 1.8 copy.85
  169.0 1.5 collective-permute-start.6
  171.1 1.6 copy.72
  172.7 3.6 %collective-permute-done.6 = f32[28,134,3]{1,0,2:T(8,128)} collective-permute-done((f32[28,134,3]{1,0,2:T(8,128)}, f32[28,134,3]{1,0,2:T(8,128)}, u32[]{:S(2)}, u32[]{:S(2)}) %collective-permute-start.6) | collective-permute-done | bytes 45056 | tf_op jit(solution)/shard_map/ppermute | solution.py:35
  176.2 2.9 %copy.73 = f32[28,134,3]{2,1,0:T(8,128)} copy(f32[28,134,3]{1,0,2:T(8,128)} %collective-permute-done.6) | data formatting | bytes 90048 | tf_op jit(solution)/shard_map/ppermute | solution.py:35
  179.1 4.8 %pad_maximum_fusion = f32[28,134,134]{2,1,0:T(8,128)S(1)} fusion(f32[28,134,3]{2,1,0:T(8,128)} %copy.73, f32[28,3,128]{2,1,0:T(4,128)} %copy-done.8, f32[4,128,128]{2,1,0:T(8,128)} %bitcast.138, f32[24,128,128]{2,1,0:T(8,128)S(1)} %copy.69, f32[28,3,128]{2,1,0:T(4,128)} %copy-done.6, f32[28,134,3]{2,1,0:T(8,128)S(1)} %copy.72), kind=kLoop, calls=%fused_computation.6 | loop fusion | flops 2513840 | bytes 4022144 | tf_op jit(solution)/shard_map/concatenate | solution.py:36
  184.2 0.9 slice.275
  186.1 3.6 %fusion.4 = f32[6,4,132,132]{3,2,1,0:T(8,128)S(1)} fusion(f32[6,4,132,132]{3,2,1,0:T(8,128)S(1)} %slice.275, f32[6,4,134,134]{3,2,1,0:T(8,128)S(1)} %bitcast.131, f32[132]{0:T(256)S(1)} %divide_multiply_fusion, f32[4,132,132]{2,1,0:T(8,128)S(1)} %pad_maximum_fusion.3), kind=kLoop, calls=%fused_computation.11 | loop fusion | flops 5018112 | bytes 10315536 | tf_op jit(solution)/shard_map/add | solution.py:243
  193.6 7.6 %all-to-all-start.2 = ((f32[32,1,4]{2,1,0:T(1,128)}), f32[32,1,4]{2,1,0:T(1,128)S(1)}, u32[]{:S(2)}, u32[]{:S(2)}) async-start(f32[32,1,4]{2,1,0:T(1,128)} %broadcast_in_dim.162), calls=%async_computation.2 | async-start | bytes 32768 | tf_op jit(solution)/shard_map/all_to_all | solution.py:43
  201.2 13.6 %all-to-all-done.2 = f32[32,1,4]{2,1,0:T(1,128)S(1)} async-done(((f32[32,1,4]{2,1,0:T(1,128)}), f32[32,1,4]{2,1,0:T(1,128)S(1)}, u32[]{:S(2)}, u32[]{:S(2)}) %all-to-all-start.2) | async-done | bytes 544 | tf_op jit(solution)/shard_map/all_to_all | solution.py:43
  215.6 6.8 %all-to-all-start.3 = ((f32[8,1,128]{2,1,0:T(1,128)}), f32[8,1,128]{2,1,0:T(1,128)S(1)}, u32[]{:S(2)}, u32[]{:S(2)}) async-start(f32[8,1,128]{2,1,0:T(1,128)} %reshape.547), calls=%async_computation.3 | async-start | bytes 8192 | tf_op jit(solution)/shard_map/all_to_all | solution.py:43
  222.5 1.2 slice.302
  223.6 3.3 %all-to-all-done.3 = f32[8,1,128]{2,1,0:T(1,128)S(1)} async-done(((f32[8,1,128]{2,1,0:T(1,128)}), f32[8,1,128]{2,1,0:T(1,128)S(1)}, u32[]{:S(2)}, u32[]{:S(2)}) %all-to-all-start.3) | async-done | bytes 4128 | tf_op jit(solution)/shard_map/all_to_all | solution.py:43
  226.9 0.7 reduce.20
  229.8 1.9 add_bitcast_fusion
  231.7 1.2 select_add_fusion
  233.4 1.2 fusion.25
  234.7 1.2 maximum_bitcast_fusion
  (123 shorter events, 20.7 us)
Async XLA Ops:
  7.1 9.6 %collective-permute-start = (s32[32,2,2,64]{3,1,2,0:T(2,128)S(1)}, s32[32,2,2,64]{3,1,2,0:T(2,128)S(1)}, u32[]{:S(2)}, u32[]{:S(2)}) collective-permute-start(s32[32,2,2,64]{3,1,2,0:T(2,128)S(1)} %pad_add_fusion), channel_id=1, source_target_pairs={{0,256},{256,0},{1,257},{257,1},{2,258},{258,2},{3,259},{259,3},{4... | collective-permute-start | bytes 98312 | tf_op jit(solution)/shard_map/ppermute | solution.py:24
  11.7 77.1 %collective-permute-start.1 = (s32[32]{0:T(128)S(1)}, s32[32]{0:T(128)S(1)}, u32[]{:S(2)}, u32[]{:S(2)}) collective-permute-start(s32[32]{0:T(128)S(1)} %multiply_add_fusion.1), channel_id=1, source_target_pairs={{0,256},{256,0},{1,257},{257,1},{2,258},{258,2},{3,259},{259,3},{4... | collective-permute-start | bytes 392 | tf_op jit(solution)/shard_map/ppermute | solution.py:24
  17.4 31.7 %all-to-all-start = ((s32[32,1,256]{2,1,0:T(1,128)}), s32[32,1,256]{2,1,0:T(1,128)S(1)}, u32[]{:S(2)}, u32[]{:S(2)}) async-start(s32[32,1,256]{2,1,0:T(1,128)} %reshape.543), calls=%async_computation | async-start | bytes 65536 | tf_op jit(solution)/shard_map/all_to_all | solution.py:187
  77.0 11.5 %copy-start.13 = (s32[1,1,2048]{2,1,0:T(1,128)S(1)}, s32[1,1,2048]{2,1,0:T(1,128)}, u32[]{:S(2)}) copy-start(s32[1,1,2048]{2,1,0:T(1,128)} %param.15) | copy-start | bytes 24580
  77.0 11.5 %copy-start.12 = (f32[1,1,2048]{2,1,0:T(1,128)S(1)}, f32[1,1,2048]{2,1,0:T(1,128)}, u32[]{:S(2)}) copy-start(f32[1,1,2048]{2,1,0:T(1,128)} %param.14) | copy-start | bytes 24580
  80.5 31.2 %all-to-all-start.1 = ((f32[32,1,3072]{2,1,0:T(1,128)}), f32[32,1,3072]{2,1,0:T(1,128)S(1)}, u32[]{:S(2)}, u32[]{:S(2)}) async-start(f32[32,1,3072]{2,1,0:T(1,128)} %reshape.545), calls=%async_computation.1 | async-start | bytes 786432 | tf_op jit(solution)/shard_map/all_to_all | solution.py:201
  114.6 8.5 %collective-permute-start.2 = (f32[32,64,24]{1,2,0:T(8,128)S(1)}, f32[32,64,24]{1,2,0:T(8,128)S(1)}, u32[]{:S(2)}, u32[]{:S(2)}) collective-permute-start(f32[32,64,24]{1,2,0:T(8,128)S(1)} %gather_fusion), channel_id=1, source_target_pairs={{0,256},{256,0},{1,257},{257,1},{2,258},{258,2},{3,259},{259,3},{4... | collective-permute-start | bytes 589832 | tf_op jit(solution)/shard_map/ppermute | solution.py:24
  136.1 5.4 %copy-start.2 = (f32[1,4,128,128]{3,2,1,0:T(8,128)S(1)}, f32[1,4,128,128]{3,2,1,0:T(8,128)}, u32[]{:S(2)}) copy-start(f32[1,4,128,128]{3,2,1,0:T(8,128)} %param.9) | copy-start | bytes 786436
  141.5 10.8 %collective-permute-start.3 = (f32[28,3,128]{2,1,0:T(4,128)S(1)}, f32[28,3,128]{2,1,0:T(4,128)S(1)}, u32[]{:S(2)}, u32[]{:S(2)}) collective-permute-start(f32[28,3,128]{2,1,0:T(4,128)S(1)} %get-tuple-element.16), channel_id=1, source_target_pairs={{0,32},{32,64},{64,96},{96,128},{128,160},{160,192},{192,224},{1,3... | collective-permute-start | bytes 129032 | tf_op jit(solution)/shard_map/ppermute | solution.py:34
  150.4 5.5 %collective-permute-start.4 = (f32[28,3,128]{2,1,0:T(4,128)S(1)}, f32[28,3,128]{2,1,0:T(4,128)S(1)}, u32[]{:S(2)}, u32[]{:S(2)}) collective-permute-start(f32[28,3,128]{2,1,0:T(4,128)S(1)} %get-tuple-element.17), channel_id=1, source_target_pairs={{32,0},{64,32},{96,64},{128,96},{160,128},{192,160},{224,192},{33,... | collective-permute-start | bytes 129032 | tf_op jit(solution)/shard_map/ppermute | solution.py:35
  152.4 3.5 %copy-start.6 = (f32[28,3,128]{2,1,0:T(4,128)}, f32[28,3,128]{2,1,0:T(4,128)S(1)}, u32[]{:S(2)}) copy-start(f32[28,3,128]{2,1,0:T(4,128)S(1)} %collective-permute-done.3) | copy-start | bytes 129028
  155.9 0.6 copy-start.8
  162.0 9.1 %collective-permute-start.5 = (f32[28,134,3]{1,0,2:T(8,128)}, f32[28,134,3]{1,0,2:T(8,128)}, u32[]{:S(2)}, u32[]{:S(2)}) collective-permute-start(f32[28,134,3]{1,0,2:T(8,128)} %copy.84), channel_id=1, source_target_pairs={{0,1},{1,2},{2,3},{3,4},{4,5},{5,6},{6,7},{7,8},{8,9},{9,10},{10,1... | collective-permute-start | bytes 135080 | tf_op jit(solution)/shard_map/ppermute | solution.py:34
  169.0 7.2 %collective-permute-start.6 = (f32[28,134,3]{1,0,2:T(8,128)}, f32[28,134,3]{1,0,2:T(8,128)}, u32[]{:S(2)}, u32[]{:S(2)}) collective-permute-start(f32[28,134,3]{1,0,2:T(8,128)} %copy.85), channel_id=1, source_target_pairs={{1,0},{2,1},{3,2},{4,3},{5,4},{6,5},{7,6},{8,7},{9,8},{10,9},{11,1... | collective-permute-start | bytes 135080 | tf_op jit(solution)/shard_map/ppermute | solution.py:35
  184.1 1.5 copy-start
  184.1 1.5 copy-start.3
  184.1 1.5 copy-start.7
  184.2 1.5 copy-start.9
  189.6 0.8 copy-start.10
  189.9 0.8 copy-start.4
  190.4 0.8 copy-start.11
  191.2 36.6 %copy-start.18 = (f32[4]{0:T(128)S(1)}, f32[4]{0:T(128)}, u32[]{:S(2)}) copy-start(f32[4]{0:T(128)} %get-tuple-element.32) | copy-start | bytes 52
  191.2 36.6 %copy-start.19 = (f32[4]{0:T(128)S(1)}, f32[4]{0:T(128)}, u32[]{:S(2)}) copy-start(f32[4]{0:T(128)} %get-tuple-element.33) | copy-start | bytes 52
  191.2 36.6 %copy-start.21 = (f32[4]{0:T(128)S(1)}, f32[4]{0:T(128)}, u32[]{:S(2)}) copy-start(f32[4]{0:T(128)} %iota_multiply_fusion.2) | copy-start | bytes 52
  191.2 36.9 %copy-start.14 = (f32[8]{0:T(128)S(1)}, f32[8]{0:T(128)}, u32[]{:S(2)}) copy-start(f32[8]{0:T(128)} %get-tuple-element.34) | copy-start | bytes 100
  191.2 36.9 %copy-start.15 = (f32[8]{0:T(128)S(1)}, f32[8]{0:T(128)}, u32[]{:S(2)}) copy-start(f32[8]{0:T(128)} %get-tuple-element.35) | copy-start | bytes 100
  191.2 37.2 %copy-start.16 = (f32[32]{0:T(128)S(1)}, f32[32]{0:T(128)}, u32[]{:S(2)}) copy-start(f32[32]{0:T(128)} %get-tuple-element.38) | copy-start | bytes 388
  191.2 37.3 %copy-start.17 = (f32[32]{0:T(128)S(1)}, f32[32]{0:T(128)}, u32[]{:S(2)}) copy-start(f32[32]{0:T(128)} %get-tuple-element.39) | copy-start | bytes 388
  191.2 37.3 %copy-start.20 = (f32[32]{0:T(128)S(1)}, f32[32]{0:T(128)}, u32[]{:S(2)}) copy-start(f32[32]{0:T(128)} %get-tuple-element.37) | copy-start | bytes 388
  191.8 0.8 copy-start.1
  193.6 21.2 %all-to-all-start.2 = ((f32[32,1,4]{2,1,0:T(1,128)}), f32[32,1,4]{2,1,0:T(1,128)S(1)}, u32[]{:S(2)}, u32[]{:S(2)}) async-start(f32[32,1,4]{2,1,0:T(1,128)} %broadcast_in_dim.162), calls=%async_computation.2 | async-start | bytes 32768 | tf_op jit(solution)/shard_map/all_to_all | solution.py:43
  215.6 11.3 %all-to-all-start.3 = ((f32[8,1,128]{2,1,0:T(1,128)}), f32[8,1,128]{2,1,0:T(1,128)S(1)}, u32[]{:S(2)}, u32[]{:S(2)}) async-start(f32[8,1,128]{2,1,0:T(1,128)} %reshape.547), calls=%async_computation.3 | async-start | bytes 8192 | tf_op jit(solution)/shard_map/all_to_all | solution.py:43
  227.7 6.9 %copy-start.5 = (f32[3,4,128,128]{3,2,1,0:T(8,128)S(1)}, f32[3,4,128,128]{3,2,1,0:T(8,128)}, u32[]{:S(2)}) copy-start(f32[3,4,128,128]{3,2,1,0:T(8,128)} %slice.302) | copy-start | bytes 2359300

commit v8 on v7

--- a/solution.py
+++ b/solution.py
@@ -185,20 +185,24 @@
     requests = partner_2(asked, "panel", 0)
     slot_mirror = partner_2(slot_of, "panel", 0)
     requests = lax.all_to_all(requests, "lon", split_axis=0, concat_axis=0, tiled=True)
-    cells_asked = requests[:, :, 0, :].reshape(-1)
-    frac_lat, frac_lon = fractions(requests[:, :, 1, :].reshape(-1))
-    weights = jnp.stack(
-        [
-            (1.0 - frac_lat) * (1.0 - frac_lon),
-            (1.0 - frac_lat) * frac_lon,
-            frac_lat * (1.0 - frac_lon),
-            frac_lat * frac_lon,
-        ],
-        axis=0,
-    )
-    served = corner_blend(flat_cells.T, cells_asked, weights, cols_dev)
-    served = served.reshape(n_lon, capacity, block_cells, channels)
-    served = lax.all_to_all(served, "lon", split_axis=0, concat_axis=0, tiled=True)
+    table = flat_cells.T
+    halves = []
+    for half in range(capacity):
+        cells_asked = requests[:, half, 0, :].reshape(-1)
+        frac_lat, frac_lon = fractions(requests[:, half, 1, :].reshape(-1))
+        weights = jnp.stack(
+            [
+                (1.0 - frac_lat) * (1.0 - frac_lon),
+                (1.0 - frac_lat) * frac_lon,
+                frac_lat * (1.0 - frac_lon),
+                frac_lat * frac_lon,
+            ],
+            axis=0,
+        )
+        blended = corner_blend(table, cells_asked, weights, cols_dev)
+        blended = blended.reshape(n_lon, block_cells, channels)
+        halves.append(lax.all_to_all(blended, "lon", split_axis=0, concat_axis=0, tiled=True))
+    served = jnp.stack(halves, axis=1)
     served = served.reshape(slot_count, block_cells, channels)[slot_mirror]
     values = partner_2(served, "panel", 0)
     values = values.reshape(blocks * block_cells, channels).T.reshape(6, levels, blocks * block_cells)

time: 237 us -> 251 us (1.059)
  starting transfers between devices: 65.2 us -> 78.6 us
  waiting for transfers between devices: 59.6 us -> 50.7 us
  Pallas kernels: 24.8 us -> 28.8 us
  local copies, waits for them, and re-layouts: 53.1 us -> 56.2 us
    all_to_all x1 -> x2, starting transfers between devices: 7.34 us -> 21.3 us  [shards(): lax.all_to_all(blended, 'lon', split_axis=0, concat_axis=0, tiled=True)]
    all_to_all x1 -> x2, waiting for transfers between devices: 22.8 us -> 13.6 us  [shards(): lax.all_to_all(blended, 'lon', split_axis=0, concat_axis=0, tiled=True)]
    pallas_call x1 -> x2, Pallas kernels: 24.8 us -> 28.8 us  [corner_blend(): pl.pallas_call(kernel, out_shape=jax.ShapeDtypeStruct((count, table.shape...]
    unnamed x57 -> x55, local copies, waits for them, and re-layouts: 13.7 us -> 14.4 us
  transfers between devices with their start and end apart: 11 -> 12, of which waited for: 7 -> 7; matrix products, arithmetic and copies ran while one was open for 10% -> 12% of each run, Pallas kernels for 11% -> 12%
where the time goes in v8:
time: 251 us; the launch traced here: 249 us
  starting transfers between devices  78.6 us (31%)
  local copies, waits for them, and re-layouts  56.2 us (22%)
  waiting for transfers between devices  50.7 us (20%)
  other arithmetic  32 us (13%)
  Pallas kernels  28.8 us (11%)
    pallas_call x2, Pallas kernels, corner_blend(): pl.pallas_call(kernel, out_shape=jax.ShapeDtypeStruct((count, table.shape...  28.8 us
    all_to_all x2, starting transfers between devices, shards(): lax.all_to_all(blended, 'lon', split_axis=0, concat_axis=0, tiled=True)  21.3 us
    all_to_all x1, starting transfers between devices, shards(): lax.all_to_all(requests, 'lon', split_axis=0, concat_axis=0, tiled=True)  17.9 us
    all_to_all x2, waiting for transfers between devices, gather_by_exchange(): lax.all_to_all(repeated, axis, split_axis=0, concat_axis=0, tiled=True)  16.9 us
    unnamed x55, local copies, waits for them, and re-layouts  14.4 us
    all_to_all x2, starting transfers between devices, gather_by_exchange(): lax.all_to_all(repeated, axis, split_axis=0, concat_axis=0, tiled=True)  14 us
    ppermute x2, starting transfers between devices, padded_2(): before = lax.ppermute(last, axis, up)  14 us
    all_to_all x2, waiting for transfers between devices, shards(): lax.all_to_all(blended, 'lon', split_axis=0, concat_axis=0, tiled=True)  13.6 us
  transfers between devices with their start and end apart: 12, of which 7 were waited for; matrix products, arithmetic and copies ran while one was open for 12% of the time, Pallas kernels for 12%

profile of v8, /device:TPU:1, one launch (start us, length us, event | category | flops | bytes accessed | tf_op | source)
XLA Modules:
  0.0 249.2 jit_solution(2877963828047008232)
XLA Ops:
  1.4 0.8 select_reduce_fusion
  3.4 1.4 reduce.33
  4.9 0.7 add_reduce_fusion
  7.1 3.9 %collective-permute-start = (s32[32,2,2,64]{3,1,0,2:T(2,128)S(1)}, s32[32,2,2,64]{3,1,0,2:T(2,128)S(1)}, u32[]{:S(2)}, u32[]{:S(2)}) collective-permute-start(s32[32,2,2,64]{3,1,0,2:T(2,128)S(1)} %pad_add_fusion), channel_id=1, source_target_pairs={{0,256},{256,0},{1,257},{257,1},{2,258},{258,2},{3,259},{259,3},{4... | collective-permute-start | bytes 98312 | tf_op jit(solution)/shard_map/ppermute | solution.py:24
  11.7 1.9 collective-permute-start.1
  15.5 0.9 fusion.108
  19.8 17.9 %all-to-all-start = ((s32[32,1,256]{2,1,0:T(1,128)}), s32[32,1,256]{2,1,0:T(1,128)S(1)}, u32[]{:S(2)}, u32[]{:S(2)}) async-start(s32[32,1,256]{2,1,0:T(1,128)} %reshape.746), calls=%async_computation | async-start | bytes 65536 | tf_op jit(solution)/shard_map/all_to_all | solution.py:187
  37.8 2.3 copy.90
  40.1 4.6 %copy.62 = f32[24,16384]{0,1:T(8,128)} copy(f32[24,16384]{1,0:T(8,128)S(1)} %bitcast.143) | data formatting | bytes 3145728 | tf_op jit(solution)/shard_map/reshape;squeeze | solution.py:172
  44.8 6.7 %all-to-all-done = s32[32,1,256]{2,1,0:T(1,128)S(1)} async-done(((s32[32,1,256]{2,1,0:T(1,128)}), s32[32,1,256]{2,1,0:T(1,128)S(1)}, u32[]{:S(2)}, u32[]{:S(2)}) %all-to-all-start) | async-done | bytes 32800 | tf_op jit(solution)/shard_map/all_to_all | solution.py:187
  54.5 14.4 %shard_map.95 = f32[2048,24]{1,0:T(8,128)} custom-call(s32[2048]{0:T(1024)} %reshape_squeeze.20.rows_ref, f32[4,2048]{1,0:T(4,128)} %pad_maximum_fusion.7.weights_ref, f32[16384,24]{1,0:T(8,128)} %bitcast.137), custom_call_target="tpu_custom_call" | custom-call | tf_op jit(solution)/shard_map/pallas_call | solution.py:61
  68.9 1.5 copy.59
  70.5 0.9 reshape.750
  71.4 7.3 %all-to-all-start.1 = ((f32[32,1,1536]{2,1,0:T(1,128)}), f32[32,1,1536]{2,1,0:T(1,128)S(1)}, u32[]{:S(2)}, u32[]{:S(2)}) async-start(f32[32,1,1536]{2,1,0:T(1,128)} %reshape.750), calls=%async_computation.1 | async-start | bytes 393216 | tf_op jit(solution)/shard_map/all_to_all | solution.py:204
  80.2 14.4 %shard_map.96 = f32[2048,24]{1,0:T(8,128)} custom-call(s32[2048]{0:T(1024)} %reshape_squeeze.22.rows_ref, f32[4,2048]{1,0:T(4,128)} %pad_maximum_fusion.8.weights_ref, f32[16384,24]{1,0:T(8,128)} %bitcast.138), custom_call_target="tpu_custom_call" | custom-call | tf_op jit(solution)/shard_map/pallas_call | solution.py:61
  94.6 1.5 copy.60
  96.2 0.9 reshape.748
  97.1 14.0 %all-to-all-start.2 = ((f32[32,1,1536]{2,1,0:T(1,128)}), f32[32,1,1536]{2,1,0:T(1,128)S(1)}, u32[]{:S(2)}, u32[]{:S(2)}) async-start(f32[32,1,1536]{2,1,0:T(1,128)} %reshape.748), calls=%async_computation.2 | async-start | bytes 393216 | tf_op jit(solution)/shard_map/all_to_all | solution.py:204
  111.8 1.1 reduce.36
  113.0 13.6 %all-to-all-done.2 = f32[32,1,1536]{2,1,0:T(1,128)S(1)} async-done(((f32[32,1,1536]{2,1,0:T(1,128)}), f32[32,1,1536]{2,1,0:T(1,128)S(1)}, u32[]{:S(2)}, u32[]{:S(2)}) %all-to-all-start.2) | async-done | bytes 196640 | tf_op jit(solution)/shard_map/all_to_all | solution.py:204
  126.6 1.1 reduce.35
  128.5 2.2 collective-permute-start.2
  130.8 6.2 %collective-permute-done.2 = f32[32,64,24]{1,2,0:T(8,128)S(1)} collective-permute-done((f32[32,64,24]{1,2,0:T(8,128)S(1)}, f32[32,64,24]{1,2,0:T(8,128)S(1)}, u32[]{:S(2)}, u32[]{:S(2)}) %collective-permute-start.2) | collective-permute-done | bytes 196640 | tf_op jit(solution)/shard_map/ppermute | solution.py:24
  137.8 12.1 %scatter_fusion = f32[24,16384]{0,1:T(8,128)} fusion(f32[24,16384]{0,1:T(8,128)} %copy.62, s32[2048]{0:T(1024)S(1)} %bitcast.173, f32[2048,24]{1,0:T(8,128)S(1)} %copy.63), kind=kCustom, calls=%fused_computation.3 | custom fusion | bytes 598016 | tf_op jit(solution)/shard_map/scatter | solution.py:223
  150.0 5.4 %copy.64 = f32[24,128,128]{2,1,0:T(8,128)S(1)} copy(f32[24,128,128]{0,2,1:T(8,128)} %bitcast.139) | data formatting | bytes 3145728 | tf_op jit(solution)/shard_map/reshape;reshape | solution.py:240
  155.4 9.5 %collective-permute-start.3 = (f32[28,3,128]{2,1,0:T(4,128)S(1)}, f32[28,3,128]{2,1,0:T(4,128)S(1)}, u32[]{:S(2)}, u32[]{:S(2)}) collective-permute-start(f32[28,3,128]{2,1,0:T(4,128)S(1)} %get-tuple-element.23), channel_id=1, source_target_pairs={{0,32},{32,64},{64,96},{96,128},{128,160},{160,192},{192,224},{1,3... | collective-permute-start | bytes 129032 | tf_op jit(solution)/shard_map/ppermute | solution.py:34
  164.9 1.9 collective-permute-start.4
  166.9 3.5 %collective-permute-done.4 = f32[28,3,128]{2,1,0:T(4,128)S(1)} collective-permute-done((f32[28,3,128]{2,1,0:T(4,128)S(1)}, f32[28,3,128]{2,1,0:T(4,128)S(1)}, u32[]{:S(2)}, u32[]{:S(2)}) %collective-permute-start.4) | collective-permute-done | bytes 43040 | tf_op jit(solution)/shard_map/ppermute | solution.py:35
  171.2 1.9 fusion.107
  173.1 3.4 %copy.79 = f32[28,134,3]{1,0,2:T(8,128)} copy(f32[28,134,3]{2,1,0:T(8,128)} %get-tuple-element.21) | data formatting | bytes 90048
  176.5 4.5 %collective-permute-start.5 = (f32[28,134,3]{1,0,2:T(8,128)}, f32[28,134,3]{1,0,2:T(8,128)}, u32[]{:S(2)}, u32[]{:S(2)}) collective-permute-start(f32[28,134,3]{1,0,2:T(8,128)} %copy.79), channel_id=1, source_target_pairs={{0,1},{1,2},{2,3},{3,4},{4,5},{5,6},{6,7},{7,8},{8,9},{9,10},{10,1... | collective-permute-start | bytes 135080 | tf_op jit(solution)/shard_map/ppermute | solution.py:34
  181.0 1.8 copy.80
  182.8 1.3 collective-permute-start.6
  184.6 1.6 copy.67
  186.2 3.8 %collective-permute-done.6 = f32[28,134,3]{1,0,2:T(8,128)} collective-permute-done((f32[28,134,3]{1,0,2:T(8,128)}, f32[28,134,3]{1,0,2:T(8,128)}, u32[]{:S(2)}, u32[]{:S(2)}) %collective-permute-start.6) | collective-permute-done | bytes 45056 | tf_op jit(solution)/shard_map/ppermute | solution.py:35
  190.0 2.8 %copy.68 = f32[28,134,3]{2,1,0:T(8,128)} copy(f32[28,134,3]{1,0,2:T(8,128)} %collective-permute-done.6) | data formatting | bytes 90048 | tf_op jit(solution)/shard_map/ppermute | solution.py:35
  192.8 4.8 %pad_maximum_fusion = f32[28,134,134]{2,1,0:T(8,128)S(1)} fusion(f32[28,134,3]{2,1,0:T(8,128)} %copy.68, f32[28,3,128]{2,1,0:T(4,128)} %copy-done.8, f32[4,128,128]{2,1,0:T(8,128)} %bitcast.147, f32[24,128,128]{2,1,0:T(8,128)S(1)} %copy.64, f32[28,3,128]{2,1,0:T(4,128)} %copy-done.6, f32[28,134,3]{2,1,0:T(8,128)S(1)} %copy.67), kind=kLoop, calls=%fused_computation.6 | loop fusion | flops 2513840 | bytes 4022144 | tf_op jit(solution)/shard_map/concatenate | solution.py:36
  197.9 0.9 slice.285
  199.8 3.6 %fusion.4 = f32[6,4,132,132]{3,2,1,0:T(8,128)S(1)} fusion(f32[6,4,132,132]{3,2,1,0:T(8,128)S(1)} %slice.285, f32[6,4,134,134]{3,2,1,0:T(8,128)S(1)} %bitcast.141, f32[132]{0:T(256)S(1)} %divide_multiply_fusion, f32[4,132,132]{2,1,0:T(8,128)S(1)} %pad_maximum_fusion.4), kind=kLoop, calls=%fused_computation.11 | loop fusion | flops 5018112 | bytes 10315536 | tf_op jit(solution)/shard_map/add | solution.py:247
  207.4 7.2 %all-to-all-start.3 = ((f32[32,1,4]{2,1,0:T(1,128)}), f32[32,1,4]{2,1,0:T(1,128)S(1)}, u32[]{:S(2)}, u32[]{:S(2)}) async-start(f32[32,1,4]{2,1,0:T(1,128)} %broadcast_in_dim.162), calls=%async_computation.3 | async-start | bytes 32768 | tf_op jit(solution)/shard_map/all_to_all | solution.py:43
  214.7 13.6 %all-to-all-done.3 = f32[32,1,4]{2,1,0:T(1,128)S(1)} async-done(((f32[32,1,4]{2,1,0:T(1,128)}), f32[32,1,4]{2,1,0:T(1,128)S(1)}, u32[]{:S(2)}, u32[]{:S(2)}) %all-to-all-start.3) | async-done | bytes 544 | tf_op jit(solution)/shard_map/all_to_all | solution.py:43
  229.0 6.8 %all-to-all-start.4 = ((f32[8,1,128]{2,1,0:T(1,128)}), f32[8,1,128]{2,1,0:T(1,128)S(1)}, u32[]{:S(2)}, u32[]{:S(2)}) async-start(f32[8,1,128]{2,1,0:T(1,128)} %reshape.752), calls=%async_computation.4 | async-start | bytes 8192 | tf_op jit(solution)/shard_map/all_to_all | solution.py:43
  235.9 1.2 slice.312
  237.1 3.3 %all-to-all-done.4 = f32[8,1,128]{2,1,0:T(1,128)S(1)} async-done(((f32[8,1,128]{2,1,0:T(1,128)}), f32[8,1,128]{2,1,0:T(1,128)S(1)}, u32[]{:S(2)}, u32[]{:S(2)}) %all-to-all-start.4) | async-done | bytes 4128 | tf_op jit(solution)/shard_map/all_to_all | solution.py:43
  243.2 1.9 add_bitcast_fusion
  245.1 1.2 select_add_fusion
  246.8 1.2 fusion.25
  248.0 1.2 maximum_bitcast_fusion
  (135 shorter events, 26.9 us)
Async XLA Ops:
  7.1 12.0 %collective-permute-start = (s32[32,2,2,64]{3,1,0,2:T(2,128)S(1)}, s32[32,2,2,64]{3,1,0,2:T(2,128)S(1)}, u32[]{:S(2)}, u32[]{:S(2)}) collective-permute-start(s32[32,2,2,64]{3,1,0,2:T(2,128)S(1)} %pad_add_fusion), channel_id=1, source_target_pairs={{0,256},{256,0},{1,257},{257,1},{2,258},{258,2},{3,259},{259,3},{4... | collective-permute-start | bytes 98312 | tf_op jit(solution)/shard_map/ppermute | solution.py:24
  11.7 99.5 %collective-permute-start.1 = (s32[32]{0:T(128)S(1)}, s32[32]{0:T(128)S(1)}, u32[]{:S(2)}, u32[]{:S(2)}) collective-permute-start(s32[32]{0:T(128)S(1)} %multiply_add_fusion.1), channel_id=1, source_target_pairs={{0,256},{256,0},{1,257},{257,1},{2,258},{258,2},{3,259},{259,3},{4... | collective-permute-start | bytes 392 | tf_op jit(solution)/shard_map/ppermute | solution.py:24
  19.8 31.7 %all-to-all-start = ((s32[32,1,256]{2,1,0:T(1,128)}), s32[32,1,256]{2,1,0:T(1,128)S(1)}, u32[]{:S(2)}, u32[]{:S(2)}) async-start(s32[32,1,256]{2,1,0:T(1,128)} %reshape.746), calls=%async_computation | async-start | bytes 65536 | tf_op jit(solution)/shard_map/all_to_all | solution.py:187
  71.4 25.7 %all-to-all-start.1 = ((f32[32,1,1536]{2,1,0:T(1,128)}), f32[32,1,1536]{2,1,0:T(1,128)S(1)}, u32[]{:S(2)}, u32[]{:S(2)}) async-start(f32[32,1,1536]{2,1,0:T(1,128)} %reshape.750), calls=%async_computation.1 | async-start | bytes 393216 | tf_op jit(solution)/shard_map/all_to_all | solution.py:204
  97.1 29.5 %all-to-all-start.2 = ((f32[32,1,1536]{2,1,0:T(1,128)}), f32[32,1,1536]{2,1,0:T(1,128)S(1)}, u32[]{:S(2)}, u32[]{:S(2)}) async-start(f32[32,1,1536]{2,1,0:T(1,128)} %reshape.748), calls=%async_computation.2 | async-start | bytes 393216 | tf_op jit(solution)/shard_map/all_to_all | solution.py:204
  128.5 8.5 %collective-permute-start.2 = (f32[32,64,24]{1,2,0:T(8,128)S(1)}, f32[32,64,24]{1,2,0:T(8,128)S(1)}, u32[]{:S(2)}, u32[]{:S(2)}) collective-permute-start(f32[32,64,24]{1,2,0:T(8,128)S(1)} %gather_fusion), channel_id=1, source_target_pairs={{0,256},{256,0},{1,257},{257,1},{2,258},{258,2},{3,259},{259,3},{4... | collective-permute-start | bytes 589832 | tf_op jit(solution)/shard_map/ppermute | solution.py:24
  150.0 5.4 %copy-start.2 = (f32[1,4,128,128]{3,2,1,0:T(8,128)S(1)}, f32[1,4,128,128]{3,2,1,0:T(8,128)}, u32[]{:S(2)}) copy-start(f32[1,4,128,128]{3,2,1,0:T(8,128)} %param.9) | copy-start | bytes 786436
  155.4 11.5 %collective-permute-start.3 = (f32[28,3,128]{2,1,0:T(4,128)S(1)}, f32[28,3,128]{2,1,0:T(4,128)S(1)}, u32[]{:S(2)}, u32[]{:S(2)}) collective-permute-start(f32[28,3,128]{2,1,0:T(4,128)S(1)} %get-tuple-element.23), channel_id=1, source_target_pairs={{0,32},{32,64},{64,96},{96,128},{128,160},{160,192},{192,224},{1,3... | collective-permute-start | bytes 129032 | tf_op jit(solution)/shard_map/ppermute | solution.py:34
  164.9 5.5 %collective-permute-start.4 = (f32[28,3,128]{2,1,0:T(4,128)S(1)}, f32[28,3,128]{2,1,0:T(4,128)S(1)}, u32[]{:S(2)}, u32[]{:S(2)}) collective-permute-start(f32[28,3,128]{2,1,0:T(4,128)S(1)} %get-tuple-element.24), channel_id=1, source_target_pairs={{32,0},{64,32},{96,64},{128,96},{160,128},{192,160},{224,192},{33,... | collective-permute-start | bytes 129032 | tf_op jit(solution)/shard_map/ppermute | solution.py:35
  166.9 3.5 %copy-start.6 = (f32[28,3,128]{2,1,0:T(4,128)}, f32[28,3,128]{2,1,0:T(4,128)S(1)}, u32[]{:S(2)}) copy-start(f32[28,3,128]{2,1,0:T(4,128)S(1)} %collective-permute-done.3) | copy-start | bytes 129028
  170.4 0.6 copy-start.8
  176.5 8.2 %collective-permute-start.5 = (f32[28,134,3]{1,0,2:T(8,128)}, f32[28,134,3]{1,0,2:T(8,128)}, u32[]{:S(2)}, u32[]{:S(2)}) collective-permute-start(f32[28,134,3]{1,0,2:T(8,128)} %copy.79), channel_id=1, source_target_pairs={{0,1},{1,2},{2,3},{3,4},{4,5},{5,6},{6,7},{7,8},{8,9},{9,10},{10,1... | collective-permute-start | bytes 135080 | tf_op jit(solution)/shard_map/ppermute | solution.py:34
  182.8 7.2 %collective-permute-start.6 = (f32[28,134,3]{1,0,2:T(8,128)}, f32[28,134,3]{1,0,2:T(8,128)}, u32[]{:S(2)}, u32[]{:S(2)}) collective-permute-start(f32[28,134,3]{1,0,2:T(8,128)} %copy.80), channel_id=1, source_target_pairs={{1,0},{2,1},{3,2},{4,3},{5,4},{6,5},{7,6},{8,7},{9,8},{10,9},{11,1... | collective-permute-start | bytes 135080 | tf_op jit(solution)/shard_map/ppermute | solution.py:35
  197.9 1.5 copy-start
  197.9 1.5 copy-start.3
  197.9 1.5 copy-start.7
  197.9 1.5 copy-start.9
  203.4 0.8 copy-start.10
  203.6 0.8 copy-start.4
  204.2 0.8 copy-start.11
  204.9 36.2 %copy-start.14 = (f32[4]{0:T(128)S(1)}, f32[4]{0:T(128)}, u32[]{:S(2)}) copy-start(f32[4]{0:T(128)} %get-tuple-element.40) | copy-start | bytes 52
  204.9 36.2 %copy-start.15 = (f32[4]{0:T(128)S(1)}, f32[4]{0:T(128)}, u32[]{:S(2)}) copy-start(f32[4]{0:T(128)} %get-tuple-element.41) | copy-start | bytes 52
  204.9 36.2 %copy-start.19 = (f32[4]{0:T(128)S(1)}, f32[4]{0:T(128)}, u32[]{:S(2)}) copy-start(f32[4]{0:T(128)} %iota_multiply_fusion.2) | copy-start | bytes 52
  204.9 36.5 %copy-start.12 = (f32[8]{0:T(128)S(1)}, f32[8]{0:T(128)}, u32[]{:S(2)}) copy-start(f32[8]{0:T(128)} %get-tuple-element.42) | copy-start | bytes 100
  204.9 36.5 %copy-start.13 = (f32[8]{0:T(128)S(1)}, f32[8]{0:T(128)}, u32[]{:S(2)}) copy-start(f32[8]{0:T(128)} %get-tuple-element.43) | copy-start | bytes 100
  204.9 36.8 %copy-start.16 = (f32[32]{0:T(128)S(1)}, f32[32]{0:T(128)}, u32[]{:S(2)}) copy-start(f32[32]{0:T(128)} %get-tuple-element.45) | copy-start | bytes 388
  205.0 36.8 %copy-start.17 = (f32[32]{0:T(128)S(1)}, f32[32]{0:T(128)}, u32[]{:S(2)}) copy-start(f32[32]{0:T(128)} %get-tuple-element.46) | copy-start | bytes 388
  205.0 36.8 %copy-start.18 = (f32[32]{0:T(128)S(1)}, f32[32]{0:T(128)}, u32[]{:S(2)}) copy-start(f32[32]{0:T(128)} %get-tuple-element.47) | copy-start | bytes 388
  205.5 0.8 copy-start.1
  207.4 20.9 %all-to-all-start.3 = ((f32[32,1,4]{2,1,0:T(1,128)}), f32[32,1,4]{2,1,0:T(1,128)S(1)}, u32[]{:S(2)}, u32[]{:S(2)}) async-start(f32[32,1,4]{2,1,0:T(1,128)} %broadcast_in_dim.162), calls=%async_computation.3 | async-start | bytes 32768 | tf_op jit(solution)/shard_map/all_to_all | solution.py:43
  229.0 11.3 %all-to-all-start.4 = ((f32[8,1,128]{2,1,0:T(1,128)}), f32[8,1,128]{2,1,0:T(1,128)S(1)}, u32[]{:S(2)}, u32[]{:S(2)}) async-start(f32[8,1,128]{2,1,0:T(1,128)} %reshape.752), calls=%async_computation.4 | async-start | bytes 8192 | tf_op jit(solution)/shard_map/all_to_all | solution.py:43
  241.1 6.9 %copy-start.5 = (f32[3,4,128,128]{3,2,1,0:T(8,128)S(1)}, f32[3,4,128,128]{3,2,1,0:T(8,128)}, u32[]{:S(2)}) copy-start(f32[3,4,128,128]{3,2,1,0:T(8,128)} %slice.312) | copy-start | bytes 2359300

commit v9 on v7

--- a/solution.py
+++ b/solution.py
@@ -182,9 +182,15 @@
     asked = jnp.stack(
         [empty.at[slot_of].set(base_cell), empty.at[slot_of].set(weight_ids)], axis=1
     ).reshape(n_lon, capacity, 2, block_cells)
-    requests = partner_2(asked, "panel", 0)
+    panel_pos = lax.axis_index("panel")
+    panel_count = lax.axis_size("panel")
+    mine = jnp.arange(panel_count, dtype=jnp.int32) != panel_pos
+    routed = jnp.where(mine[:, None, None, None, None], asked[None], 0)
+    routed = routed.reshape((panel_count * n_lon,) + asked.shape[1:])
     slot_mirror = partner_2(slot_of, "panel", 0)
-    requests = lax.all_to_all(requests, "lon", split_axis=0, concat_axis=0, tiled=True)
+    routed = lax.all_to_all(routed, ("panel", "lon"), split_axis=0, concat_axis=0, tiled=True)
+    routed = routed.reshape((panel_count, n_lon) + asked.shape[1:])
+    requests = jnp.sum(jnp.where(mine[:, None, None, None, None], routed, 0), axis=0)
     cells_asked = requests[:, :, 0, :].reshape(-1)
     frac_lat, frac_lon = fractions(requests[:, :, 1, :].reshape(-1))
     weights = jnp.stack(

time: 237 us -> 235 us (level)
  waiting for transfers between devices: 59.6 us -> 55.9 us
    all_to_all x1, waiting for transfers between devices: 6.69 us -> 0.16 us  [shards(): lax.all_to_all(routed, ('panel', 'lon'), split_axis=0, concat_axis=0, til...]
    all_to_all x1, starting transfers between devices: 7.34 us -> 13.6 us  [shards(): lax.all_to_all(served, 'lon', split_axis=0, concat_axis=0, tiled=True)]
    ppermute x3 -> x2, starting transfers between devices: 8.08 us -> 4.93 us  [partner_2(): return lax.ppermute(block, axis, route)]
    ppermute x3 -> x2, waiting for transfers between devices: 6.23 us -> 7.37 us  [partner_2(): return lax.ppermute(block, axis, route)]
  transfers between devices with their start and end apart: 11 -> 10, of which waited for: 7 -> 7; matrix products, arithmetic and copies ran while one was open for 10% -> 10% of each run, Pallas kernels for 11% -> 11%
where the time goes in v9:
time: 235 us; the launch traced here: 234 us
  starting transfers between devices  66.8 us (28%)
  waiting for transfers between devices  55.9 us (24%)
  local copies, waits for them, and re-layouts  53.4 us (23%)
  other arithmetic  30.3 us (13%)
  Pallas kernels  24.8 us (11%)
    pallas_call x1, Pallas kernels, corner_blend(): pl.pallas_call(kernel, out_shape=jax.ShapeDtypeStruct((count, table.shape...  24.8 us
    all_to_all x1, waiting for transfers between devices, shards(): lax.all_to_all(served, 'lon', split_axis=0, concat_axis=0, tiled=True)  24.2 us
    all_to_all x1, starting transfers between devices, shards(): lax.all_to_all(routed, ('panel', 'lon'), split_axis=0, concat_axis=0, til...  19.1 us
    all_to_all x2, waiting for transfers between devices, gather_by_exchange(): lax.all_to_all(repeated, axis, split_axis=0, concat_axis=0, tiled=True)  16.9 us
    all_to_all x2, starting transfers between devices, gather_by_exchange(): lax.all_to_all(repeated, axis, split_axis=0, concat_axis=0, tiled=True)  14.2 us
    unnamed x57, local copies, waits for them, and re-layouts  13.8 us
    all_to_all x1, starting transfers between devices, shards(): lax.all_to_all(served, 'lon', split_axis=0, concat_axis=0, tiled=True)  13.6 us
    scatter x1, local copies, waits for them, and re-layouts, shards(): flat_cells.at[:, dest_cell[0, 0]].set(rotated)  12.2 us
  transfers between devices with their start and end apart: 10, of which 7 were waited for; matrix products, arithmetic and copies ran while one was open for 10% of the time, Pallas kernels for 11%

profile of v9, /device:TPU:1, one launch (start us, length us, event | category | flops | bytes accessed | tf_op | source)
XLA Modules:
  0.0 234.2 jit_solution(18223130685171084507)
XLA Ops:
  0.6 0.7 fusion.49
  1.4 0.8 select_reduce_fusion.1
  3.4 1.4 reduce.17
  4.9 0.7 add_reduce_fusion
  7.5 0.8 reshape.553
  8.3 19.1 %all-to-all-start = ((s32[64,1,256]{2,1,0:T(1,128)}), s32[64,1,256]{2,1,0:T(1,128)S(1)}, u32[]{:S(2)}, u32[]{:S(2)}) async-start(s32[64,1,256]{2,1,0:T(1,128)} %reshape.553), calls=%async_computation | async-start | bytes 131072 | tf_op jit(solution)/shard_map/all_to_all | solution.py:191
  28.1 3.0 %collective-permute-start = (s32[32]{0:T(128)S(1)}, s32[32]{0:T(128)S(1)}, u32[]{:S(2)}, u32[]{:S(2)}) collective-permute-start(s32[32]{0:T(128)S(1)} %multiply_add_fusion.1), channel_id=1, source_target_pairs={{0,256},{256,0},{1,257},{257,1},{2,258},{258,2},{3,259},{259,3},{4... | collective-permute-start | bytes 392 | tf_op jit(solution)/shard_map/ppermute | solution.py:24
  33.4 2.3 copy.174
  35.8 4.6 %copy.144 = f32[24,16384]{0,1:T(8,128)} copy(f32[24,16384]{1,0:T(8,128)S(1)} %bitcast.139) | data formatting | bytes 3145728 | tf_op jit(solution)/shard_map/reshape;squeeze | solution.py:172
  40.4 0.7 broadcast_and_fusion
  41.8 0.8 reduce.18
  43.2 0.7 reshape_squeeze.14.rows_ref
  43.9 0.7 pad_maximum_fusion.4.weights_ref
  44.6 24.8 %shard_map.95 = f32[4096,24]{1,0:T(8,128)} custom-call(s32[4096]{0:T(1024)} %reshape_squeeze.14.rows_ref, f32[4,4096]{1,0:T(4,128)} %pad_maximum_fusion.4.weights_ref, f32[16384,24]{1,0:T(8,128)} %bitcast.136), custom_call_target="tpu_custom_call" | custom-call | tf_op jit(solution)/shard_map/pallas_call | solution.py:61
  69.4 2.2 copy.142
  71.6 1.2 reshape.555
  72.9 13.6 %all-to-all-start.1 = ((f32[32,1,3072]{2,1,0:T(1,128)}), f32[32,1,3072]{2,1,0:T(1,128)S(1)}, u32[]{:S(2)}, u32[]{:S(2)}) async-start(f32[32,1,3072]{2,1,0:T(1,128)} %reshape.555), calls=%async_computation.1 | async-start | bytes 786432 | tf_op jit(solution)/shard_map/all_to_all | solution.py:207
  86.5 0.7 broadcast_and_fusion.1
  87.6 24.2 %all-to-all-done.1 = f32[32,1,3072]{2,1,0:T(1,128)S(1)} async-done(((f32[32,1,3072]{2,1,0:T(1,128)}), f32[32,1,3072]{2,1,0:T(1,128)S(1)}, u32[]{:S(2)}, u32[]{:S(2)}) %all-to-all-start.1) | async-done | bytes 393248 | tf_op jit(solution)/shard_map/all_to_all | solution.py:207
  112.3 1.6 reduce.19
  114.7 1.9 collective-permute-start.1
  116.7 7.4 %collective-permute-done.1 = f32[32,64,24]{1,2,0:T(8,128)S(1)} collective-permute-done((f32[32,64,24]{1,2,0:T(8,128)S(1)}, f32[32,64,24]{1,2,0:T(8,128)S(1)}, u32[]{:S(2)}, u32[]{:S(2)}) %collective-permute-start.1) | collective-permute-done | bytes 196640 | tf_op jit(solution)/shard_map/ppermute | solution.py:24
  124.9 12.2 %scatter_fusion = f32[24,16384]{0,1:T(8,128)} fusion(f32[24,16384]{0,1:T(8,128)} %copy.144, s32[2048]{0:T(1024)S(1)} %bitcast.165, f32[2048,24]{1,0:T(8,128)S(1)} %copy.145), kind=kCustom, calls=%fused_computation.3 | custom fusion | bytes 598016 | tf_op jit(solution)/shard_map/scatter | solution.py:225
  137.0 5.4 %copy.146 = f32[24,128,128]{2,1,0:T(8,128)S(1)} copy(f32[24,128,128]{0,2,1:T(8,128)} %bitcast.137) | data formatting | bytes 3145728 | tf_op jit(solution)/shard_map/reshape;reshape | solution.py:242
  142.5 7.1 %collective-permute-start.2 = (f32[28,3,128]{2,1,0:T(4,128)S(1)}, f32[28,3,128]{2,1,0:T(4,128)S(1)}, u32[]{:S(2)}, u32[]{:S(2)}) collective-permute-start(f32[28,3,128]{2,1,0:T(4,128)S(1)} %get-tuple-element.16), channel_id=1, source_target_pairs={{0,32},{32,64},{64,96},{96,128},{128,160},{160,192},{192,224},{1,3... | collective-permute-start | bytes 129032 | tf_op jit(solution)/shard_map/ppermute | solution.py:34
  149.6 1.9 collective-permute-start.3
  151.6 3.5 %collective-permute-done.3 = f32[28,3,128]{2,1,0:T(4,128)S(1)} collective-permute-done((f32[28,3,128]{2,1,0:T(4,128)S(1)}, f32[28,3,128]{2,1,0:T(4,128)S(1)}, u32[]{:S(2)}, u32[]{:S(2)}) %collective-permute-start.3) | collective-permute-done | bytes 43040 | tf_op jit(solution)/shard_map/ppermute | solution.py:35
  155.9 1.9 fusion.103
  157.8 3.4 %copy.164 = f32[28,134,3]{1,0,2:T(8,128)} copy(f32[28,134,3]{2,1,0:T(8,128)} %get-tuple-element.14) | data formatting | bytes 90048
  161.2 4.6 %collective-permute-start.4 = (f32[28,134,3]{1,0,2:T(8,128)}, f32[28,134,3]{1,0,2:T(8,128)}, u32[]{:S(2)}, u32[]{:S(2)}) collective-permute-start(f32[28,134,3]{1,0,2:T(8,128)} %copy.164), channel_id=1, source_target_pairs={{0,1},{1,2},{2,3},{3,4},{4,5},{5,6},{6,7},{7,8},{8,9},{9,10},{10,1... | collective-permute-start | bytes 135080 | tf_op jit(solution)/shard_map/ppermute | solution.py:34
  165.8 1.8 copy.165
  167.7 1.3 collective-permute-start.5
  169.5 1.6 copy.149
  171.1 3.7 %collective-permute-done.5 = f32[28,134,3]{1,0,2:T(8,128)} collective-permute-done((f32[28,134,3]{1,0,2:T(8,128)}, f32[28,134,3]{1,0,2:T(8,128)}, u32[]{:S(2)}, u32[]{:S(2)}) %collective-permute-start.5) | collective-permute-done | bytes 45056 | tf_op jit(solution)/shard_map/ppermute | solution.py:35
  174.8 2.9 %copy.150 = f32[28,134,3]{2,1,0:T(8,128)} copy(f32[28,134,3]{1,0,2:T(8,128)} %collective-permute-done.5) | data formatting | bytes 90048 | tf_op jit(solution)/shard_map/ppermute | solution.py:35
  177.7 4.8 %pad_maximum_fusion = f32[28,134,134]{2,1,0:T(8,128)S(1)} fusion(f32[28,134,3]{2,1,0:T(8,128)} %copy.150, f32[28,3,128]{2,1,0:T(4,128)} %copy-done.8, f32[4,128,128]{2,1,0:T(8,128)} %bitcast.141, f32[24,128,128]{2,1,0:T(8,128)S(1)} %copy.146, f32[28,3,128]{2,1,0:T(4,128)} %copy-done.6, f32[28,134,3]{2,1,0:T(8,128)S(1)} %copy.149), kind=kLoop, calls=%fused_computation.6 | loop fusion | flops 2513840 | bytes 4022144 | tf_op jit(solution)/shard_map/concatenate | solution.py:36
  182.8 0.9 slice.275
  184.6 3.6 %fusion.4 = f32[6,4,132,132]{3,2,1,0:T(8,128)S(1)} fusion(f32[6,4,132,132]{3,2,1,0:T(8,128)S(1)} %slice.275, f32[6,4,134,134]{3,2,1,0:T(8,128)S(1)} %bitcast.134, f32[132]{0:T(256)S(1)} %divide_multiply_fusion, f32[4,132,132]{2,1,0:T(8,128)S(1)} %pad_maximum_fusion.3), kind=kLoop, calls=%fused_computation.11 | loop fusion | flops 5018112 | bytes 10315536 | tf_op jit(solution)/shard_map/add | solution.py:249
  192.2 7.3 %all-to-all-start.2 = ((f32[32,1,4]{2,1,0:T(1,128)}), f32[32,1,4]{2,1,0:T(1,128)S(1)}, u32[]{:S(2)}, u32[]{:S(2)}) async-start(f32[32,1,4]{2,1,0:T(1,128)} %broadcast_in_dim.213), calls=%async_computation.2 | async-start | bytes 32768 | tf_op jit(solution)/shard_map/all_to_all | solution.py:43
  199.6 13.6 %all-to-all-done.2 = f32[32,1,4]{2,1,0:T(1,128)S(1)} async-done(((f32[32,1,4]{2,1,0:T(1,128)}), f32[32,1,4]{2,1,0:T(1,128)S(1)}, u32[]{:S(2)}, u32[]{:S(2)}) %all-to-all-start.2) | async-done | bytes 544 | tf_op jit(solution)/shard_map/all_to_all | solution.py:43
  213.3 0.7 reshape.557
  214.0 6.8 %all-to-all-start.3 = ((f32[8,1,128]{2,1,0:T(1,128)}), f32[8,1,128]{2,1,0:T(1,128)S(1)}, u32[]{:S(2)}, u32[]{:S(2)}) async-start(f32[8,1,128]{2,1,0:T(1,128)} %reshape.557), calls=%async_computation.3 | async-start | bytes 8192 | tf_op jit(solution)/shard_map/all_to_all | solution.py:43
  220.8 1.2 slice.302
  222.0 3.3 %all-to-all-done.3 = f32[8,1,128]{2,1,0:T(1,128)S(1)} async-done(((f32[8,1,128]{2,1,0:T(1,128)}), f32[8,1,128]{2,1,0:T(1,128)S(1)}, u32[]{:S(2)}, u32[]{:S(2)}) %all-to-all-start.3) | async-done | bytes 4128 | tf_op jit(solution)/shard_map/all_to_all | solution.py:43
  228.1 1.9 add_bitcast_fusion
  230.0 1.2 select_add_fusion
  231.7 1.2 fusion.25
  232.9 1.2 maximum_bitcast_fusion
  (130 shorter events, 19.8 us)
Async XLA Ops:
  8.3 33.0 %all-to-all-start = ((s32[64,1,256]{2,1,0:T(1,128)}), s32[64,1,256]{2,1,0:T(1,128)S(1)}, u32[]{:S(2)}, u32[]{:S(2)}) async-start(s32[64,1,256]{2,1,0:T(1,128)} %reshape.553), calls=%async_computation | async-start | bytes 131072 | tf_op jit(solution)/shard_map/all_to_all | solution.py:191
  28.1 59.5 %collective-permute-start = (s32[32]{0:T(128)S(1)}, s32[32]{0:T(128)S(1)}, u32[]{:S(2)}, u32[]{:S(2)}) collective-permute-start(s32[32]{0:T(128)S(1)} %multiply_add_fusion.1), channel_id=1, source_target_pairs={{0,256},{256,0},{1,257},{257,1},{2,258},{258,2},{3,259},{259,3},{4... | collective-permute-start | bytes 392 | tf_op jit(solution)/shard_map/ppermute | solution.py:24
  69.4 17.8 %copy-start.13 = (s32[1,1,2048]{2,1,0:T(1,128)S(1)}, s32[1,1,2048]{2,1,0:T(1,128)}, u32[]{:S(2)}) copy-start(s32[1,1,2048]{2,1,0:T(1,128)} %param.15) | copy-start | bytes 24580
  69.4 17.8 %copy-start.12 = (f32[1,1,2048]{2,1,0:T(1,128)S(1)}, f32[1,1,2048]{2,1,0:T(1,128)}, u32[]{:S(2)}) copy-start(f32[1,1,2048]{2,1,0:T(1,128)} %param.14) | copy-start | bytes 24580
  72.9 38.9 %all-to-all-start.1 = ((f32[32,1,3072]{2,1,0:T(1,128)}), f32[32,1,3072]{2,1,0:T(1,128)S(1)}, u32[]{:S(2)}, u32[]{:S(2)}) async-start(f32[32,1,3072]{2,1,0:T(1,128)} %reshape.555), calls=%async_computation.1 | async-start | bytes 786432 | tf_op jit(solution)/shard_map/all_to_all | solution.py:207
  114.7 9.4 %collective-permute-start.1 = (f32[32,64,24]{1,2,0:T(8,128)S(1)}, f32[32,64,24]{1,2,0:T(8,128)S(1)}, u32[]{:S(2)}, u32[]{:S(2)}) collective-permute-start(f32[32,64,24]{1,2,0:T(8,128)S(1)} %gather_fusion), channel_id=1, source_target_pairs={{0,256},{256,0},{1,257},{257,1},{2,258},{258,2},{3,259},{259,3},{4... | collective-permute-start | bytes 589832 | tf_op jit(solution)/shard_map/ppermute | solution.py:24
  137.0 5.4 %copy-start.2 = (f32[1,4,128,128]{3,2,1,0:T(8,128)S(1)}, f32[1,4,128,128]{3,2,1,0:T(8,128)}, u32[]{:S(2)}) copy-start(f32[1,4,128,128]{3,2,1,0:T(8,128)} %param.9) | copy-start | bytes 786436
  142.5 9.1 %collective-permute-start.2 = (f32[28,3,128]{2,1,0:T(4,128)S(1)}, f32[28,3,128]{2,1,0:T(4,128)S(1)}, u32[]{:S(2)}, u32[]{:S(2)}) collective-permute-start(f32[28,3,128]{2,1,0:T(4,128)S(1)} %get-tuple-element.16), channel_id=1, source_target_pairs={{0,32},{32,64},{64,96},{96,128},{128,160},{160,192},{192,224},{1,3... | collective-permute-start | bytes 129032 | tf_op jit(solution)/shard_map/ppermute | solution.py:34
  149.6 5.5 %collective-permute-start.3 = (f32[28,3,128]{2,1,0:T(4,128)S(1)}, f32[28,3,128]{2,1,0:T(4,128)S(1)}, u32[]{:S(2)}, u32[]{:S(2)}) collective-permute-start(f32[28,3,128]{2,1,0:T(4,128)S(1)} %get-tuple-element.17), channel_id=1, source_target_pairs={{32,0},{64,32},{96,64},{128,96},{160,128},{192,160},{224,192},{33,... | collective-permute-start | bytes 129032 | tf_op jit(solution)/shard_map/ppermute | solution.py:35
  151.6 3.5 %copy-start.6 = (f32[28,3,128]{2,1,0:T(4,128)}, f32[28,3,128]{2,1,0:T(4,128)S(1)}, u32[]{:S(2)}) copy-start(f32[28,3,128]{2,1,0:T(4,128)S(1)} %collective-permute-done.2) | copy-start | bytes 129028
  155.1 0.6 copy-start.8
  161.2 8.3 %collective-permute-start.4 = (f32[28,134,3]{1,0,2:T(8,128)}, f32[28,134,3]{1,0,2:T(8,128)}, u32[]{:S(2)}, u32[]{:S(2)}) collective-permute-start(f32[28,134,3]{1,0,2:T(8,128)} %copy.164), channel_id=1, source_target_pairs={{0,1},{1,2},{2,3},{3,4},{4,5},{5,6},{6,7},{7,8},{8,9},{9,10},{10,1... | collective-permute-start | bytes 135080 | tf_op jit(solution)/shard_map/ppermute | solution.py:34
  167.7 7.2 %collective-permute-start.5 = (f32[28,134,3]{1,0,2:T(8,128)}, f32[28,134,3]{1,0,2:T(8,128)}, u32[]{:S(2)}, u32[]{:S(2)}) collective-permute-start(f32[28,134,3]{1,0,2:T(8,128)} %copy.165), channel_id=1, source_target_pairs={{1,0},{2,1},{3,2},{4,3},{5,4},{6,5},{7,6},{8,7},{9,8},{10,9},{11,1... | collective-permute-start | bytes 135080 | tf_op jit(solution)/shard_map/ppermute | solution.py:35
  182.7 1.5 copy-start
  182.7 1.5 copy-start.3
  182.7 1.5 copy-start.7
  182.7 1.5 copy-start.9
  188.2 0.8 copy-start.10
  188.5 0.8 copy-start.4
  189.0 0.8 copy-start.11
  189.8 36.3 %copy-start.18 = (f32[4]{0:T(128)S(1)}, f32[4]{0:T(128)}, u32[]{:S(2)}) copy-start(f32[4]{0:T(128)} %get-tuple-element.32) | copy-start | bytes 52
  189.8 36.3 %copy-start.19 = (f32[4]{0:T(128)S(1)}, f32[4]{0:T(128)}, u32[]{:S(2)}) copy-start(f32[4]{0:T(128)} %get-tuple-element.33) | copy-start | bytes 52
  189.8 36.3 %copy-start.21 = (f32[4]{0:T(128)S(1)}, f32[4]{0:T(128)}, u32[]{:S(2)}) copy-start(f32[4]{0:T(128)} %iota_multiply_fusion.2) | copy-start | bytes 52
  189.8 36.6 %copy-start.14 = (f32[8]{0:T(128)S(1)}, f32[8]{0:T(128)}, u32[]{:S(2)}) copy-start(f32[8]{0:T(128)} %get-tuple-element.34) | copy-start | bytes 100
  189.8 36.6 %copy-start.15 = (f32[8]{0:T(128)S(1)}, f32[8]{0:T(128)}, u32[]{:S(2)}) copy-start(f32[8]{0:T(128)} %get-tuple-element.35) | copy-start | bytes 100
  189.8 37.0 %copy-start.16 = (f32[32]{0:T(128)S(1)}, f32[32]{0:T(128)}, u32[]{:S(2)}) copy-start(f32[32]{0:T(128)} %get-tuple-element.38) | copy-start | bytes 388
  189.8 37.0 %copy-start.17 = (f32[32]{0:T(128)S(1)}, f32[32]{0:T(128)}, u32[]{:S(2)}) copy-start(f32[32]{0:T(128)} %get-tuple-element.39) | copy-start | bytes 388
  189.8 37.0 %copy-start.20 = (f32[32]{0:T(128)S(1)}, f32[32]{0:T(128)}, u32[]{:S(2)}) copy-start(f32[32]{0:T(128)} %get-tuple-element.37) | copy-start | bytes 388
  190.4 0.8 copy-start.1
  192.2 21.0 %all-to-all-start.2 = ((f32[32,1,4]{2,1,0:T(1,128)}), f32[32,1,4]{2,1,0:T(1,128)S(1)}, u32[]{:S(2)}, u32[]{:S(2)}) async-start(f32[32,1,4]{2,1,0:T(1,128)} %broadcast_in_dim.213), calls=%async_computation.2 | async-start | bytes 32768 | tf_op jit(solution)/shard_map/all_to_all | solution.py:43
  214.0 11.3 %all-to-all-start.3 = ((f32[8,1,128]{2,1,0:T(1,128)}), f32[8,1,128]{2,1,0:T(1,128)S(1)}, u32[]{:S(2)}, u32[]{:S(2)}) async-start(f32[8,1,128]{2,1,0:T(1,128)} %reshape.557), calls=%async_computation.3 | async-start | bytes 8192 | tf_op jit(solution)/shard_map/all_to_all | solution.py:43
  226.0 6.9 %copy-start.5 = (f32[3,4,128,128]{3,2,1,0:T(8,128)S(1)}, f32[3,4,128,128]{3,2,1,0:T(8,128)}, u32[]{:S(2)}) copy-start(f32[3,4,128,128]{3,2,1,0:T(8,128)} %slice.302) | copy-start | bytes 2359300

commit v10 on v9

--- a/solution.py
+++ b/solution.py
@@ -179,18 +179,19 @@
     base_cell = (src_row[0, 0] * cols_dev + src_col[0, 0]).reshape(blocks, block_cells)
     weight_ids = weight_id[0, 0].reshape(blocks, block_cells)
     empty = jnp.zeros((slot_count, block_cells), jnp.int32)
+    slot_row = jnp.broadcast_to(jnp.pad(slot_of, (0, block_cells - blocks)), empty.shape)
     asked = jnp.stack(
-        [empty.at[slot_of].set(base_cell), empty.at[slot_of].set(weight_ids)], axis=1
-    ).reshape(n_lon, capacity, 2, block_cells)
+        [empty.at[slot_of].set(base_cell), empty.at[slot_of].set(weight_ids), slot_row], axis=1
+    ).reshape(n_lon, capacity, 3, block_cells)
     panel_pos = lax.axis_index("panel")
     panel_count = lax.axis_size("panel")
     mine = jnp.arange(panel_count, dtype=jnp.int32) != panel_pos
     routed = jnp.where(mine[:, None, None, None, None], asked[None], 0)
     routed = routed.reshape((panel_count * n_lon,) + asked.shape[1:])
-    slot_mirror = partner_2(slot_of, "panel", 0)
     routed = lax.all_to_all(routed, ("panel", "lon"), split_axis=0, concat_axis=0, tiled=True)
     routed = routed.reshape((panel_count, n_lon) + asked.shape[1:])
     requests = jnp.sum(jnp.where(mine[:, None, None, None, None], routed, 0), axis=0)
+    slot_mirror = lax.dynamic_index_in_dim(requests, lon_pos, 0, keepdims=False)[0, 2, :blocks]
     cells_asked = requests[:, :, 0, :].reshape(-1)
     frac_lat, frac_lon = fractions(requests[:, :, 1, :].reshape(-1))
     weights = jnp.stack(

time: 235 us -> 233 us (level)
  starting transfers between devices: 66.8 us -> 59.6 us
  waiting for transfers between devices: 55.9 us -> 60.5 us
    all_to_all x1, waiting for transfers between devices: 0.16 us -> 3.96 us  [shards(): lax.all_to_all(routed, ('panel', 'lon'), split_axis=0, concat_axis=0, til...]
    all_to_all x1, starting transfers between devices: 13.6 us -> 9.84 us  [shards(): lax.all_to_all(served, 'lon', split_axis=0, concat_axis=0, tiled=True)]
    ppermute x2 -> x1, starting transfers between devices: 4.93 us -> 2.4 us  [partner_2(): return lax.ppermute(block, axis, route)]
    ppermute x2 -> x1, waiting for transfers between devices: 7.37 us -> 7.5 us  [partner_2(): return lax.ppermute(block, axis, route)]
  transfers between devices with their start and end apart: 10 -> 9, of which waited for: 7 -> 7; matrix products, arithmetic and copies ran while one was open for 10% -> 7% of each run, Pallas kernels for 11% -> 0%
where the time goes in v10:
time: 233 us; the launch traced here: 232 us
  waiting for transfers between devices  60.5 us (26%)
  starting transfers between devices  59.6 us (26%)
  local copies, waits for them, and re-layouts  53.4 us (23%)
  other arithmetic  30.6 us (13%)
  Pallas kernels  24.8 us (11%)
    all_to_all x1, waiting for transfers between devices, shards(): lax.all_to_all(served, 'lon', split_axis=0, concat_axis=0, tiled=True)  24.9 us
    pallas_call x1, Pallas kernels, corner_blend(): pl.pallas_call(kernel, out_shape=jax.ShapeDtypeStruct((count, table.shape...  24.8 us
    all_to_all x1, starting transfers between devices, shards(): lax.all_to_all(routed, ('panel', 'lon'), split_axis=0, concat_axis=0, til...  19.1 us
    all_to_all x2, waiting for transfers between devices, gather_by_exchange(): lax.all_to_all(repeated, axis, split_axis=0, concat_axis=0, tiled=True)  16.9 us
    all_to_all x2, starting transfers between devices, gather_by_exchange(): lax.all_to_all(repeated, axis, split_axis=0, concat_axis=0, tiled=True)  14.5 us
    unnamed x57, local copies, waits for them, and re-layouts  13.9 us
    scatter x1, local copies, waits for them, and re-layouts, shards(): flat_cells.at[:, dest_cell[0, 0]].set(rotated)  12.1 us
    ppermute x2, starting transfers between devices, padded_2(): before = lax.ppermute(last, axis, up)  10.6 us
  transfers between devices with their start and end apart: 9, of which 7 were waited for; matrix products, arithmetic and copies ran while one was open for 7% of the time, Pallas kernels for 0%

profile of v10, /device:TPU:1, one launch (start us, length us, event | category | flops | bytes accessed | tf_op | source)
XLA Modules:
  0.0 232.1 jit_solution(18071624518900187855)
XLA Ops:
  0.6 0.7 fusion.49
  1.4 0.8 select_reduce_fusion.1
  4.1 1.4 reduce.17
  5.5 0.7 add_reduce_fusion
  8.1 0.8 reshape.581
  9.0 19.1 %all-to-all-start = ((s32[64,1,384]{2,1,0:T(1,128)}), s32[64,1,384]{2,1,0:T(1,128)S(1)}, u32[]{:S(2)}, u32[]{:S(2)}) async-start(s32[64,1,384]{2,1,0:T(1,128)} %reshape.581), calls=%async_computation | async-start | bytes 196608 | tf_op jit(solution)/shard_map/all_to_all | solution.py:191
  30.6 2.3 %copy.115 = f32[3,8,128,128]{3,1,2,0:T(8,128)S(1)} copy(f32[3,8,128,128]{3,2,1,0:T(8,128)} %bitcast.156) | data formatting | bytes 3145728
  32.9 4.6 %copy.88 = f32[24,16384]{0,1:T(8,128)} copy(f32[24,16384]{1,0:T(8,128)S(1)} %bitcast.149) | data formatting | bytes 3145728 | tf_op jit(solution)/shard_map/reshape;squeeze | solution.py:172
  37.6 0.7 broadcast_and_fusion
  38.3 4.0 %all-to-all-done = s32[64,1,384]{2,1,0:T(1,128)S(1)} async-done(((s32[64,1,384]{2,1,0:T(1,128)}), s32[64,1,384]{2,1,0:T(1,128)S(1)}, u32[]{:S(2)}, u32[]{:S(2)}) %all-to-all-start) | async-done | bytes 98336 | tf_op jit(solution)/shard_map/all_to_all | solution.py:191
  42.7 0.9 reduce.18
  44.3 0.7 reshape_squeeze.14.rows_ref
  45.0 0.7 pad_maximum_fusion.4.weights_ref
  45.7 24.8 %shard_map.95 = f32[4096,24]{1,0:T(8,128)} custom-call(s32[4096]{0:T(1024)} %reshape_squeeze.14.rows_ref, f32[4,4096]{1,0:T(4,128)} %pad_maximum_fusion.4.weights_ref, f32[16384,24]{1,0:T(8,128)} %bitcast.146), custom_call_target="tpu_custom_call" | custom-call | tf_op jit(solution)/shard_map/pallas_call | solution.py:61
  70.6 2.2 copy.86
  72.8 1.2 reshape.583
  74.0 9.8 %all-to-all-start.1 = ((f32[32,1,3072]{2,1,0:T(1,128)}), f32[32,1,3072]{2,1,0:T(1,128)S(1)}, u32[]{:S(2)}, u32[]{:S(2)}) async-start(f32[32,1,3072]{2,1,0:T(1,128)} %reshape.583), calls=%async_computation.1 | async-start | bytes 786432 | tf_op jit(solution)/shard_map/all_to_all | solution.py:208
  83.9 0.7 broadcast_and_fusion.1
  84.9 24.9 %all-to-all-done.1 = f32[32,1,3072]{2,1,0:T(1,128)S(1)} async-done(((f32[32,1,3072]{2,1,0:T(1,128)}), f32[32,1,3072]{2,1,0:T(1,128)S(1)}, u32[]{:S(2)}, u32[]{:S(2)}) %all-to-all-start.1) | async-done | bytes 393248 | tf_op jit(solution)/shard_map/all_to_all | solution.py:208
  110.3 1.6 reduce.19
  112.7 2.4 %collective-permute-start = (f32[32,64,24]{1,2,0:T(8,128)S(1)}, f32[32,64,24]{1,2,0:T(8,128)S(1)}, u32[]{:S(2)}, u32[]{:S(2)}) collective-permute-start(f32[32,64,24]{1,2,0:T(8,128)S(1)} %gather_fusion), channel_id=1, source_target_pairs={{0,256},{256,0},{1,257},{257,1},{2,258},{258,2},{3,259},{259,3},{4... | collective-permute-start | bytes 589832 | tf_op jit(solution)/shard_map/ppermute | solution.py:24
  115.2 7.5 %collective-permute-done = f32[32,64,24]{1,2,0:T(8,128)S(1)} collective-permute-done((f32[32,64,24]{1,2,0:T(8,128)S(1)}, f32[32,64,24]{1,2,0:T(8,128)S(1)}, u32[]{:S(2)}, u32[]{:S(2)}) %collective-permute-start) | collective-permute-done | bytes 196640 | tf_op jit(solution)/shard_map/ppermute | solution.py:24
  123.5 12.1 %scatter_fusion = f32[24,16384]{0,1:T(8,128)} fusion(f32[24,16384]{0,1:T(8,128)} %copy.88, s32[2048]{0:T(1024)S(1)} %bitcast.176, f32[2048,24]{1,0:T(8,128)S(1)} %copy.89), kind=kCustom, calls=%fused_computation.3 | custom fusion | bytes 598016 | tf_op jit(solution)/shard_map/scatter | solution.py:226
  135.6 5.4 %copy.90 = f32[24,128,128]{2,1,0:T(8,128)S(1)} copy(f32[24,128,128]{0,2,1:T(8,128)} %bitcast.147) | data formatting | bytes 3145728 | tf_op jit(solution)/shard_map/reshape;reshape | solution.py:243
  141.1 6.5 %collective-permute-start.1 = (f32[28,3,128]{2,1,0:T(4,128)S(1)}, f32[28,3,128]{2,1,0:T(4,128)S(1)}, u32[]{:S(2)}, u32[]{:S(2)}) collective-permute-start(f32[28,3,128]{2,1,0:T(4,128)S(1)} %get-tuple-element.16), channel_id=1, source_target_pairs={{0,32},{32,64},{64,96},{96,128},{128,160},{160,192},{192,224},{1,3... | collective-permute-start | bytes 129032 | tf_op jit(solution)/shard_map/ppermute | solution.py:34
  147.6 1.9 collective-permute-start.2
  149.6 3.5 %collective-permute-done.2 = f32[28,3,128]{2,1,0:T(4,128)S(1)} collective-permute-done((f32[28,3,128]{2,1,0:T(4,128)S(1)}, f32[28,3,128]{2,1,0:T(4,128)S(1)}, u32[]{:S(2)}, u32[]{:S(2)}) %collective-permute-start.2) | collective-permute-done | bytes 43040 | tf_op jit(solution)/shard_map/ppermute | solution.py:35
  153.9 1.9 fusion.104
  155.8 3.4 %copy.105 = f32[28,134,3]{1,0,2:T(8,128)} copy(f32[28,134,3]{2,1,0:T(8,128)} %get-tuple-element.14) | data formatting | bytes 90048
  159.2 4.0 %collective-permute-start.3 = (f32[28,134,3]{1,0,2:T(8,128)}, f32[28,134,3]{1,0,2:T(8,128)}, u32[]{:S(2)}, u32[]{:S(2)}) collective-permute-start(f32[28,134,3]{1,0,2:T(8,128)} %copy.105), channel_id=1, source_target_pairs={{0,1},{1,2},{2,3},{3,4},{4,5},{5,6},{6,7},{7,8},{8,9},{9,10},{10,1... | collective-permute-start | bytes 135080 | tf_op jit(solution)/shard_map/ppermute | solution.py:34
  163.3 1.8 copy.106
  165.1 1.3 collective-permute-start.4
  166.9 1.6 copy.93
  168.5 3.8 %collective-permute-done.4 = f32[28,134,3]{1,0,2:T(8,128)} collective-permute-done((f32[28,134,3]{1,0,2:T(8,128)}, f32[28,134,3]{1,0,2:T(8,128)}, u32[]{:S(2)}, u32[]{:S(2)}) %collective-permute-start.4) | collective-permute-done | bytes 45056 | tf_op jit(solution)/shard_map/ppermute | solution.py:35
  172.3 2.9 %copy.94 = f32[28,134,3]{2,1,0:T(8,128)} copy(f32[28,134,3]{1,0,2:T(8,128)} %collective-permute-done.4) | data formatting | bytes 90048 | tf_op jit(solution)/shard_map/ppermute | solution.py:35
  175.1 4.8 %pad_maximum_fusion = f32[28,134,134]{2,1,0:T(8,128)S(1)} fusion(f32[28,134,3]{2,1,0:T(8,128)} %copy.94, f32[28,3,128]{2,1,0:T(4,128)} %copy-done.8, f32[4,128,128]{2,1,0:T(8,128)} %bitcast.151, f32[24,128,128]{2,1,0:T(8,128)S(1)} %copy.90, f32[28,3,128]{2,1,0:T(4,128)} %copy-done.6, f32[28,134,3]{2,1,0:T(8,128)S(1)} %copy.93), kind=kLoop, calls=%fused_computation.6 | loop fusion | flops 2513840 | bytes 4022144 | tf_op jit(solution)/shard_map/concatenate | solution.py:36
  180.2 0.9 slice.280
  182.1 3.6 %fusion.4 = f32[6,4,132,132]{3,2,1,0:T(8,128)S(1)} fusion(f32[6,4,132,132]{3,2,1,0:T(8,128)S(1)} %slice.280, f32[6,4,134,134]{3,2,1,0:T(8,128)S(1)} %bitcast.144, f32[132]{0:T(256)S(1)} %divide_multiply_fusion, f32[4,132,132]{2,1,0:T(8,128)S(1)} %pad_maximum_fusion.3), kind=kLoop, calls=%fused_computation.11 | loop fusion | flops 5018112 | bytes 10315536 | tf_op jit(solution)/shard_map/add | solution.py:250
  189.7 7.7 %all-to-all-start.2 = ((f32[32,1,4]{2,1,0:T(1,128)}), f32[32,1,4]{2,1,0:T(1,128)S(1)}, u32[]{:S(2)}, u32[]{:S(2)}) async-start(f32[32,1,4]{2,1,0:T(1,128)} %broadcast_in_dim.210), calls=%async_computation.2 | async-start | bytes 32768 | tf_op jit(solution)/shard_map/all_to_all | solution.py:43
  197.4 13.6 %all-to-all-done.2 = f32[32,1,4]{2,1,0:T(1,128)S(1)} async-done(((f32[32,1,4]{2,1,0:T(1,128)}), f32[32,1,4]{2,1,0:T(1,128)S(1)}, u32[]{:S(2)}, u32[]{:S(2)}) %all-to-all-start.2) | async-done | bytes 544 | tf_op jit(solution)/shard_map/all_to_all | solution.py:43
  211.1 0.7 reshape.585
  211.8 6.8 %all-to-all-start.3 = ((f32[8,1,128]{2,1,0:T(1,128)}), f32[8,1,128]{2,1,0:T(1,128)S(1)}, u32[]{:S(2)}, u32[]{:S(2)}) async-start(f32[8,1,128]{2,1,0:T(1,128)} %reshape.585), calls=%async_computation.3 | async-start | bytes 8192 | tf_op jit(solution)/shard_map/all_to_all | solution.py:43
  218.7 1.2 slice.307
  219.8 3.3 %all-to-all-done.3 = f32[8,1,128]{2,1,0:T(1,128)S(1)} async-done(((f32[8,1,128]{2,1,0:T(1,128)}), f32[8,1,128]{2,1,0:T(1,128)S(1)}, u32[]{:S(2)}, u32[]{:S(2)}) %all-to-all-start.3) | async-done | bytes 4128 | tf_op jit(solution)/shard_map/all_to_all | solution.py:43
  226.0 1.9 add_bitcast_fusion
  227.9 1.2 select_add_fusion
  229.6 1.2 fusion.25
  230.8 1.2 maximum_bitcast_fusion
  (127 shorter events, 19.9 us)
Async XLA Ops:
  9.0 33.2 %all-to-all-start = ((s32[64,1,384]{2,1,0:T(1,128)}), s32[64,1,384]{2,1,0:T(1,128)S(1)}, u32[]{:S(2)}, u32[]{:S(2)}) async-start(s32[64,1,384]{2,1,0:T(1,128)} %reshape.581), calls=%async_computation | async-start | bytes 196608 | tf_op jit(solution)/shard_map/all_to_all | solution.py:191
  70.6 14.0 %copy-start.13 = (s32[1,1,2048]{2,1,0:T(1,128)S(1)}, s32[1,1,2048]{2,1,0:T(1,128)}, u32[]{:S(2)}) copy-start(s32[1,1,2048]{2,1,0:T(1,128)} %param.15) | copy-start | bytes 24580
  70.6 14.0 %copy-start.12 = (f32[1,1,2048]{2,1,0:T(1,128)S(1)}, f32[1,1,2048]{2,1,0:T(1,128)}, u32[]{:S(2)}) copy-start(f32[1,1,2048]{2,1,0:T(1,128)} %param.14) | copy-start | bytes 24580
  74.0 35.7 %all-to-all-start.1 = ((f32[32,1,3072]{2,1,0:T(1,128)}), f32[32,1,3072]{2,1,0:T(1,128)S(1)}, u32[]{:S(2)}, u32[]{:S(2)}) async-start(f32[32,1,3072]{2,1,0:T(1,128)} %reshape.583), calls=%async_computation.1 | async-start | bytes 786432 | tf_op jit(solution)/shard_map/all_to_all | solution.py:208
  112.7 10.0 %collective-permute-start = (f32[32,64,24]{1,2,0:T(8,128)S(1)}, f32[32,64,24]{1,2,0:T(8,128)S(1)}, u32[]{:S(2)}, u32[]{:S(2)}) collective-permute-start(f32[32,64,24]{1,2,0:T(8,128)S(1)} %gather_fusion), channel_id=1, source_target_pairs={{0,256},{256,0},{1,257},{257,1},{2,258},{258,2},{3,259},{259,3},{4... | collective-permute-start | bytes 589832 | tf_op jit(solution)/shard_map/ppermute | solution.py:24
  135.6 5.4 %copy-start.2 = (f32[1,4,128,128]{3,2,1,0:T(8,128)S(1)}, f32[1,4,128,128]{3,2,1,0:T(8,128)}, u32[]{:S(2)}) copy-start(f32[1,4,128,128]{3,2,1,0:T(8,128)} %param.9) | copy-start | bytes 786436
  141.1 8.5 %collective-permute-start.1 = (f32[28,3,128]{2,1,0:T(4,128)S(1)}, f32[28,3,128]{2,1,0:T(4,128)S(1)}, u32[]{:S(2)}, u32[]{:S(2)}) collective-permute-start(f32[28,3,128]{2,1,0:T(4,128)S(1)} %get-tuple-element.16), channel_id=1, source_target_pairs={{0,32},{32,64},{64,96},{96,128},{128,160},{160,192},{192,224},{1,3... | collective-permute-start | bytes 129032 | tf_op jit(solution)/shard_map/ppermute | solution.py:34
  147.6 5.5 %collective-permute-start.2 = (f32[28,3,128]{2,1,0:T(4,128)S(1)}, f32[28,3,128]{2,1,0:T(4,128)S(1)}, u32[]{:S(2)}, u32[]{:S(2)}) collective-permute-start(f32[28,3,128]{2,1,0:T(4,128)S(1)} %get-tuple-element.17), channel_id=1, source_target_pairs={{32,0},{64,32},{96,64},{128,96},{160,128},{192,160},{224,192},{33,... | collective-permute-start | bytes 129032 | tf_op jit(solution)/shard_map/ppermute | solution.py:35
  149.6 3.5 %copy-start.6 = (f32[28,3,128]{2,1,0:T(4,128)}, f32[28,3,128]{2,1,0:T(4,128)S(1)}, u32[]{:S(2)}) copy-start(f32[28,3,128]{2,1,0:T(4,128)S(1)} %collective-permute-done.1) | copy-start | bytes 129028
  153.1 0.6 copy-start.8
  159.2 7.7 %collective-permute-start.3 = (f32[28,134,3]{1,0,2:T(8,128)}, f32[28,134,3]{1,0,2:T(8,128)}, u32[]{:S(2)}, u32[]{:S(2)}) collective-permute-start(f32[28,134,3]{1,0,2:T(8,128)} %copy.105), channel_id=1, source_target_pairs={{0,1},{1,2},{2,3},{3,4},{4,5},{5,6},{6,7},{7,8},{8,9},{9,10},{10,1... | collective-permute-start | bytes 135080 | tf_op jit(solution)/shard_map/ppermute | solution.py:34
  165.1 7.2 %collective-permute-start.4 = (f32[28,134,3]{1,0,2:T(8,128)}, f32[28,134,3]{1,0,2:T(8,128)}, u32[]{:S(2)}, u32[]{:S(2)}) collective-permute-start(f32[28,134,3]{1,0,2:T(8,128)} %copy.106), channel_id=1, source_target_pairs={{1,0},{2,1},{3,2},{4,3},{5,4},{6,5},{7,6},{8,7},{9,8},{10,9},{11,1... | collective-permute-start | bytes 135080 | tf_op jit(solution)/shard_map/ppermute | solution.py:35
  180.2 1.5 copy-start
  180.2 1.5 copy-start.3
  180.2 1.5 copy-start.7
  180.2 1.5 copy-start.9
  185.7 0.8 copy-start.10
  185.9 0.8 copy-start.4
  186.4 0.8 copy-start.11
  187.2 36.7 %copy-start.18 = (f32[4]{0:T(128)S(1)}, f32[4]{0:T(128)}, u32[]{:S(2)}) copy-start(f32[4]{0:T(128)} %get-tuple-element.32) | copy-start | bytes 52
  187.2 36.7 %copy-start.19 = (f32[4]{0:T(128)S(1)}, f32[4]{0:T(128)}, u32[]{:S(2)}) copy-start(f32[4]{0:T(128)} %get-tuple-element.33) | copy-start | bytes 52
  187.2 36.7 %copy-start.21 = (f32[4]{0:T(128)S(1)}, f32[4]{0:T(128)}, u32[]{:S(2)}) copy-start(f32[4]{0:T(128)} %iota_multiply_fusion.2) | copy-start | bytes 52
  187.2 37.1 %copy-start.14 = (f32[8]{0:T(128)S(1)}, f32[8]{0:T(128)}, u32[]{:S(2)}) copy-start(f32[8]{0:T(128)} %get-tuple-element.34) | copy-start | bytes 100
  187.2 37.1 %copy-start.15 = (f32[8]{0:T(128)S(1)}, f32[8]{0:T(128)}, u32[]{:S(2)}) copy-start(f32[8]{0:T(128)} %get-tuple-element.35) | copy-start | bytes 100
  187.2 37.4 %copy-start.16 = (f32[32]{0:T(128)S(1)}, f32[32]{0:T(128)}, u32[]{:S(2)}) copy-start(f32[32]{0:T(128)} %get-tuple-element.38) | copy-start | bytes 388
  187.2 37.4 %copy-start.17 = (f32[32]{0:T(128)S(1)}, f32[32]{0:T(128)}, u32[]{:S(2)}) copy-start(f32[32]{0:T(128)} %get-tuple-element.39) | copy-start | bytes 388
  187.2 37.4 %copy-start.20 = (f32[32]{0:T(128)S(1)}, f32[32]{0:T(128)}, u32[]{:S(2)}) copy-start(f32[32]{0:T(128)} %get-tuple-element.37) | copy-start | bytes 388
  187.8 0.8 copy-start.1
  189.7 21.3 %all-to-all-start.2 = ((f32[32,1,4]{2,1,0:T(1,128)}), f32[32,1,4]{2,1,0:T(1,128)S(1)}, u32[]{:S(2)}, u32[]{:S(2)}) async-start(f32[32,1,4]{2,1,0:T(1,128)} %broadcast_in_dim.210), calls=%async_computation.2 | async-start | bytes 32768 | tf_op jit(solution)/shard_map/all_to_all | solution.py:43
  211.8 11.3 %all-to-all-start.3 = ((f32[8,1,128]{2,1,0:T(1,128)}), f32[8,1,128]{2,1,0:T(1,128)S(1)}, u32[]{:S(2)}, u32[]{:S(2)}) async-start(f32[8,1,128]{2,1,0:T(1,128)} %reshape.585), calls=%async_computation.3 | async-start | bytes 8192 | tf_op jit(solution)/shard_map/all_to_all | solution.py:43
  223.9 6.9 %copy-start.5 = (f32[3,4,128,128]{3,2,1,0:T(8,128)S(1)}, f32[3,4,128,128]{3,2,1,0:T(8,128)}, u32[]{:S(2)}) copy-start(f32[3,4,128,128]{3,2,1,0:T(8,128)} %slice.307) | copy-start | bytes 2359300

commit v11 on v9

--- a/solution.py
+++ b/solution.py
@@ -187,7 +187,6 @@
     mine = jnp.arange(panel_count, dtype=jnp.int32) != panel_pos
     routed = jnp.where(mine[:, None, None, None, None], asked[None], 0)
     routed = routed.reshape((panel_count * n_lon,) + asked.shape[1:])
-    slot_mirror = partner_2(slot_of, "panel", 0)
     routed = lax.all_to_all(routed, ("panel", "lon"), split_axis=0, concat_axis=0, tiled=True)
     routed = routed.reshape((panel_count, n_lon) + asked.shape[1:])
     requests = jnp.sum(jnp.where(mine[:, None, None, None, None], routed, 0), axis=0)
@@ -204,9 +203,12 @@
     )
     served = corner_blend(flat_cells.T, cells_asked, weights, cols_dev)
     served = served.reshape(n_lon, capacity, block_cells, channels)
-    served = lax.all_to_all(served, "lon", split_axis=0, concat_axis=0, tiled=True)
-    served = served.reshape(slot_count, block_cells, channels)[slot_mirror]
-    values = partner_2(served, "panel", 0)
+    sent = jnp.where(mine[:, None, None, None, None], served[None], 0.0)
+    sent = sent.reshape((panel_count * n_lon,) + served.shape[1:])
+    sent = lax.all_to_all(sent, ("panel", "lon"), split_axis=0, concat_axis=0, tiled=True)
+    sent = sent.reshape((panel_count, n_lon) + served.shape[1:])
+    back = lax.dynamic_index_in_dim(sent, 1 - panel_pos, 0, keepdims=False)
+    values = back.reshape(slot_count, block_cells, channels)[slot_of]
     values = values.reshape(blocks * block_cells, channels).T.reshape(6, levels, blocks * block_cells)
     turn = border_angle[0, 0]
     cos_angle = jnp.cos(turn)

time: 235 us -> 238 us (1.013)
  starting transfers between devices: 66.8 us -> 60.2 us
  waiting for transfers between devices: 55.9 us -> 60.1 us
  other arithmetic: 30.3 us -> 33.9 us
    ppermute x2 -> x0, waiting for transfers between devices: 7.37 us -> none  [partner_2(): return lax.ppermute(block, axis, route)]
    all_to_all x1, waiting for transfers between devices: 0.16 us -> 6.92 us  [shards(): lax.all_to_all(routed, ('panel', 'lon'), split_axis=0, concat_axis=0, til...]
    all_to_all x1, starting transfers between devices: 13.6 us -> 7.51 us  [shards(): lax.all_to_all(sent, ('panel', 'lon'), split_axis=0, concat_axis=0, tiled...]
    ppermute x2 -> x0, starting transfers between devices: 4.93 us -> none  [partner_2(): return lax.ppermute(block, axis, route)]
    all_to_all x1, waiting for transfers between devices: 24.2 us -> 28.4 us  [shards(): lax.all_to_all(sent, ('panel', 'lon'), split_axis=0, concat_axis=0, tiled...]
    ppermute x2, starting transfers between devices: 11.7 us -> 14.8 us  [padded_2(): before = lax.ppermute(last, axis, up)]
    unnamed x57 -> x71, local copies, waits for them, and re-layouts: 13.8 us -> 15.1 us
  transfers between devices with their start and end apart: 10 -> 8, of which waited for: 7 -> 6; matrix products, arithmetic and copies ran while one was open for 10% -> 8% of each run, Pallas kernels for 11% -> 0%
where the time goes in v11:
time: 238 us; the launch traced here: 237 us
  starting transfers between devices  60.2 us (25%)
  waiting for transfers between devices  60.1 us (25%)
  local copies, waits for them, and re-layouts  54.8 us (23%)
  other arithmetic  33.9 us (14%)
  Pallas kernels  24.8 us (10%)
    all_to_all x1, waiting for transfers between devices, shards(): lax.all_to_all(sent, ('panel', 'lon'), split_axis=0, concat_axis=0, tiled...  28.4 us
    pallas_call x1, Pallas kernels, corner_blend(): pl.pallas_call(kernel, out_shape=jax.ShapeDtypeStruct((count, table.shape...  24.8 us
    all_to_all x1, starting transfers between devices, shards(): lax.all_to_all(routed, ('panel', 'lon'), split_axis=0, concat_axis=0, til...  19.1 us
    all_to_all x2, waiting for transfers between devices, gather_by_exchange(): lax.all_to_all(repeated, axis, split_axis=0, concat_axis=0, tiled=True)  16.9 us
    all_to_all x2, starting transfers between devices, gather_by_exchange(): lax.all_to_all(repeated, axis, split_axis=0, concat_axis=0, tiled=True)  15.6 us
    unnamed x71, local copies, waits for them, and re-layouts  15.1 us
    ppermute x2, starting transfers between devices, padded_2(): before = lax.ppermute(last, axis, up)  14.8 us
    scatter x1, local copies, waits for them, and re-layouts, shards(): flat_cells.at[:, dest_cell[0, 0]].set(rotated)  12.1 us
  transfers between devices with their start and end apart: 8, of which 6 were waited for; matrix products, arithmetic and copies ran while one was open for 8% of the time, Pallas kernels for 0%

profile of v11, /device:TPU:1, one launch (start us, length us, event | category | flops | bytes accessed | tf_op | source)
XLA Modules:
  0.0 236.9 jit_solution(2031976102105407078)
XLA Ops:
  0.6 0.7 fusion.49
  1.4 0.8 select_reduce_fusion.1
  3.4 1.4 reduce.17
  4.9 0.7 add_reduce_fusion
  5.7 0.7 scatter_custom_fusion.1
  7.5 0.8 reshape.557
  8.3 19.1 %all-to-all-start = ((s32[64,1,256]{2,1,0:T(1,128)}), s32[64,1,256]{2,1,0:T(1,128)S(1)}, u32[]{:S(2)}, u32[]{:S(2)}) async-start(s32[64,1,256]{2,1,0:T(1,128)} %reshape.557), calls=%async_computation | async-start | bytes 131072 | tf_op jit(solution)/shard_map/all_to_all | solution.py:190
  27.4 2.3 copy.174
  29.7 4.6 %copy.144 = f32[24,16384]{0,1:T(8,128)} copy(f32[24,16384]{1,0:T(8,128)S(1)} %bitcast.142) | data formatting | bytes 3145728 | tf_op jit(solution)/shard_map/reshape;squeeze | solution.py:172
  34.3 6.9 %all-to-all-done = s32[64,1,256]{2,1,0:T(1,128)S(1)} async-done(((s32[64,1,256]{2,1,0:T(1,128)}), s32[64,1,256]{2,1,0:T(1,128)S(1)}, u32[]{:S(2)}, u32[]{:S(2)}) %all-to-all-start) | async-done | bytes 65568 | tf_op jit(solution)/shard_map/all_to_all | solution.py:190
  41.8 0.8 reduce.18
  43.2 0.7 reshape_squeeze.14.rows_ref
  43.9 0.7 pad_maximum_fusion.4.weights_ref
  44.6 24.8 %shard_map.95 = f32[4096,24]{1,0:T(8,128)} custom-call(s32[4096]{0:T(1024)} %reshape_squeeze.14.rows_ref, f32[4,4096]{1,0:T(4,128)} %pad_maximum_fusion.4.weights_ref, f32[16384,24]{1,0:T(8,128)} %bitcast.138), custom_call_target="tpu_custom_call" | custom-call | tf_op jit(solution)/shard_map/pallas_call | solution.py:61
  69.4 2.2 copy.142
  71.8 1.9 reshape.559
  73.7 7.5 %all-to-all-start.1 = ((f32[64,1,3072]{2,1,0:T(1,128)}), f32[64,1,3072]{2,1,0:T(1,128)S(1)}, u32[]{:S(2)}, u32[]{:S(2)}) async-start(f32[64,1,3072]{2,1,0:T(1,128)} %reshape.559), calls=%async_computation.1 | async-start | bytes 1572864 | tf_op jit(solution)/shard_map/all_to_all | solution.py:208
  86.7 0.7 broadcast_and_fusion
  87.4 0.7 broadcast_and_fusion.1
  89.0 28.4 %all-to-all-done.1 = f32[64,1,3072]{2,1,0:T(1,128)S(1)} async-done(((f32[64,1,3072]{2,1,0:T(1,128)}), f32[64,1,3072]{2,1,0:T(1,128)S(1)}, u32[]{:S(2)}, u32[]{:S(2)}) %all-to-all-start.1) | async-done | bytes 786464 | tf_op jit(solution)/shard_map/all_to_all | solution.py:208
  118.0 2.5 %reduce.19 = f32[64,3072]{1,0:T(8,128)S(1)} reduce(f32[64,1,3072]{2,1,0:T(1,128)S(1)} %all-to-all-done.1, f32[]{:T(128)} %broadcast.866), dimensions={1}, to_apply=%all_to_all.13.reduce_sub_computation | reduce | bytes 1572868 | tf_op jit(solution)/shard_map/all_to_all | solution.py:208
  121.0 0.7 gather_fusion
  122.5 12.1 %scatter_fusion = f32[24,16384]{0,1:T(8,128)} fusion(f32[24,16384]{0,1:T(8,128)} %copy.144, s32[2048]{0:T(1024)S(1)} %bitcast.168, f32[2048,24]{1,0:T(8,128)S(1)} %copy.145), kind=kCustom, calls=%fused_computation.3 | custom fusion | bytes 598016 | tf_op jit(solution)/shard_map/scatter | solution.py:227
  134.7 5.4 %copy.146 = f32[24,128,128]{2,1,0:T(8,128)S(1)} copy(f32[24,128,128]{0,2,1:T(8,128)} %bitcast.139) | data formatting | bytes 3145728 | tf_op jit(solution)/shard_map/reshape;reshape | solution.py:244
  140.1 9.5 %collective-permute-start = (f32[28,3,128]{2,1,0:T(4,128)S(1)}, f32[28,3,128]{2,1,0:T(4,128)S(1)}, u32[]{:S(2)}, u32[]{:S(2)}) collective-permute-start(f32[28,3,128]{2,1,0:T(4,128)S(1)} %get-tuple-element.16), channel_id=1, source_target_pairs={{0,32},{32,64},{64,96},{96,128},{128,160},{160,192},{192,224},{1,3... | collective-permute-start | bytes 129032 | tf_op jit(solution)/shard_map/ppermute | solution.py:34
  149.6 1.9 collective-permute-start.1
  151.6 3.5 %collective-permute-done.1 = f32[28,3,128]{2,1,0:T(4,128)S(1)} collective-permute-done((f32[28,3,128]{2,1,0:T(4,128)S(1)}, f32[28,3,128]{2,1,0:T(4,128)S(1)}, u32[]{:S(2)}, u32[]{:S(2)}) %collective-permute-start.1) | collective-permute-done | bytes 43040 | tf_op jit(solution)/shard_map/ppermute | solution.py:35
  155.9 1.9 fusion.103
  157.8 3.4 %copy.164 = f32[28,134,3]{1,0,2:T(8,128)} copy(f32[28,134,3]{2,1,0:T(8,128)} %get-tuple-element.14) | data formatting | bytes 90048
  161.2 5.3 %collective-permute-start.2 = (f32[28,134,3]{1,0,2:T(8,128)}, f32[28,134,3]{1,0,2:T(8,128)}, u32[]{:S(2)}, u32[]{:S(2)}) collective-permute-start(f32[28,134,3]{1,0,2:T(8,128)} %copy.164), channel_id=1, source_target_pairs={{0,1},{1,2},{2,3},{3,4},{4,5},{5,6},{6,7},{7,8},{8,9},{9,10},{10,1... | collective-permute-start | bytes 135080 | tf_op jit(solution)/shard_map/ppermute | solution.py:34
  166.5 1.8 copy.165
  168.3 1.3 collective-permute-start.3
  169.6 1.6 copy.149
  171.2 4.3 %collective-permute-done.3 = f32[28,134,3]{1,0,2:T(8,128)} collective-permute-done((f32[28,134,3]{1,0,2:T(8,128)}, f32[28,134,3]{1,0,2:T(8,128)}, u32[]{:S(2)}, u32[]{:S(2)}) %collective-permute-start.3) | collective-permute-done | bytes 45056 | tf_op jit(solution)/shard_map/ppermute | solution.py:35
  175.5 2.9 %copy.150 = f32[28,134,3]{2,1,0:T(8,128)} copy(f32[28,134,3]{1,0,2:T(8,128)} %collective-permute-done.3) | data formatting | bytes 90048 | tf_op jit(solution)/shard_map/ppermute | solution.py:35
  178.4 4.8 %pad_maximum_fusion = f32[28,134,134]{2,1,0:T(8,128)S(1)} fusion(f32[28,134,3]{2,1,0:T(8,128)} %copy.150, f32[28,3,128]{2,1,0:T(4,128)} %copy-done.8, f32[4,128,128]{2,1,0:T(8,128)} %bitcast.144, f32[24,128,128]{2,1,0:T(8,128)S(1)} %copy.146, f32[28,3,128]{2,1,0:T(4,128)} %copy-done.6, f32[28,134,3]{2,1,0:T(8,128)S(1)} %copy.149), kind=kLoop, calls=%fused_computation.6 | loop fusion | flops 2513840 | bytes 4022144 | tf_op jit(solution)/shard_map/concatenate | solution.py:36
  183.5 0.9 slice.275
  185.6 3.5 %fusion.4 = f32[6,4,132,132]{3,2,1,0:T(8,128)S(1)} fusion(f32[6,4,132,132]{3,2,1,0:T(8,128)S(1)} %slice.275, f32[6,4,134,134]{3,2,1,0:T(8,128)S(1)} %bitcast.136, f32[132]{0:T(256)S(1)} %copy-done.20, f32[4,132,132]{2,1,0:T(8,128)S(1)} %pad_maximum_fusion.3), kind=kLoop, calls=%fused_computation.11 | loop fusion | flops 5018112 | bytes 10315536 | tf_op jit(solution)/shard_map/add | solution.py:251
  193.4 8.8 %all-to-all-start.2 = ((f32[32,1,4]{2,1,0:T(1,128)}), f32[32,1,4]{2,1,0:T(1,128)S(1)}, u32[]{:S(2)}, u32[]{:S(2)}) async-start(f32[32,1,4]{2,1,0:T(1,128)} %broadcast_in_dim.240), calls=%async_computation.2 | async-start | bytes 32768 | tf_op jit(solution)/shard_map/all_to_all | solution.py:43
  202.2 13.6 %all-to-all-done.2 = f32[32,1,4]{2,1,0:T(1,128)S(1)} async-done(((f32[32,1,4]{2,1,0:T(1,128)}), f32[32,1,4]{2,1,0:T(1,128)S(1)}, u32[]{:S(2)}, u32[]{:S(2)}) %all-to-all-start.2) | async-done | bytes 544 | tf_op jit(solution)/shard_map/all_to_all | solution.py:43
  215.9 0.7 reshape.561
  216.6 6.8 %all-to-all-start.3 = ((f32[8,1,128]{2,1,0:T(1,128)}), f32[8,1,128]{2,1,0:T(1,128)S(1)}, u32[]{:S(2)}, u32[]{:S(2)}) async-start(f32[8,1,128]{2,1,0:T(1,128)} %reshape.561), calls=%async_computation.3 | async-start | bytes 8192 | tf_op jit(solution)/shard_map/all_to_all | solution.py:43
  223.5 1.2 slice.302
  224.6 3.3 %all-to-all-done.3 = f32[8,1,128]{2,1,0:T(1,128)S(1)} async-done(((f32[8,1,128]{2,1,0:T(1,128)}), f32[8,1,128]{2,1,0:T(1,128)S(1)}, u32[]{:S(2)}, u32[]{:S(2)}) %all-to-all-start.3) | async-done | bytes 4128 | tf_op jit(solution)/shard_map/all_to_all | solution.py:43
  230.7 1.9 add_bitcast_fusion
  232.6 1.3 select_add_fusion
  234.5 1.2 fusion.25
  235.7 1.2 maximum_bitcast_fusion
  (140 shorter events, 21.7 us)
Async XLA Ops:
  8.3 33.0 %all-to-all-start = ((s32[64,1,256]{2,1,0:T(1,128)}), s32[64,1,256]{2,1,0:T(1,128)S(1)}, u32[]{:S(2)}, u32[]{:S(2)}) async-start(s32[64,1,256]{2,1,0:T(1,128)} %reshape.557), calls=%async_computation | async-start | bytes 131072 | tf_op jit(solution)/shard_map/all_to_all | solution.py:190
  71.8 16.3 %copy-start.14 = (s32[1,1,2048]{2,1,0:T(1,128)S(1)}, s32[1,1,2048]{2,1,0:T(1,128)}, u32[]{:S(2)}) copy-start(s32[1,1,2048]{2,1,0:T(1,128)} %param.15) | copy-start | bytes 24580
  71.8 16.9 %copy-start.13 = (f32[1,1,2048]{2,1,0:T(1,128)S(1)}, f32[1,1,2048]{2,1,0:T(1,128)}, u32[]{:S(2)}) copy-start(f32[1,1,2048]{2,1,0:T(1,128)} %param.14) | copy-start | bytes 24580
  73.7 43.8 %all-to-all-start.1 = ((f32[64,1,3072]{2,1,0:T(1,128)}), f32[64,1,3072]{2,1,0:T(1,128)S(1)}, u32[]{:S(2)}, u32[]{:S(2)}) async-start(f32[64,1,3072]{2,1,0:T(1,128)} %reshape.559), calls=%async_computation.1 | async-start | bytes 1572864 | tf_op jit(solution)/shard_map/all_to_all | solution.py:208
  121.7 0.8 copy-start.12
  134.7 5.4 %copy-start.2 = (f32[1,4,128,128]{3,2,1,0:T(8,128)S(1)}, f32[1,4,128,128]{3,2,1,0:T(8,128)}, u32[]{:S(2)}) copy-start(f32[1,4,128,128]{3,2,1,0:T(8,128)} %param.9) | copy-start | bytes 786436
  140.1 11.5 %collective-permute-start = (f32[28,3,128]{2,1,0:T(4,128)S(1)}, f32[28,3,128]{2,1,0:T(4,128)S(1)}, u32[]{:S(2)}, u32[]{:S(2)}) collective-permute-start(f32[28,3,128]{2,1,0:T(4,128)S(1)} %get-tuple-element.16), channel_id=1, source_target_pairs={{0,32},{32,64},{64,96},{96,128},{128,160},{160,192},{192,224},{1,3... | collective-permute-start | bytes 129032 | tf_op jit(solution)/shard_map/ppermute | solution.py:34
  149.6 5.5 %collective-permute-start.1 = (f32[28,3,128]{2,1,0:T(4,128)S(1)}, f32[28,3,128]{2,1,0:T(4,128)S(1)}, u32[]{:S(2)}, u32[]{:S(2)}) collective-permute-start(f32[28,3,128]{2,1,0:T(4,128)S(1)} %get-tuple-element.17), channel_id=1, source_target_pairs={{32,0},{64,32},{96,64},{128,96},{160,128},{192,160},{224,192},{33,... | collective-permute-start | bytes 129032 | tf_op jit(solution)/shard_map/ppermute | solution.py:35
  151.6 3.5 %copy-start.6 = (f32[28,3,128]{2,1,0:T(4,128)}, f32[28,3,128]{2,1,0:T(4,128)S(1)}, u32[]{:S(2)}) copy-start(f32[28,3,128]{2,1,0:T(4,128)S(1)} %collective-permute-done) | copy-start | bytes 129028
  155.1 0.6 copy-start.8
  161.2 8.4 %collective-permute-start.2 = (f32[28,134,3]{1,0,2:T(8,128)}, f32[28,134,3]{1,0,2:T(8,128)}, u32[]{:S(2)}, u32[]{:S(2)}) collective-permute-start(f32[28,134,3]{1,0,2:T(8,128)} %copy.164), channel_id=1, source_target_pairs={{0,1},{1,2},{2,3},{3,4},{4,5},{5,6},{6,7},{7,8},{8,9},{9,10},{10,1... | collective-permute-start | bytes 135080 | tf_op jit(solution)/shard_map/ppermute | solution.py:34
  168.3 7.2 %collective-permute-start.3 = (f32[28,134,3]{1,0,2:T(8,128)}, f32[28,134,3]{1,0,2:T(8,128)}, u32[]{:S(2)}, u32[]{:S(2)}) collective-permute-start(f32[28,134,3]{1,0,2:T(8,128)} %copy.165), channel_id=1, source_target_pairs={{1,0},{2,1},{3,2},{4,3},{5,4},{6,5},{7,6},{8,7},{9,8},{10,9},{11,1... | collective-permute-start | bytes 135080 | tf_op jit(solution)/shard_map/ppermute | solution.py:35
  183.4 1.5 copy-start
  183.4 1.5 copy-start.3
  183.4 1.5 copy-start.7
  183.4 1.5 copy-start.9
  185.0 0.6 copy-start.20
  189.4 0.8 copy-start.4
  189.4 0.8 copy-start.11
  190.2 0.8 copy-start.10
  190.2 0.8 copy-start.15
  190.2 0.8 copy-start.16
  191.5 0.8 copy-start.1
  191.5 37.1 %copy-start.26 = (f32[4]{0:T(128)S(1)}, f32[4]{0:T(128)}, u32[]{:S(2)}) copy-start(f32[4]{0:T(128)} %get-tuple-element.32) | copy-start | bytes 52
  191.5 37.1 %copy-start.27 = (f32[4]{0:T(128)S(1)}, f32[4]{0:T(128)}, u32[]{:S(2)}) copy-start(f32[4]{0:T(128)} %get-tuple-element.33) | copy-start | bytes 52
  191.5 37.5 %copy-start.22 = (f32[8]{0:T(128)S(1)}, f32[8]{0:T(128)}, u32[]{:S(2)}) copy-start(f32[8]{0:T(128)} %get-tuple-element.34) | copy-start | bytes 100
  191.5 37.5 %copy-start.23 = (f32[8]{0:T(128)S(1)}, f32[8]{0:T(128)}, u32[]{:S(2)}) copy-start(f32[8]{0:T(128)} %get-tuple-element.35) | copy-start | bytes 100
  191.6 37.8 %copy-start.17 = (f32[4,8]{1,0:T(4,128)S(1)}, f32[4,8]{1,0:T(4,128)}, u32[]{:S(2)}) copy-start(f32[4,8]{1,0:T(4,128)} %broadcast_add_fusion) | copy-start | bytes 388
  191.6 37.8 %copy-start.21 = (f32[32]{0:T(128)S(1)}, f32[32]{0:T(128)}, u32[]{:S(2)}) copy-start(f32[32]{0:T(128)} %get-tuple-element.36) | copy-start | bytes 388
  191.6 37.8 %copy-start.24 = (f32[32]{0:T(128)S(1)}, f32[32]{0:T(128)}, u32[]{:S(2)}) copy-start(f32[32]{0:T(128)} %get-tuple-element.38) | copy-start | bytes 388
  191.6 37.8 %copy-start.25 = (f32[32]{0:T(128)S(1)}, f32[32]{0:T(128)}, u32[]{:S(2)}) copy-start(f32[32]{0:T(128)} %get-tuple-element.39) | copy-start | bytes 388
  191.6 37.8 %copy-start.28 = (f32[32]{0:T(128)S(1)}, f32[32]{0:T(128)}, u32[]{:S(2)}) copy-start(f32[32]{0:T(128)} %get-tuple-element.37) | copy-start | bytes 388
  192.3 40.3 %copy-start.18 = (pred[130]{0:T(512)(128)(4,1)S(1)}, pred[130]{0:T(512)(128)(4,1)}, u32[]{:S(2)}) copy-start(pred[130]{0:T(512)(128)(4,1)} %get-tuple-element.40) | copy-start | bytes 394
  192.3 40.3 %copy-start.19 = (pred[130]{0:T(512)(128)(4,1)S(1)}, pred[130]{0:T(512)(128)(4,1)}, u32[]{:S(2)}) copy-start(pred[130]{0:T(512)(128)(4,1)} %get-tuple-element.41) | copy-start | bytes 394
  193.4 22.4 %all-to-all-start.2 = ((f32[32,1,4]{2,1,0:T(1,128)}), f32[32,1,4]{2,1,0:T(1,128)S(1)}, u32[]{:S(2)}, u32[]{:S(2)}) async-start(f32[32,1,4]{2,1,0:T(1,128)} %broadcast_in_dim.240), calls=%async_computation.2 | async-start | bytes 32768 | tf_op jit(solution)/shard_map/all_to_all | solution.py:43
  216.6 11.3 %all-to-all-start.3 = ((f32[8,1,128]{2,1,0:T(1,128)}), f32[8,1,128]{2,1,0:T(1,128)S(1)}, u32[]{:S(2)}, u32[]{:S(2)}) async-start(f32[8,1,128]{2,1,0:T(1,128)} %reshape.561), calls=%async_computation.3 | async-start | bytes 8192 | tf_op jit(solution)/shard_map/all_to_all | solution.py:43
  232.6 3.0 %copy-start.5 = (f32[3,4,128,128]{3,2,1,0:T(8,128)S(1)}, f32[3,4,128,128]{3,2,1,0:T(8,128)}, u32[]{:S(2)}) copy-start(f32[3,4,128,128]{3,2,1,0:T(8,128)} %slice.302) | copy-start | bytes 2359300

commit v12 on v10

--- a/solution.py
+++ b/solution.py
@@ -56,7 +56,7 @@
             out_ref[pl.ds(t, 1), :] = total
             return carry
 
-        lax.fori_loop(0, count, body, 0, unroll=16)
+        lax.fori_loop(0, count, body, 0, unroll=32)
 
     return pl.pallas_call(
         kernel,

time: 233 us -> 232 us (level)
  no operation moved by 1% of the time
where the time goes in v12:
time: 232 us; the launch traced here: 231 us
  waiting for transfers between devices  60.5 us (26%)
  starting transfers between devices  59.6 us (26%)
  local copies, waits for them, and re-layouts  53.4 us (23%)
  other arithmetic  30.6 us (13%)
  Pallas kernels  23.9 us (10%)
    all_to_all x1, waiting for transfers between devices, shards(): lax.all_to_all(served, 'lon', split_axis=0, concat_axis=0, tiled=True)  24.9 us
    pallas_call x1, Pallas kernels, corner_blend(): pl.pallas_call(kernel, out_shape=jax.ShapeDtypeStruct((count, table.shape...  23.9 us
    all_to_all x1, starting transfers between devices, shards(): lax.all_to_all(routed, ('panel', 'lon'), split_axis=0, concat_axis=0, til...  19.1 us
    all_to_all x2, waiting for transfers between devices, gather_by_exchange(): lax.all_to_all(repeated, axis, split_axis=0, concat_axis=0, tiled=True)  16.9 us
    all_to_all x2, starting transfers between devices, gather_by_exchange(): lax.all_to_all(repeated, axis, split_axis=0, concat_axis=0, tiled=True)  14.5 us
    unnamed x57, local copies, waits for them, and re-layouts  13.9 us
    scatter x1, local copies, waits for them, and re-layouts, shards(): flat_cells.at[:, dest_cell[0, 0]].set(rotated)  12.1 us
    ppermute x2, starting transfers between devices, padded_2(): before = lax.ppermute(last, axis, up)  10.6 us
  transfers between devices with their start and end apart: 9, of which 7 were waited for; matrix products, arithmetic and copies ran while one was open for 7% of the time, Pallas kernels for 0%

profile of v12, /device:TPU:1, one launch (start us, length us, event | category | flops | bytes accessed | tf_op | source)
XLA Modules:
  0.0 231.2 jit_solution(5384529008458837743)
XLA Ops:
  0.6 0.7 fusion.49
  1.4 0.8 select_reduce_fusion.1
  4.1 1.4 reduce.17
  5.5 0.7 add_reduce_fusion
  8.1 0.8 reshape.581
  9.0 19.1 %all-to-all-start = ((s32[64,1,384]{2,1,0:T(1,128)}), s32[64,1,384]{2,1,0:T(1,128)S(1)}, u32[]{:S(2)}, u32[]{:S(2)}) async-start(s32[64,1,384]{2,1,0:T(1,128)} %reshape.581), calls=%async_computation | async-start | bytes 196608 | tf_op jit(solution)/shard_map/all_to_all | solution.py:191
  30.6 2.3 %copy.115 = f32[3,8,128,128]{3,1,2,0:T(8,128)S(1)} copy(f32[3,8,128,128]{3,2,1,0:T(8,128)} %bitcast.156) | data formatting | bytes 3145728
  32.9 4.6 %copy.88 = f32[24,16384]{0,1:T(8,128)} copy(f32[24,16384]{1,0:T(8,128)S(1)} %bitcast.149) | data formatting | bytes 3145728 | tf_op jit(solution)/shard_map/reshape;squeeze | solution.py:172
  37.6 0.7 broadcast_and_fusion
  38.3 4.0 %all-to-all-done = s32[64,1,384]{2,1,0:T(1,128)S(1)} async-done(((s32[64,1,384]{2,1,0:T(1,128)}), s32[64,1,384]{2,1,0:T(1,128)S(1)}, u32[]{:S(2)}, u32[]{:S(2)}) %all-to-all-start) | async-done | bytes 98336 | tf_op jit(solution)/shard_map/all_to_all | solution.py:191
  42.7 0.9 reduce.18
  44.3 0.7 reshape_squeeze.14.rows_ref
  45.0 0.7 pad_maximum_fusion.4.weights_ref
  45.7 23.9 %shard_map.95 = f32[4096,24]{1,0:T(8,128)} custom-call(s32[4096]{0:T(1024)} %reshape_squeeze.14.rows_ref, f32[4,4096]{1,0:T(4,128)} %pad_maximum_fusion.4.weights_ref, f32[16384,24]{1,0:T(8,128)} %bitcast.146), custom_call_target="tpu_custom_call" | custom-call | tf_op jit(solution)/shard_map/pallas_call | solution.py:61
  69.7 2.2 copy.86
  71.9 1.2 reshape.583
  73.1 9.8 %all-to-all-start.1 = ((f32[32,1,3072]{2,1,0:T(1,128)}), f32[32,1,3072]{2,1,0:T(1,128)S(1)}, u32[]{:S(2)}, u32[]{:S(2)}) async-start(f32[32,1,3072]{2,1,0:T(1,128)} %reshape.583), calls=%async_computation.1 | async-start | bytes 786432 | tf_op jit(solution)/shard_map/all_to_all | solution.py:208
  83.0 0.7 broadcast_and_fusion.1
  84.0 24.9 %all-to-all-done.1 = f32[32,1,3072]{2,1,0:T(1,128)S(1)} async-done(((f32[32,1,3072]{2,1,0:T(1,128)}), f32[32,1,3072]{2,1,0:T(1,128)S(1)}, u32[]{:S(2)}, u32[]{:S(2)}) %all-to-all-start.1) | async-done | bytes 393248 | tf_op jit(solution)/shard_map/all_to_all | solution.py:208
  109.4 1.6 reduce.19
  111.8 2.4 %collective-permute-start = (f32[32,64,24]{1,2,0:T(8,128)S(1)}, f32[32,64,24]{1,2,0:T(8,128)S(1)}, u32[]{:S(2)}, u32[]{:S(2)}) collective-permute-start(f32[32,64,24]{1,2,0:T(8,128)S(1)} %gather_fusion), channel_id=1, source_target_pairs={{0,256},{256,0},{1,257},{257,1},{2,258},{258,2},{3,259},{259,3},{4... | collective-permute-start | bytes 589832 | tf_op jit(solution)/shard_map/ppermute | solution.py:24
  114.3 7.5 %collective-permute-done = f32[32,64,24]{1,2,0:T(8,128)S(1)} collective-permute-done((f32[32,64,24]{1,2,0:T(8,128)S(1)}, f32[32,64,24]{1,2,0:T(8,128)S(1)}, u32[]{:S(2)}, u32[]{:S(2)}) %collective-permute-start) | collective-permute-done | bytes 196640 | tf_op jit(solution)/shard_map/ppermute | solution.py:24
  122.6 12.1 %scatter_fusion = f32[24,16384]{0,1:T(8,128)} fusion(f32[24,16384]{0,1:T(8,128)} %copy.88, s32[2048]{0:T(1024)S(1)} %bitcast.176, f32[2048,24]{1,0:T(8,128)S(1)} %copy.89), kind=kCustom, calls=%fused_computation.3 | custom fusion | bytes 598016 | tf_op jit(solution)/shard_map/scatter | solution.py:226
  134.8 5.4 %copy.90 = f32[24,128,128]{2,1,0:T(8,128)S(1)} copy(f32[24,128,128]{0,2,1:T(8,128)} %bitcast.147) | data formatting | bytes 3145728 | tf_op jit(solution)/shard_map/reshape;reshape | solution.py:243
  140.2 6.5 %collective-permute-start.1 = (f32[28,3,128]{2,1,0:T(4,128)S(1)}, f32[28,3,128]{2,1,0:T(4,128)S(1)}, u32[]{:S(2)}, u32[]{:S(2)}) collective-permute-start(f32[28,3,128]{2,1,0:T(4,128)S(1)} %get-tuple-element.16), channel_id=1, source_target_pairs={{0,32},{32,64},{64,96},{96,128},{128,160},{160,192},{192,224},{1,3... | collective-permute-start | bytes 129032 | tf_op jit(solution)/shard_map/ppermute | solution.py:34
  146.7 1.9 collective-permute-start.2
  148.7 3.5 %collective-permute-done.2 = f32[28,3,128]{2,1,0:T(4,128)S(1)} collective-permute-done((f32[28,3,128]{2,1,0:T(4,128)S(1)}, f32[28,3,128]{2,1,0:T(4,128)S(1)}, u32[]{:S(2)}, u32[]{:S(2)}) %collective-permute-start.2) | collective-permute-done | bytes 43040 | tf_op jit(solution)/shard_map/ppermute | solution.py:35
  153.1 1.9 fusion.104
  155.0 3.4 %copy.105 = f32[28,134,3]{1,0,2:T(8,128)} copy(f32[28,134,3]{2,1,0:T(8,128)} %get-tuple-element.14) | data formatting | bytes 90048
  158.3 4.0 %collective-permute-start.3 = (f32[28,134,3]{1,0,2:T(8,128)}, f32[28,134,3]{1,0,2:T(8,128)}, u32[]{:S(2)}, u32[]{:S(2)}) collective-permute-start(f32[28,134,3]{1,0,2:T(8,128)} %copy.105), channel_id=1, source_target_pairs={{0,1},{1,2},{2,3},{3,4},{4,5},{5,6},{6,7},{7,8},{8,9},{9,10},{10,1... | collective-permute-start | bytes 135080 | tf_op jit(solution)/shard_map/ppermute | solution.py:34
  162.4 1.8 copy.106
  164.2 1.3 collective-permute-start.4
  166.1 1.6 copy.93
  167.6 3.8 %collective-permute-done.4 = f32[28,134,3]{1,0,2:T(8,128)} collective-permute-done((f32[28,134,3]{1,0,2:T(8,128)}, f32[28,134,3]{1,0,2:T(8,128)}, u32[]{:S(2)}, u32[]{:S(2)}) %collective-permute-start.4) | collective-permute-done | bytes 45056 | tf_op jit(solution)/shard_map/ppermute | solution.py:35
  171.4 2.9 %copy.94 = f32[28,134,3]{2,1,0:T(8,128)} copy(f32[28,134,3]{1,0,2:T(8,128)} %collective-permute-done.4) | data formatting | bytes 90048 | tf_op jit(solution)/shard_map/ppermute | solution.py:35
  174.3 4.8 %pad_maximum_fusion = f32[28,134,134]{2,1,0:T(8,128)S(1)} fusion(f32[28,134,3]{2,1,0:T(8,128)} %copy.94, f32[28,3,128]{2,1,0:T(4,128)} %copy-done.8, f32[4,128,128]{2,1,0:T(8,128)} %bitcast.151, f32[24,128,128]{2,1,0:T(8,128)S(1)} %copy.90, f32[28,3,128]{2,1,0:T(4,128)} %copy-done.6, f32[28,134,3]{2,1,0:T(8,128)S(1)} %copy.93), kind=kLoop, calls=%fused_computation.6 | loop fusion | flops 2513840 | bytes 4022144 | tf_op jit(solution)/shard_map/concatenate | solution.py:36
  179.3 0.9 slice.280
  181.2 3.6 %fusion.4 = f32[6,4,132,132]{3,2,1,0:T(8,128)S(1)} fusion(f32[6,4,132,132]{3,2,1,0:T(8,128)S(1)} %slice.280, f32[6,4,134,134]{3,2,1,0:T(8,128)S(1)} %bitcast.144, f32[132]{0:T(256)S(1)} %divide_multiply_fusion, f32[4,132,132]{2,1,0:T(8,128)S(1)} %pad_maximum_fusion.3), kind=kLoop, calls=%fused_computation.11 | loop fusion | flops 5018112 | bytes 10315536 | tf_op jit(solution)/shard_map/add | solution.py:250
  188.8 7.7 %all-to-all-start.2 = ((f32[32,1,4]{2,1,0:T(1,128)}), f32[32,1,4]{2,1,0:T(1,128)S(1)}, u32[]{:S(2)}, u32[]{:S(2)}) async-start(f32[32,1,4]{2,1,0:T(1,128)} %broadcast_in_dim.210), calls=%async_computation.2 | async-start | bytes 32768 | tf_op jit(solution)/shard_map/all_to_all | solution.py:43
  196.5 13.6 %all-to-all-done.2 = f32[32,1,4]{2,1,0:T(1,128)S(1)} async-done(((f32[32,1,4]{2,1,0:T(1,128)}), f32[32,1,4]{2,1,0:T(1,128)S(1)}, u32[]{:S(2)}, u32[]{:S(2)}) %all-to-all-start.2) | async-done | bytes 544 | tf_op jit(solution)/shard_map/all_to_all | solution.py:43
  210.2 0.7 reshape.585
  210.9 6.8 %all-to-all-start.3 = ((f32[8,1,128]{2,1,0:T(1,128)}), f32[8,1,128]{2,1,0:T(1,128)S(1)}, u32[]{:S(2)}, u32[]{:S(2)}) async-start(f32[8,1,128]{2,1,0:T(1,128)} %reshape.585), calls=%async_computation.3 | async-start | bytes 8192 | tf_op jit(solution)/shard_map/all_to_all | solution.py:43
  217.8 1.2 slice.307
  218.9 3.3 %all-to-all-done.3 = f32[8,1,128]{2,1,0:T(1,128)S(1)} async-done(((f32[8,1,128]{2,1,0:T(1,128)}), f32[8,1,128]{2,1,0:T(1,128)S(1)}, u32[]{:S(2)}, u32[]{:S(2)}) %all-to-all-start.3) | async-done | bytes 4128 | tf_op jit(solution)/shard_map/all_to_all | solution.py:43
  225.1 1.9 add_bitcast_fusion
  227.0 1.2 select_add_fusion
  228.7 1.2 fusion.25
  229.9 1.2 maximum_bitcast_fusion
  (127 shorter events, 19.9 us)
Async XLA Ops:
  9.0 33.2 %all-to-all-start = ((s32[64,1,384]{2,1,0:T(1,128)}), s32[64,1,384]{2,1,0:T(1,128)S(1)}, u32[]{:S(2)}, u32[]{:S(2)}) async-start(s32[64,1,384]{2,1,0:T(1,128)} %reshape.581), calls=%async_computation | async-start | bytes 196608 | tf_op jit(solution)/shard_map/all_to_all | solution.py:191
  69.7 14.0 %copy-start.13 = (s32[1,1,2048]{2,1,0:T(1,128)S(1)}, s32[1,1,2048]{2,1,0:T(1,128)}, u32[]{:S(2)}) copy-start(s32[1,1,2048]{2,1,0:T(1,128)} %param.15) | copy-start | bytes 24580
  69.7 14.0 %copy-start.12 = (f32[1,1,2048]{2,1,0:T(1,128)S(1)}, f32[1,1,2048]{2,1,0:T(1,128)}, u32[]{:S(2)}) copy-start(f32[1,1,2048]{2,1,0:T(1,128)} %param.14) | copy-start | bytes 24580
  73.1 35.7 %all-to-all-start.1 = ((f32[32,1,3072]{2,1,0:T(1,128)}), f32[32,1,3072]{2,1,0:T(1,128)S(1)}, u32[]{:S(2)}, u32[]{:S(2)}) async-start(f32[32,1,3072]{2,1,0:T(1,128)} %reshape.583), calls=%async_computation.1 | async-start | bytes 786432 | tf_op jit(solution)/shard_map/all_to_all | solution.py:208
  111.8 10.0 %collective-permute-start = (f32[32,64,24]{1,2,0:T(8,128)S(1)}, f32[32,64,24]{1,2,0:T(8,128)S(1)}, u32[]{:S(2)}, u32[]{:S(2)}) collective-permute-start(f32[32,64,24]{1,2,0:T(8,128)S(1)} %gather_fusion), channel_id=1, source_target_pairs={{0,256},{256,0},{1,257},{257,1},{2,258},{258,2},{3,259},{259,3},{4... | collective-permute-start | bytes 589832 | tf_op jit(solution)/shard_map/ppermute | solution.py:24
  134.8 5.4 %copy-start.2 = (f32[1,4,128,128]{3,2,1,0:T(8,128)S(1)}, f32[1,4,128,128]{3,2,1,0:T(8,128)}, u32[]{:S(2)}) copy-start(f32[1,4,128,128]{3,2,1,0:T(8,128)} %param.9) | copy-start | bytes 786436
  140.2 8.5 %collective-permute-start.1 = (f32[28,3,128]{2,1,0:T(4,128)S(1)}, f32[28,3,128]{2,1,0:T(4,128)S(1)}, u32[]{:S(2)}, u32[]{:S(2)}) collective-permute-start(f32[28,3,128]{2,1,0:T(4,128)S(1)} %get-tuple-element.16), channel_id=1, source_target_pairs={{0,32},{32,64},{64,96},{96,128},{128,160},{160,192},{192,224},{1,3... | collective-permute-start | bytes 129032 | tf_op jit(solution)/shard_map/ppermute | solution.py:34
  146.7 5.5 %collective-permute-start.2 = (f32[28,3,128]{2,1,0:T(4,128)S(1)}, f32[28,3,128]{2,1,0:T(4,128)S(1)}, u32[]{:S(2)}, u32[]{:S(2)}) collective-permute-start(f32[28,3,128]{2,1,0:T(4,128)S(1)} %get-tuple-element.17), channel_id=1, source_target_pairs={{32,0},{64,32},{96,64},{128,96},{160,128},{192,160},{224,192},{33,... | collective-permute-start | bytes 129032 | tf_op jit(solution)/shard_map/ppermute | solution.py:35
  148.7 3.5 %copy-start.6 = (f32[28,3,128]{2,1,0:T(4,128)}, f32[28,3,128]{2,1,0:T(4,128)S(1)}, u32[]{:S(2)}) copy-start(f32[28,3,128]{2,1,0:T(4,128)S(1)} %collective-permute-done.1) | copy-start | bytes 129028
  152.2 0.6 copy-start.8
  158.3 7.7 %collective-permute-start.3 = (f32[28,134,3]{1,0,2:T(8,128)}, f32[28,134,3]{1,0,2:T(8,128)}, u32[]{:S(2)}, u32[]{:S(2)}) collective-permute-start(f32[28,134,3]{1,0,2:T(8,128)} %copy.105), channel_id=1, source_target_pairs={{0,1},{1,2},{2,3},{3,4},{4,5},{5,6},{6,7},{7,8},{8,9},{9,10},{10,1... | collective-permute-start | bytes 135080 | tf_op jit(solution)/shard_map/ppermute | solution.py:34
  164.2 7.2 %collective-permute-start.4 = (f32[28,134,3]{1,0,2:T(8,128)}, f32[28,134,3]{1,0,2:T(8,128)}, u32[]{:S(2)}, u32[]{:S(2)}) collective-permute-start(f32[28,134,3]{1,0,2:T(8,128)} %copy.106), channel_id=1, source_target_pairs={{1,0},{2,1},{3,2},{4,3},{5,4},{6,5},{7,6},{8,7},{9,8},{10,9},{11,1... | collective-permute-start | bytes 135080 | tf_op jit(solution)/shard_map/ppermute | solution.py:35
  179.3 1.5 copy-start
  179.3 1.5 copy-start.3
  179.3 1.5 copy-start.7
  179.3 1.5 copy-start.9
  184.8 0.8 copy-start.10
  185.0 0.8 copy-start.4
  185.6 0.8 copy-start.11
  186.3 36.7 %copy-start.18 = (f32[4]{0:T(128)S(1)}, f32[4]{0:T(128)}, u32[]{:S(2)}) copy-start(f32[4]{0:T(128)} %get-tuple-element.32) | copy-start | bytes 52
  186.3 36.7 %copy-start.19 = (f32[4]{0:T(128)S(1)}, f32[4]{0:T(128)}, u32[]{:S(2)}) copy-start(f32[4]{0:T(128)} %get-tuple-element.33) | copy-start | bytes 52
  186.3 36.7 %copy-start.21 = (f32[4]{0:T(128)S(1)}, f32[4]{0:T(128)}, u32[]{:S(2)}) copy-start(f32[4]{0:T(128)} %iota_multiply_fusion.2) | copy-start | bytes 52
  186.3 37.1 %copy-start.14 = (f32[8]{0:T(128)S(1)}, f32[8]{0:T(128)}, u32[]{:S(2)}) copy-start(f32[8]{0:T(128)} %get-tuple-element.34) | copy-start | bytes 100
  186.3 37.1 %copy-start.15 = (f32[8]{0:T(128)S(1)}, f32[8]{0:T(128)}, u32[]{:S(2)}) copy-start(f32[8]{0:T(128)} %get-tuple-element.35) | copy-start | bytes 100
  186.3 37.4 %copy-start.16 = (f32[32]{0:T(128)S(1)}, f32[32]{0:T(128)}, u32[]{:S(2)}) copy-start(f32[32]{0:T(128)} %get-tuple-element.38) | copy-start | bytes 388
  186.4 37.4 %copy-start.17 = (f32[32]{0:T(128)S(1)}, f32[32]{0:T(128)}, u32[]{:S(2)}) copy-start(f32[32]{0:T(128)} %get-tuple-element.39) | copy-start | bytes 388
  186.4 37.4 %copy-start.20 = (f32[32]{0:T(128)S(1)}, f32[32]{0:T(128)}, u32[]{:S(2)}) copy-start(f32[32]{0:T(128)} %get-tuple-element.37) | copy-start | bytes 388
  186.9 0.8 copy-start.1
  188.8 21.3 %all-to-all-start.2 = ((f32[32,1,4]{2,1,0:T(1,128)}), f32[32,1,4]{2,1,0:T(1,128)S(1)}, u32[]{:S(2)}, u32[]{:S(2)}) async-start(f32[32,1,4]{2,1,0:T(1,128)} %broadcast_in_dim.210), calls=%async_computation.2 | async-start | bytes 32768 | tf_op jit(solution)/shard_map/all_to_all | solution.py:43
  210.9 11.3 %all-to-all-start.3 = ((f32[8,1,128]{2,1,0:T(1,128)}), f32[8,1,128]{2,1,0:T(1,128)S(1)}, u32[]{:S(2)}, u32[]{:S(2)}) async-start(f32[8,1,128]{2,1,0:T(1,128)} %reshape.585), calls=%async_computation.3 | async-start | bytes 8192 | tf_op jit(solution)/shard_map/all_to_all | solution.py:43
  223.0 6.9 %copy-start.5 = (f32[3,4,128,128]{3,2,1,0:T(8,128)S(1)}, f32[3,4,128,128]{3,2,1,0:T(8,128)}, u32[]{:S(2)}) copy-start(f32[3,4,128,128]{3,2,1,0:T(8,128)} %slice.307) | copy-start | bytes 2359300

commit v13 on v12

--- a/solution.py
+++ b/solution.py
@@ -247,16 +247,22 @@
     inv_two, gain_two = metric(row_first + jnp.arange(-2, rows_dev + 2, dtype=jnp.int32), total_rows)
     inv_one, gain_one = metric(row_first + jnp.arange(-1, rows_dev + 1, dtype=jnp.int32), total_rows)
     centre = wide_fields[..., 1:-1, 1:-1]
-    stepped_wide = centre + wide_visc[None, :, 1:-1, 1:-1] * lap_shrink(wide_fields, gain_two)
+    stepped_wide = centre[0:3] + wide_visc[None, :, 1:-1, 1:-1] * lap_shrink(
+        wide_fields[0:3], gain_two
+    )
     stepped_wide = jnp.concatenate(
         [stepped_wide[0:1] + BUOYANCY * centre[3:4], stepped_wide[1:]], axis=0
     )
-    velocity = jnp.where(inside(2), stepped_wide[0:3], 0.0)
+    scalars = wide_fields[3:6, :, 2:-2, 2:-2]
+    stepped_rest = scalars[..., 1:-1, 1:-1] + wide_visc[None, :, 3:-3, 3:-3] * lap_shrink(
+        scalars, gain_own
+    )
+    velocity = jnp.where(inside(2), stepped_wide, 0.0)
     divergence_wide = diverge(velocity, inv_one)
     press_wide = jnp.where(inside(1), -divergence_wide / (4.0 + 2.0 * gain_one)[:, None], 0.0)
     divergence = divergence_wide[:, 1:-1, 1:-1]
     press_one = press_wide[:, 1:-1, 1:-1]
-    stepped = stepped_wide[:, :, 2:-2, 2:-2]
+    stepped = jnp.concatenate([stepped_wide[:, :, 2:-2, 2:-2], stepped_rest], axis=0)
     resid_one = -divergence + lap_shrink(press_wide, gain_own)
     block_sum = jnp.sum(resid_one, axis=(1, 2)) * (1.0 / math.sqrt(rows_dev * cols_dev))
     gathered = gather_by_exchange(block_sum[None], "lon")

time: 232 us -> 233 us (level)
  waiting for transfers between devices: 60.5 us -> 56.3 us
  other arithmetic: 30.6 us -> 34.8 us
    all_to_all x2, waiting for transfers between devices: 16.9 us -> 13.4 us  [gather_by_exchange(): lax.all_to_all(repeated, axis, split_axis=0, concat_axis=0, tiled=True)]
    add x1 -> x2, other arithmetic: 3.57 us -> 5.31 us  [the longest x1 3.47 us: shards(): scalars[..., 1:-1, 1:-1]]
    unnamed x57 -> x65, local copies, waits for them, and re-layouts: 13.9 us -> 14.9 us
  transfers between devices with their start and end apart: 9 -> 9, of which waited for: 7 -> 7; matrix products, arithmetic and copies ran while one was open for 7% -> 9% of each run, Pallas kernels for 0% -> 0%
where the time goes in v13:
time: 233 us; the launch traced here: 232 us
  starting transfers between devices  59.7 us (26%)
  waiting for transfers between devices  56.3 us (24%)
  local copies, waits for them, and re-layouts  53.9 us (23%)
  other arithmetic  34.8 us (15%)
  Pallas kernels  24 us (10%)
    all_to_all x1, waiting for transfers between devices, shards(): lax.all_to_all(served, 'lon', split_axis=0, concat_axis=0, tiled=True)  24.9 us
    pallas_call x1, Pallas kernels, corner_blend(): pl.pallas_call(kernel, out_shape=jax.ShapeDtypeStruct((count, table.shape...  24 us
    all_to_all x1, starting transfers between devices, shards(): lax.all_to_all(routed, ('panel', 'lon'), split_axis=0, concat_axis=0, til...  19.1 us
    unnamed x65, local copies, waits for them, and re-layouts  14.9 us
    all_to_all x2, starting transfers between devices, gather_by_exchange(): lax.all_to_all(repeated, axis, split_axis=0, concat_axis=0, tiled=True)  14.5 us
    all_to_all x2, waiting for transfers between devices, gather_by_exchange(): lax.all_to_all(repeated, axis, split_axis=0, concat_axis=0, tiled=True)  13.4 us
    scatter x1, local copies, waits for them, and re-layouts, shards(): flat_cells.at[:, dest_cell[0, 0]].set(rotated)  12.2 us
    ppermute x2, starting transfers between devices, padded_2(): before = lax.ppermute(last, axis, up)  10.6 us
  transfers between devices with their start and end apart: 9, of which 7 were waited for; matrix products, arithmetic and copies ran while one was open for 9% of the time, Pallas kernels for 0%

profile of v13, /device:TPU:1, one launch (start us, length us, event | category | flops | bytes accessed | tf_op | source)
XLA Modules:
  0.0 231.8 jit_solution(5763221278823624327)
XLA Ops:
  0.6 0.7 fusion.57
  1.4 0.8 select_reduce_fusion.1
  4.1 1.4 reduce.17
  5.5 0.7 add_reduce_fusion
  8.1 0.8 reshape.594
  9.0 19.1 %all-to-all-start = ((s32[64,1,384]{2,1,0:T(1,128)}), s32[64,1,384]{2,1,0:T(1,128)S(1)}, u32[]{:S(2)}, u32[]{:S(2)}) async-start(s32[64,1,384]{2,1,0:T(1,128)} %reshape.594), calls=%async_computation | async-start | bytes 196608 | tf_op jit(solution)/shard_map/all_to_all | solution.py:191
  30.6 2.3 %copy.119 = f32[3,8,128,128]{3,1,2,0:T(8,128)S(1)} copy(f32[3,8,128,128]{3,2,1,0:T(8,128)} %bitcast.162) | data formatting | bytes 3145728
  32.9 4.6 %copy.92 = f32[24,16384]{0,1:T(8,128)} copy(f32[24,16384]{1,0:T(8,128)S(1)} %bitcast.159) | data formatting | bytes 3145728 | tf_op jit(solution)/shard_map/reshape;squeeze | solution.py:172
  37.6 0.7 broadcast_and_fusion
  38.3 3.9 %all-to-all-done = s32[64,1,384]{2,1,0:T(1,128)S(1)} async-done(((s32[64,1,384]{2,1,0:T(1,128)}), s32[64,1,384]{2,1,0:T(1,128)S(1)}, u32[]{:S(2)}, u32[]{:S(2)}) %all-to-all-start) | async-done | bytes 98336 | tf_op jit(solution)/shard_map/all_to_all | solution.py:191
  42.7 0.9 reduce.18
  45.7 24.0 %shard_map.95 = f32[4096,24]{1,0:T(8,128)} custom-call(s32[4096]{0:T(1024)} %reshape_squeeze.14.rows_ref, f32[4,4096]{1,0:T(4,128)} %pad_maximum_fusion.4.weights_ref, f32[16384,24]{1,0:T(8,128)} %bitcast.144), custom_call_target="tpu_custom_call" | custom-call | tf_op jit(solution)/shard_map/pallas_call | solution.py:61
  69.7 2.2 copy.90
  71.9 1.2 reshape.596
  73.1 9.9 %all-to-all-start.1 = ((f32[32,1,3072]{2,1,0:T(1,128)}), f32[32,1,3072]{2,1,0:T(1,128)S(1)}, u32[]{:S(2)}, u32[]{:S(2)}) async-start(f32[32,1,3072]{2,1,0:T(1,128)} %reshape.596), calls=%async_computation.1 | async-start | bytes 786432 | tf_op jit(solution)/shard_map/all_to_all | solution.py:208
  84.1 24.9 %all-to-all-done.1 = f32[32,1,3072]{2,1,0:T(1,128)S(1)} async-done(((f32[32,1,3072]{2,1,0:T(1,128)}), f32[32,1,3072]{2,1,0:T(1,128)S(1)}, u32[]{:S(2)}, u32[]{:S(2)}) %all-to-all-start.1) | async-done | bytes 393248 | tf_op jit(solution)/shard_map/all_to_all | solution.py:208
  109.5 1.5 reduce.19
  111.8 2.4 %collective-permute-start = (f32[32,64,24]{1,2,0:T(8,128)S(1)}, f32[32,64,24]{1,2,0:T(8,128)S(1)}, u32[]{:S(2)}, u32[]{:S(2)}) collective-permute-start(f32[32,64,24]{1,2,0:T(8,128)S(1)} %gather_fusion), channel_id=1, source_target_pairs={{0,256},{256,0},{1,257},{257,1},{2,258},{258,2},{3,259},{259,3},{4... | collective-permute-start | bytes 589832 | tf_op jit(solution)/shard_map/ppermute | solution.py:24
  114.2 7.5 %collective-permute-done = f32[32,64,24]{1,2,0:T(8,128)S(1)} collective-permute-done((f32[32,64,24]{1,2,0:T(8,128)S(1)}, f32[32,64,24]{1,2,0:T(8,128)S(1)}, u32[]{:S(2)}, u32[]{:S(2)}) %collective-permute-start) | collective-permute-done | bytes 196640 | tf_op jit(solution)/shard_map/ppermute | solution.py:24
  122.5 12.2 %scatter_fusion = f32[24,16384]{0,1:T(8,128)} fusion(f32[24,16384]{0,1:T(8,128)} %copy.92, s32[2048]{0:T(1024)S(1)} %bitcast.182, f32[2048,24]{1,0:T(8,128)S(1)} %copy.93), kind=kCustom, calls=%fused_computation.3 | custom fusion | bytes 598016 | tf_op jit(solution)/shard_map/scatter | solution.py:226
  134.7 5.4 %copy.94 = f32[24,128,128]{2,1,0:T(8,128)S(1)} copy(f32[24,128,128]{0,2,1:T(8,128)} %bitcast.145) | data formatting | bytes 3145728 | tf_op jit(solution)/shard_map/reshape;reshape | solution.py:243
  140.1 6.5 %collective-permute-start.1 = (f32[28,3,128]{2,1,0:T(4,128)S(1)}, f32[28,3,128]{2,1,0:T(4,128)S(1)}, u32[]{:S(2)}, u32[]{:S(2)}) collective-permute-start(f32[28,3,128]{2,1,0:T(4,128)S(1)} %get-tuple-element.16), channel_id=1, source_target_pairs={{0,32},{32,64},{64,96},{96,128},{128,160},{160,192},{192,224},{1,3... | collective-permute-start | bytes 129032 | tf_op jit(solution)/shard_map/ppermute | solution.py:34
  146.7 1.9 collective-permute-start.2
  149.2 3.0 %collective-permute-done.2 = f32[28,3,128]{2,1,0:T(4,128)S(1)} collective-permute-done((f32[28,3,128]{2,1,0:T(4,128)S(1)}, f32[28,3,128]{2,1,0:T(4,128)S(1)}, u32[]{:S(2)}, u32[]{:S(2)}) %collective-permute-start.2) | collective-permute-done | bytes 43040 | tf_op jit(solution)/shard_map/ppermute | solution.py:35
  153.0 1.9 fusion.112
  154.9 3.4 %copy.109 = f32[28,134,3]{1,0,2:T(8,128)} copy(f32[28,134,3]{2,1,0:T(8,128)} %get-tuple-element.14) | data formatting | bytes 90048
  158.3 4.0 %collective-permute-start.3 = (f32[28,134,3]{1,0,2:T(8,128)}, f32[28,134,3]{1,0,2:T(8,128)}, u32[]{:S(2)}, u32[]{:S(2)}) collective-permute-start(f32[28,134,3]{1,0,2:T(8,128)} %copy.109), channel_id=1, source_target_pairs={{0,1},{1,2},{2,3},{3,4},{4,5},{5,6},{6,7},{7,8},{8,9},{9,10},{10,1... | collective-permute-start | bytes 135080 | tf_op jit(solution)/shard_map/ppermute | solution.py:34
  162.3 1.8 copy.110
  164.2 1.3 collective-permute-start.4
  166.0 1.6 copy.97
  167.6 3.7 %collective-permute-done.4 = f32[28,134,3]{1,0,2:T(8,128)} collective-permute-done((f32[28,134,3]{1,0,2:T(8,128)}, f32[28,134,3]{1,0,2:T(8,128)}, u32[]{:S(2)}, u32[]{:S(2)}) %collective-permute-start.4) | collective-permute-done | bytes 45056 | tf_op jit(solution)/shard_map/ppermute | solution.py:35
  171.3 2.9 %copy.98 = f32[28,134,3]{2,1,0:T(8,128)} copy(f32[28,134,3]{1,0,2:T(8,128)} %collective-permute-done.4) | data formatting | bytes 90048 | tf_op jit(solution)/shard_map/ppermute | solution.py:35
  174.2 1.9 pad_maximum_fusion.2
  176.7 1.0 copy-done
  177.7 3.6 %pad_maximum_fusion = f32[28,134,134]{2,1,0:T(8,128)S(1)} fusion(f32[28,134,3]{2,1,0:T(8,128)S(1)} %copy-done, f32[28,3,128]{2,1,0:T(4,128)S(1)} %copy-done.12, f32[4,128,128]{2,1,0:T(8,128)S(1)} %bitcast.156, f32[24,128,128]{2,1,0:T(8,128)S(1)} %copy.94, f32[28,3,128]{2,1,0:T(4,128)S(1)} %copy-done.10, f32[28,134,3]{2,1,0:T(8,128)S(1)} %copy.97), kind=kLoop, calls=%fused_computation.4 | loop fusion | flops 2513840 | bytes 4022144 | tf_op jit(solution)/shard_map/concatenate | solution.py:36
  181.9 1.8 fusion.4
  184.1 0.9 copy-done.6
  188.2 7.7 %all-to-all-start.2 = ((f32[32,1,4]{2,1,0:T(1,128)}), f32[32,1,4]{2,1,0:T(1,128)S(1)}, u32[]{:S(2)}, u32[]{:S(2)}) async-start(f32[32,1,4]{2,1,0:T(1,128)} %broadcast_in_dim.211), calls=%async_computation.2 | async-start | bytes 32768 | tf_op jit(solution)/shard_map/all_to_all | solution.py:43
  196.0 1.2 slice.349
  197.1 12.4 %all-to-all-done.2 = f32[32,1,4]{2,1,0:T(1,128)S(1)} async-done(((f32[32,1,4]{2,1,0:T(1,128)}), f32[32,1,4]{2,1,0:T(1,128)S(1)}, u32[]{:S(2)}, u32[]{:S(2)}) %all-to-all-start.2) | async-done | bytes 544 | tf_op jit(solution)/shard_map/all_to_all | solution.py:43
  210.3 6.8 %all-to-all-start.3 = ((f32[8,1,128]{2,1,0:T(1,128)}), f32[8,1,128]{2,1,0:T(1,128)S(1)}, u32[]{:S(2)}, u32[]{:S(2)}) async-start(f32[8,1,128]{2,1,0:T(1,128)} %reshape.598), calls=%async_computation.3 | async-start | bytes 8192 | tf_op jit(solution)/shard_map/all_to_all | solution.py:43
  217.2 3.5 %fusion.13 = f32[3,4,128,128]{3,2,1,0:T(8,128)} fusion(f32[3,4,128,128]{3,2,1,0:T(8,128)} %slice.349, f32[6,4,134,134]{3,2,1,0:T(8,128)S(1)} %bitcast.151, f32[128]{0:T(128)S(1)} %fusion.103, f32[4,128,128]{2,1,0:T(8,128)} %bitcast.153), kind=kLoop, calls=%fused_computation.35 | loop fusion | flops 2359296 | bytes 4981248 | tf_op jit(solution)/shard_map/add | solution.py:257
  220.7 1.0 all-to-all-done.3
  224.4 1.9 add_bitcast_fusion
  226.3 1.2 select_add_fusion
  227.5 1.8 fusion.39
  229.3 1.2 fusion.33
  230.5 1.2 maximum_bitcast_fusion
  (137 shorter events, 22.1 us)
Async XLA Ops:
  9.0 33.2 %all-to-all-start = ((s32[64,1,384]{2,1,0:T(1,128)}), s32[64,1,384]{2,1,0:T(1,128)S(1)}, u32[]{:S(2)}, u32[]{:S(2)}) async-start(s32[64,1,384]{2,1,0:T(1,128)} %reshape.594), calls=%async_computation | async-start | bytes 196608 | tf_op jit(solution)/shard_map/all_to_all | solution.py:191
  71.9 11.9 %copy-start.16 = (s32[1,1,2048]{2,1,0:T(1,128)S(1)}, s32[1,1,2048]{2,1,0:T(1,128)}, u32[]{:S(2)}) copy-start(s32[1,1,2048]{2,1,0:T(1,128)} %param.15) | copy-start | bytes 24580
  71.9 11.9 %copy-start.15 = (f32[1,1,2048]{2,1,0:T(1,128)S(1)}, f32[1,1,2048]{2,1,0:T(1,128)}, u32[]{:S(2)}) copy-start(f32[1,1,2048]{2,1,0:T(1,128)} %param.14) | copy-start | bytes 24580
  73.1 35.8 %all-to-all-start.1 = ((f32[32,1,3072]{2,1,0:T(1,128)}), f32[32,1,3072]{2,1,0:T(1,128)S(1)}, u32[]{:S(2)}, u32[]{:S(2)}) async-start(f32[32,1,3072]{2,1,0:T(1,128)} %reshape.596), calls=%async_computation.1 | async-start | bytes 786432 | tf_op jit(solution)/shard_map/all_to_all | solution.py:208
  111.8 10.0 %collective-permute-start = (f32[32,64,24]{1,2,0:T(8,128)S(1)}, f32[32,64,24]{1,2,0:T(8,128)S(1)}, u32[]{:S(2)}, u32[]{:S(2)}) collective-permute-start(f32[32,64,24]{1,2,0:T(8,128)S(1)} %gather_fusion), channel_id=1, source_target_pairs={{0,256},{256,0},{1,257},{257,1},{2,258},{258,2},{3,259},{259,3},{4... | collective-permute-start | bytes 589832 | tf_op jit(solution)/shard_map/ppermute | solution.py:24
  134.7 5.4 %copy-start.4 = (f32[1,4,128,128]{3,2,1,0:T(8,128)S(1)}, f32[1,4,128,128]{3,2,1,0:T(8,128)}, u32[]{:S(2)}) copy-start(f32[1,4,128,128]{3,2,1,0:T(8,128)} %param.9) | copy-start | bytes 786436
  140.1 9.1 %collective-permute-start.1 = (f32[28,3,128]{2,1,0:T(4,128)S(1)}, f32[28,3,128]{2,1,0:T(4,128)S(1)}, u32[]{:S(2)}, u32[]{:S(2)}) collective-permute-start(f32[28,3,128]{2,1,0:T(4,128)S(1)} %get-tuple-element.16), channel_id=1, source_target_pairs={{0,32},{32,64},{64,96},{96,128},{128,160},{160,192},{192,224},{1,3... | collective-permute-start | bytes 129032 | tf_op jit(solution)/shard_map/ppermute | solution.py:34
  146.7 5.5 %collective-permute-start.2 = (f32[28,3,128]{2,1,0:T(4,128)S(1)}, f32[28,3,128]{2,1,0:T(4,128)S(1)}, u32[]{:S(2)}, u32[]{:S(2)}) collective-permute-start(f32[28,3,128]{2,1,0:T(4,128)S(1)} %get-tuple-element.17), channel_id=1, source_target_pairs={{32,0},{64,32},{96,64},{128,96},{160,128},{192,160},{224,192},{33,... | collective-permute-start | bytes 129032 | tf_op jit(solution)/shard_map/ppermute | solution.py:35
  149.2 3.0 %copy-start.9 = (f32[28,3,128]{2,1,0:T(4,128)}, f32[28,3,128]{2,1,0:T(4,128)S(1)}, u32[]{:S(2)}) copy-start(f32[28,3,128]{2,1,0:T(4,128)S(1)} %collective-permute-done.1) | copy-start | bytes 129028
  152.2 0.6 copy-start.11
  158.3 7.7 %collective-permute-start.3 = (f32[28,134,3]{1,0,2:T(8,128)}, f32[28,134,3]{1,0,2:T(8,128)}, u32[]{:S(2)}, u32[]{:S(2)}) collective-permute-start(f32[28,134,3]{1,0,2:T(8,128)} %copy.109), channel_id=1, source_target_pairs={{0,1},{1,2},{2,3},{3,4},{4,5},{5,6},{6,7},{7,8},{8,9},{9,10},{10,1... | collective-permute-start | bytes 135080 | tf_op jit(solution)/shard_map/ppermute | solution.py:34
  164.2 7.2 %collective-permute-start.4 = (f32[28,134,3]{1,0,2:T(8,128)}, f32[28,134,3]{1,0,2:T(8,128)}, u32[]{:S(2)}, u32[]{:S(2)}) collective-permute-start(f32[28,134,3]{1,0,2:T(8,128)} %copy.110), channel_id=1, source_target_pairs={{1,0},{2,1},{3,2},{4,3},{5,4},{6,5},{7,6},{8,7},{9,8},{10,9},{11,1... | collective-permute-start | bytes 135080 | tf_op jit(solution)/shard_map/ppermute | solution.py:35
  176.1 1.5 copy-start
  176.2 1.5 copy-start.5
  176.2 1.5 copy-start.10
  176.2 1.5 copy-start.12
  181.5 2.2 copy-start.1
  183.8 1.2 copy-start.6
  183.8 1.2 copy-start.13
  184.0 1.2 copy-start.7
  185.0 0.8 copy-start.14
  185.8 10.2 %copy-start.2 = (f32[24,134,134]{2,1,0:T(8,128)S(1)}, f32[24,134,134]{2,1,0:T(8,128)}, u32[]{:S(2)}) copy-start(f32[24,134,134]{2,1,0:T(8,128)} %copy-done.1) | copy-start | bytes 5171332
  186.3 0.8 copy-start.3
  188.2 21.3 %all-to-all-start.2 = ((f32[32,1,4]{2,1,0:T(1,128)}), f32[32,1,4]{2,1,0:T(1,128)S(1)}, u32[]{:S(2)}, u32[]{:S(2)}) async-start(f32[32,1,4]{2,1,0:T(1,128)} %broadcast_in_dim.211), calls=%async_computation.2 | async-start | bytes 32768 | tf_op jit(solution)/shard_map/all_to_all | solution.py:43
  210.3 11.3 %all-to-all-start.3 = ((f32[8,1,128]{2,1,0:T(1,128)}), f32[8,1,128]{2,1,0:T(1,128)S(1)}, u32[]{:S(2)}, u32[]{:S(2)}) async-start(f32[8,1,128]{2,1,0:T(1,128)} %reshape.598), calls=%async_computation.3 | async-start | bytes 8192 | tf_op jit(solution)/shard_map/all_to_all | solution.py:43
  217.1 5.2 %copy-start.21 = (f32[4]{0:T(128)S(1)}, f32[4]{0:T(128)}, u32[]{:S(2)}) copy-start(f32[4]{0:T(128)} %get-tuple-element.32) | copy-start | bytes 52
  217.1 5.2 %copy-start.22 = (f32[4]{0:T(128)S(1)}, f32[4]{0:T(128)}, u32[]{:S(2)}) copy-start(f32[4]{0:T(128)} %get-tuple-element.33) | copy-start | bytes 52
  217.1 5.2 %copy-start.24 = (f32[4]{0:T(128)S(1)}, f32[4]{0:T(128)}, u32[]{:S(2)}) copy-start(f32[4]{0:T(128)} %iota_multiply_fusion.2) | copy-start | bytes 52
  217.1 5.5 %copy-start.17 = (f32[8]{0:T(128)S(1)}, f32[8]{0:T(128)}, u32[]{:S(2)}) copy-start(f32[8]{0:T(128)} %get-tuple-element.34) | copy-start | bytes 100
  217.2 5.5 %copy-start.18 = (f32[8]{0:T(128)S(1)}, f32[8]{0:T(128)}, u32[]{:S(2)}) copy-start(f32[8]{0:T(128)} %get-tuple-element.35) | copy-start | bytes 100
  217.2 5.5 %copy-start.25 = (f32[8]{0:T(128)S(1)}, f32[8]{0:T(128)}, u32[]{:S(2)}) copy-start(f32[8]{0:T(128)} %iota_multiply_fusion.1) | copy-start | bytes 100
  217.2 5.8 %copy-start.19 = (f32[32]{0:T(128)S(1)}, f32[32]{0:T(128)}, u32[]{:S(2)}) copy-start(f32[32]{0:T(128)} %get-tuple-element.38) | copy-start | bytes 388
  217.2 5.8 %copy-start.20 = (f32[32]{0:T(128)S(1)}, f32[32]{0:T(128)}, u32[]{:S(2)}) copy-start(f32[32]{0:T(128)} %get-tuple-element.39) | copy-start | bytes 388
  217.2 5.8 %copy-start.23 = (f32[32]{0:T(128)S(1)}, f32[32]{0:T(128)}, u32[]{:S(2)}) copy-start(f32[32]{0:T(128)} %get-tuple-element.37) | copy-start | bytes 388
  227.5 3.0 %copy-start.8 = (f32[3,4,128,128]{3,2,1,0:T(8,128)S(1)}, f32[3,4,128,128]{3,2,1,0:T(8,128)}, u32[]{:S(2)}) copy-start(f32[3,4,128,128]{3,2,1,0:T(8,128)} %fusion.13) | copy-start | bytes 2359300
